TPU v7x, 128 devices: a whole 4x4x4 slice. The times are simulated.
128 devices in a mesh: grp: 4 (over z_hi, core), orb: 32 (over y, z_lo, x).
Axes of the slice: x: 4, y: 4, z: 4 (z_hi: 2, z_lo: 2; z = z_hi * 2 + z_lo), core: 2. Of those that a mesh axis runs over, the one named last changes fastest.
Arguments:
- df_panels: bfloat16 [128, 1024, 512], P(('grp', 'orb')), may hold values from -1.0546875 to 1.0546875
- occ_energy: float32 [128], replicated, may hold values from -2 to -0.5
- virt_energy: float32 [512], replicated, may hold values from 0.2 to 4
- fock_off: float32 [512, 512], replicated, may hold values from -0.25 to 0.25
- i_plan: int32 [3, 4], replicated, may hold values from 0 to 31
- pair_owner: int32 [1536, 1], P(('grp', 'orb')), may hold values from 0 to 3; in each aligned block of 12 rows (0 to 11, 12 to 23, ...) at most 4 rows name the same one
- pair_weight: float32 [1536], P(('grp', 'orb')), may hold values from -4 to 4
Outputs:
- residual: float32 [128, 512, 512], P(('grp', 'orb'))
Inputs may be any that keep to these rules, and one draw needn't show every extreme that they name: `pair_owner`: each orbital's 12 rows name no group more than 4 times; some orbital names one group exactly 4 times.
All inputs are finite; a program needn't handle non-finite values.
Results may differ from a plain program's by a relative error of at most 0.0029.
Values may be sent and summed in bfloat16 or wider, within the bound.
No kernel may reach another device: no remote copies, remote signals or barrier semaphores. Data moves between devices by JAX's collectives and lax.ppermute only.
A program may use at most 128 MiB of HBM per device.

v0:
```python
import jax
import jax.numpy as jnp
from jax import lax
from jax.sharding import PartitionSpec as P

NVIR = 512
STEPS = 3
CAP = 4


def from_root(value, axis, source):
    kept = jnp.where(lax.axis_index(axis) == source, value, 0).astype(value.dtype)
    return lax.psum(kept, axis)


def shards(df_panels, occ_energy, virt_energy, fock_off, i_plan, pair_owner, pair_weight):
    highest = lax.Precision.HIGHEST
    group_count = lax.axis_size("grp")
    orbit_count = lax.axis_size("orb")
    my_group = lax.axis_index("grp")
    my_orbital = my_group * orbit_count + lax.axis_index("orb")
    own_panel = df_panels[0]
    own_energy = lax.dynamic_index_in_dim(occ_energy, my_orbital, 0, keepdims=False)
    pair_sum = virt_energy[:, None] + virt_energy[None, :]
    groups_range = jnp.arange(group_count, dtype=jnp.int32)
    tiles = []
    for step_index in range(STEPS):
        pieces = []
        for group_index in range(group_count):
            source = group_index * orbit_count + i_plan[step_index, group_index]
            pieces.append(from_root(own_panel, ("grp", "orb"), source))
        gathered = jnp.stack(pieces, 0)
        i_ids = groups_range * orbit_count + i_plan[step_index]
        integral = jnp.einsum(
            "gxa,xb->gab", gathered, own_panel, preferred_element_type=jnp.float32
        )
        denominator = pair_sum[None] - occ_energy[i_ids][:, None, None] - own_energy
        tiles.append(integral / denominator)
    amplitude = (jnp.concatenate(tiles, 0) * pair_weight[:, None, None]).astype(jnp.bfloat16)
    tile_count = amplitude.shape[0]
    flat_tiles = amplitude.reshape(tile_count, NVIR * NVIR)
    owners = pair_owner[:, 0]
    one_hot = (owners[:, None] == groups_range[None, :]).astype(jnp.int32)
    slot_rank = jnp.sum((jnp.cumsum(one_hot, 0) - one_hot) * one_hot, 1)
    position = owners * CAP + slot_rank
    slot_range = jnp.arange(group_count * CAP, dtype=jnp.int32)
    selector = (position[None, :] == slot_range[:, None]).astype(jnp.bfloat16)
    send_tiles = jnp.dot(selector, flat_tiles, preferred_element_type=jnp.float32).astype(
        jnp.bfloat16
    )
    send_tiles = send_tiles.reshape(group_count, CAP, NVIR, NVIR)
    received = lax.all_to_all(send_tiles, "grp", split_axis=0, concat_axis=0, tiled=True)
    ones_row = jnp.ones((1, group_count * CAP), jnp.bfloat16)
    summed = jnp.dot(
        ones_row,
        received.reshape(group_count * CAP, NVIR * NVIR),
        preferred_element_type=jnp.float32,
    )
    summed = summed.reshape(NVIR, NVIR)
    fock_matrix = jnp.diag(virt_energy) + 0.5 * (fock_off + fock_off.T)
    left = jnp.dot(fock_matrix, summed, precision=highest)
    right = jnp.dot(summed, fock_matrix, precision=highest)
    return (left + right)[None]


def solution(mesh):
    placed = (
        P(("grp", "orb"), None, None),
        P(),
        P(),
        P(),
        P(),
        P(("grp", "orb"), None),
        P(("grp", "orb")),
    )
    return jax.shard_map(
        shards, mesh=mesh, in_specs=placed, out_specs=P(("grp", "orb"), None, None), check_vma=False
    )
```

profile of v0, /device:TPU:1, one launch (start us, length us, event | category | flops | bytes accessed | tf_op | source)
XLA Modules:
  0.0 356.4 jit_solution(11401939642927229969)
XLA Ops:
  6.5 0.0 all-reduce.3.cloned.1.call-start
  6.5 1.8 fusion.72
  15.9 1.5 copy.19
  17.4 4.6 %fusion.43 = (bf16[1,1024,512]{1,2,0:T(8,128)(2,1)}, bf16[1,1024,512]{1,2,0:T(8,128)(2,1)}, bf16[1,1024,512]{1,2,0:T(8,128)(2,1)}, bf16[1,1024,512]{1,2,0:T(8,12...) fusion(bf16[1,1024,512]{1,2,0:T(8,128)(2,1)S(1)} %copy.19, ...), kind=kLoop, calls=%fused_computation.57 | loop fusion | flops 6291456 | bytes 13631500 | tf_op jit(solution)/shard_map/stack | solution.py:32
  22.1 0.0 copy-start
  22.1 0.0 copy-start.4
  22.1 0.0 copy-start.5
  22.1 0.0 copy-start.3
  22.1 0.0 copy-start.2
  22.1 0.0 all-reduce.3.cloned.1.call-update
  22.1 0.6 copy-done
  22.7 0.6 dynamic_slice.4
  23.3 0.0 copy-done.4
  23.3 0.6 gather_fusion
  24.0 0.6 gather_fusion.1
  24.6 0.6 gather_fusion.2
  25.3 0.0 copy-done.5
  25.3 0.2 reduce_window_sum.11
  25.5 0.0 copy-done.3
  25.5 0.1 broadcast_add_fusion
  25.6 174.9 %all-reduce.3.cloned.1.call-done = (bf16[1,1024,512]{1,2,0:T(8,128)(2,1)}, bf16[1,1024,512]{1,2,0:T(8,128)(2,1)}, bf16[1,1024,512]{1,2,0:T(8,128)(2,1)}, bf16[1,...) async-done(((bf16[1,1024,512]{1,2,0:T(8,128)(2,1)}, ...) | async-done | bytes 12582928 | tf_op jit(solution)/shard_map/psum | solution.py:13
  200.6 0.0 copy-done.2
  200.6 4.9 %divide_bitcast_fusion.2 = f32[1,4,512,512]{3,2,1,0:T(8,128)S(1)} fusion(f32[]{:T(128)} %bitcast.15, f32[4]{0:T(128)S(1)} %gather_fusion, f32[512,512]{1,0:T(8,128)S(1)} %broadcast_add_fusion, bf16[1,1024,512]{1,2,0:T(8,128)(2,1)} %get-tuple-element.13, bf16[1,1024,512]{1,2,0:T(8,128)(2,1)} %get-tuple-element.14, ...), kind=kOutput, calls=%fused_computation.36 | convolution fusion | flops 2156920832 | bytes 10485780 | tf_op jit(solution)/shard_map/gxa,xb->gab/dot_general | solution.py:34
  205.5 0.0 copy-start.10
  205.5 0.0 copy-start.11
  205.5 0.0 copy-start.12
  205.5 0.0 copy-start.13
  205.6 2.7 copy.32
  208.3 0.0 copy-done.10
  208.3 0.0 copy-done.11
  208.3 0.0 copy-done.12
  208.3 0.0 copy-done.13
  208.3 3.4 divide_bitcast_fusion.1
  211.7 0.0 copy-start.6
  211.7 0.0 copy-start.7
  211.7 0.0 copy-start.8
  211.7 0.0 copy-start.9
  211.7 2.7 copy.33
  214.4 0.0 copy-done.6
  214.4 0.0 copy-done.7
  214.4 0.0 copy-done.8
  214.4 0.0 copy-done.9
  214.5 3.4 divide_bitcast_fusion
  217.8 0.0 copy-start.14
  217.9 2.9 copy.34
  220.8 0.0 copy-done.14
  220.8 5.9 %convolution_convert_fusion = bf16[16,262144]{1,0:T(8,128)(2,1)} fusion(f32[4,262144]{1,0:T(4,128)S(1)} %bitcast.150, f32[4,262144]{1,0:T(4,128)S(1)} %bitcast.149, f32[4,262144]{1,0:T(4,128)S(1)} %bitcast.148, f32[12]{0:T(128)S(1)} %copy-done.14, s32[12]{0:T(128)S(1)} %multiply_add_fusion), kind=kOutput, calls=%fused_computation.3 | convolution fusion | flops 117440704 | bytes 20971616 | tf_op jit(solution)/shard_map/dot_general | solution.py:48
  226.7 9.6 %copy.35 = bf16[2,8,512,512]{3,2,1,0:T(8,128)(2,1)} copy(bf16[2,8,512,512]{3,1,2,0:T(8,128)(2,1)} %bitcast.147) | data formatting | bytes 16777216
  236.3 0.0 copy-start.1
  236.3 6.3 %all-to-all-start = ((bf16[4,4,512,512]{3,2,1,0:T(8,128)(2,1)}), bf16[4,4,512,512]{3,2,1,0:T(8,128)(2,1)}, u32[]{:S(2)}, u32[]{:S(2)}) async-start(bf16[4,4,512,512]{3,2,1,0:T(8,128)(2,1)} %bitcast.146), calls=%async_computation | async-start | bytes 16777216 | tf_op jit(solution)/shard_map/all_to_all | solution.py:52
  242.6 0.0 copy-done.1
  242.6 0.3 copy.18
  242.9 93.4 %all-to-all-done = bf16[4,4,512,512]{3,2,1,0:T(8,128)(2,1)} async-done(((bf16[4,4,512,512]{3,2,1,0:T(8,128)(2,1)}), bf16[4,4,512,512]{3,2,1,0:T(8,128)(2,1)}, u32[]{:S(2)}, u32[]{:S(2)}) %all-to-all-start) | async-done | bytes 8388640 | tf_op jit(solution)/shard_map/all_to_all | solution.py:52
  336.3 8.4 %fusion.2 = f32[1,512,512]{2,0,1:T(1,128)S(1)} fusion(bf16[2,8,512,512]{3,2,1,0:T(8,128)(2,1)} %bitcast.56), kind=kOutput, calls=%fused_computation.6 | convolution fusion | flops 8388608 | bytes 9437184 | tf_op jit(solution)/shard_map/dot_general | solution.py:54
  344.7 1.9 fusion.41
  346.6 3.0 fusion.30
  (6 shorter events, 0.1 us)
Async XLA Ops:
  6.5 194.0 %all-reduce.3.cloned.1.call-start = ((), (), s32[]{:S(2)}) async-start(), calls=%async_computation.1 | async-start | bytes 25165824 | tf_op jit(solution)/shard_map/psum | solution.py:13
  22.1 0.7 copy-start
  22.1 1.2 copy-start.4
  22.1 3.2 copy-start.5
  22.1 3.4 copy-start.3
  22.1 178.5 %copy-start.2 = (bf16[1,1024,512]{2,1,0:T(8,128)(2,1)S(1)}, bf16[1,1024,512]{2,1,0:T(8,128)(2,1)}, u32[]{:S(2)}) copy-start(bf16[1,1024,512]{2,1,0:T(8,128)(2,1)} %param.7) | copy-start | bytes 3145732
  205.5 2.7 copy-start.10
  205.5 2.7 copy-start.11
  205.5 2.7 copy-start.12
  205.5 2.7 copy-start.13
  211.7 2.7 copy-start.6
  211.7 2.7 copy-start.7
  211.7 2.7 copy-start.8
  211.7 2.7 copy-start.9
  217.8 2.9 copy-start.14
  236.3 6.3 %copy-start.1 = (f32[512,512]{1,0:T(8,128)S(1)}, f32[512,512]{1,0:T(8,128)}, u32[]{:S(2)}) copy-start(f32[512,512]{1,0:T(8,128)} %param.10) | copy-start | bytes 3145732
  236.3 100.0 %all-to-all-start = ((bf16[4,4,512,512]{3,2,1,0:T(8,128)(2,1)}), bf16[4,4,512,512]{3,2,1,0:T(8,128)(2,1)}, u32[]{:S(2)}, u32[]{:S(2)}) async-start(bf16[4,4,512,512]{3,2,1,0:T(8,128)(2,1)} %bitcast.146), calls=%async_computation | async-start | bytes 16777216 | tf_op jit(solution)/shard_map/all_to_all | solution.py:52
Sparse Core Ops, SparseCore 0:
  22.3 178.2 all-reduce.2
where the time goes:
time: 357 us; the launch traced here: 356 us
  waiting for transfers between devices  268 us (75%)
  matrix products  30.8 us (9%)
  local copies, waits for them, and re-layouts  24.7 us (7%)
  between operations  21.3 us (6%)
  starting transfers between devices  6.25 us (2%)
  other arithmetic  5.01 us (1%)
    psum x1, waiting for transfers between devices, from_root(): return lax.psum(kept, axis)  175 us
    all_to_all x1, waiting for transfers between devices, shards(): lax.all_to_all(send_tiles, 'grp', split_axis=0, concat_axis=0, tiled=True)  93.4 us
    unnamed x36, local copies, waits for them, and re-layouts  20.4 us
    dot_general x3, matrix products, shards(): jnp.einsum('gxa,xb->gab', gathered, own_panel, preferred_element_type=jnp...  11.7 us
    dot_general x1, matrix products, shards(): jnp.dot(ones_row, received.reshape(group_count * CAP, NVIR * NVIR), prefe...  8.36 us
  transfers between devices with their start and end apart: 2, of which 2 were waited for; matrix products, arithmetic and copies ran while one was open for 1% of the time, Pallas kernels for 0%

commit v1 on v0

v1 whole, which is shorter than its diff:
```python
import jax
import jax.numpy as jnp
from jax import lax
from jax.sharding import PartitionSpec as P

NVIR = 512
STEPS = 3
CAP = 4


def shards(df_panels, occ_energy, virt_energy, fock_off, i_plan, pair_owner, pair_weight):
    highest = lax.Precision.HIGHEST
    group_count = lax.axis_size("grp")
    orbit_count = lax.axis_size("orb")
    my_group = lax.axis_index("grp")
    my_index = lax.axis_index("orb")
    my_orbital = my_group * orbit_count + my_index
    own_panel = df_panels[0]
    tile_count = STEPS * group_count

    groups_range = jnp.arange(group_count, dtype=jnp.int32)
    i_ids = (groups_range[None, :] * orbit_count + i_plan).reshape(tile_count)
    masked = jnp.where(
        (i_ids == my_orbital)[:, None, None], own_panel[None], jnp.zeros((), own_panel.dtype)
    )
    broadcast = lax.psum(masked, ("grp", "orb"))

    meta = jnp.concatenate([pair_weight, pair_owner[:, 0].astype(jnp.float32)])
    across = [(g, g ^ 2) for g in range(group_count)]
    beside = [(g, g ^ 1) for g in range(group_count)]
    far_panel = lax.ppermute(own_panel, "grp", across)
    far_meta = lax.ppermute(meta, "grp", across)
    near = lax.ppermute(jnp.stack([own_panel, far_panel]), "grp", beside)
    near_meta = lax.ppermute(jnp.stack([meta, far_meta]), "grp", beside)
    column = jnp.stack([own_panel, far_panel, near[0], near[1]])
    column_meta = jnp.stack([meta, far_meta, near_meta[0], near_meta[1]])
    source_groups = jnp.stack([my_group, my_group ^ 2, my_group ^ 1, my_group ^ 3])

    weights = column_meta[:, :tile_count]
    owners = column_meta[:, tile_count:]
    mine = owners == my_group.astype(jnp.float32)
    rank = jnp.cumsum(mine.astype(jnp.int32), axis=1) - 1
    slot_hit = mine[:, None, :] & (rank[:, None, :] == jnp.arange(CAP)[None, :, None])
    tile_range = jnp.arange(tile_count, dtype=jnp.int32)
    slot_tile = jnp.sum(jnp.where(slot_hit, tile_range, 0), axis=2)
    slot_weight = jnp.sum(jnp.where(slot_hit, weights[:, None, :], 0.0), axis=2)

    gathered = jnp.take(broadcast, slot_tile.reshape(-1), axis=0).reshape(
        group_count, CAP, *own_panel.shape
    )
    integral = jnp.einsum(
        "qkxa,qxb->qkab", gathered, column, preferred_element_type=jnp.float32
    )
    pair_sum = virt_energy[:, None] + virt_energy[None, :]
    i_energy = occ_energy[i_ids][slot_tile]
    j_energy = occ_energy[source_groups * orbit_count + my_index]
    denominator = (pair_sum[None, None] - i_energy[:, :, None, None]) - j_energy[:, None, None, None]
    amplitude = ((integral / denominator) * slot_weight[:, :, None, None]).astype(jnp.bfloat16)
    summed = jnp.sum(amplitude.astype(jnp.float32), axis=(0, 1))

    fock_matrix = jnp.diag(virt_energy) + 0.5 * (fock_off + fock_off.T)
    left = jnp.dot(fock_matrix, summed, precision=highest)
    right = jnp.dot(summed, fock_matrix, precision=highest)
    return (left + right)[None]


def solution(mesh):
    placed = (
        P(("grp", "orb"), None, None),
        P(),
        P(),
        P(),
        P(),
        P(("grp", "orb"), None),
        P(("grp", "orb")),
    )
    return jax.shard_map(
        shards, mesh=mesh, in_specs=placed, out_specs=P(("grp", "orb"), None, None), check_vma=False
    )
```

time: 357 us -> 260 us (0.73)
  waiting for transfers between devices: 268 us -> 171 us
  matrix products: 30.8 us -> 19.4 us
  local copies, waits for them, and re-layouts: 24.7 us -> 36.1 us
  between operations: 21.3 us -> 13.5 us
  other arithmetic: 5.01 us -> 10.9 us
    all_to_all x1 -> x0, waiting for transfers between devices: 93.4 us -> none  [shards(): lax.all_to_all(send_tiles, 'grp', split_axis=0, concat_axis=0, tiled=True)]
    psum x1, waiting for transfers between devices: 175 us -> 140 us  [shards(): broadcast = lax.psum(masked, ('grp', 'orb'))]
    gather x3 -> x6, local copies, waits for them, and re-layouts: 1.92 us -> 35.4 us  [the longest x2 33.4 us: shards(): jnp.take(broadcast, slot_tile.reshape(-1), axis=0)]
    ppermute x0 -> x4, waiting for transfers between devices: none -> 31.2 us  [the longest x1 29 us: shards(): far_panel = lax.ppermute(own_panel, 'grp', across)]
    unnamed x36 -> x17, local copies, waits for them, and re-layouts: 20.4 us -> 0.36 us
    dot_general x5 -> x1, matrix products: 25.9 us -> 14.5 us  [shards(): jnp.einsum('qkxa,qxb->qkab', gathered, column, preferred_element_type=jnp...]
    ppermute x0 -> x4, starting transfers between devices: none -> 7.48 us  [the longest x1 4.49 us: shards(): far_panel = lax.ppermute(own_panel, 'grp', across)]
    select_n x1 -> x5, other arithmetic: 0.01 us -> 6.76 us  [the longest x1 6.67 us: shards(): jnp.where((i_ids == my_orbital)[:, None, None], own_panel[None], jnp.zero...]
  transfers between devices with their start and end apart: 2 -> 5, of which waited for: 2 -> 3; matrix products, arithmetic and copies ran while one was open for 1% -> 15% of each run, Pallas kernels for 0% -> 0%
where the time goes in v1:
time: 260 us; the launch traced here: 259 us
  waiting for transfers between devices  171 us (66%)
  local copies, waits for them, and re-layouts  36.1 us (14%)
  matrix products  19.4 us (7%)
  between operations  13.5 us (5%)
  other arithmetic  10.9 us (4%)
  starting transfers between devices  7.48 us (3%)
    psum x1, waiting for transfers between devices, shards(): broadcast = lax.psum(masked, ('grp', 'orb'))  140 us
    gather x2, local copies, waits for them, and re-layouts, shards(): jnp.take(broadcast, slot_tile.reshape(-1), axis=0)  33.4 us
    ppermute x1, waiting for transfers between devices, shards(): far_panel = lax.ppermute(own_panel, 'grp', across)  29 us
    dot_general x1, matrix products, shards(): jnp.einsum('qkxa,qxb->qkab', gathered, column, preferred_element_type=jnp...  14.5 us
    select_n x1, other arithmetic, shards(): jnp.where((i_ids == my_orbital)[:, None, None], own_panel[None], jnp.zero...  6.67 us
  transfers between devices with their start and end apart: 5, of which 3 were waited for; matrix products, arithmetic and copies ran while one was open for 15% of the time, Pallas kernels for 0%

profile of v1, /device:TPU:1, one launch (start us, length us, event | category | flops | bytes accessed | tf_op | source)
XLA Modules:
  0.0 258.8 jit_solution(6814516232530975786)
XLA Ops:
  6.5 0.0 copy-start
  6.5 0.0 all-reduce.2.cloned.1.call-start
  6.5 0.7 broadcast_compare_fusion
  7.2 0.1 eq.44
  7.3 0.0 copy-start.3
  7.3 0.0 copy-start.6
  7.3 0.0 copy-start.7
  7.3 0.0 copy-start.5
  7.3 6.7 %broadcast_select_fusion = bf16[12,1024,512]{2,1,0:T(8,128)(2,1)} fusion(pred[12]{0:T(512)(128)(4,1)S(1)} %eq.44, bf16[1024,512]{1,0:T(8,128)(2,1)} %bitcast.43), kind=kLoop, calls=%fused_computation.9 | loop fusion | flops 6291456 | bytes 13631500 | tf_op jit(solution)/shard_map/jit(_where)/select_n | solution.py:23
  14.0 0.0 copy-start.2
  14.0 0.0 all-reduce.2.cloned.1.call-update
  14.0 0.0 copy-done.3
  14.0 4.5 %collective-permute-start.2 = (bf16[1024,512]{1,0:T(8,128)(2,1)S(1)}, bf16[1024,512]{1,0:T(8,128)(2,1)S(1)}, u32[]{:S(2)}, u32[]{:S(2)}) collective-permute-start(bf16[1024,512]{1,0:T(8,128)(2,1)S(1)} %bitcast.44), channel_id=1, source_target_pairs={{0,64},{32,96},{64,0},{96,32},{1,65},{33,97},{65,1},{97,33},{2,66}... | collective-permute-start | bytes 3145736 | tf_op jit(solution)/shard_map/ppermute | solution.py:31
  18.5 0.0 copy-done.6
  18.5 0.0 copy-done.7
  18.5 0.1 pad_maximum_fusion.3
  18.6 0.1 collective-permute-start
  18.7 0.1 reshape.207
  18.8 0.1 fusion.18
  18.9 29.0 %collective-permute-done.2 = bf16[1024,512]{1,0:T(8,128)(2,1)S(1)} collective-permute-done((bf16[1024,512]{1,0:T(8,128)(2,1)S(1)}, bf16[1024,512]{1,0:T(8,128)(2,1)S(1)}, u32[]{:S(2)}, u32[]{:S(2)}) %collective-permute-start.2) | collective-permute-done | bytes 1048608 | tf_op jit(solution)/shard_map/ppermute | solution.py:31
  47.8 0.0 copy-start.4
  47.8 1.7 pad_maximum_fusion
  49.5 2.7 %collective-permute-start.3 = (bf16[2,1024,512]{2,1,0:T(8,128)(2,1)}, bf16[2,1024,512]{2,1,0:T(8,128)(2,1)}, u32[]{:S(2)}, u32[]{:S(2)}) collective-permute-start(bf16[2,1024,512]{2,1,0:T(8,128)(2,1)} %pad_maximum_fusion), channel_id=1, source_target_pairs={{0,32},{32,0},{64,96},{96,64},{1,33},{33,1},{65,97},{97,65},{2,34}... | collective-permute-start | bytes 6291464 | tf_op jit(solution)/shard_map/ppermute | solution.py:33
  52.2 0.1 fusion.28
  52.2 0.0 copy-done.5
  52.2 1.1 broadcast_add_fusion
  53.4 0.0 copy-done
  53.4 0.7 gather_fusion.1
  54.0 0.0 collective-permute-done
  54.0 0.3 collective-permute-start.1
  54.3 0.0 copy-done.4
  54.3 0.6 gather_fusion.3
  55.0 0.0 copy-done.2
  55.0 0.3 copy.11
  55.3 2.2 collective-permute-done.1
  57.5 0.1 fusion.25
  57.6 0.2 reduce_window_sum.11
  57.8 0.1 select_reduce_fusion.1
  57.9 0.1 reshape.206
  58.0 0.1 reshape.226
  58.1 0.7 gather_fusion.2
  58.8 0.1 reshape.225
  58.9 0.1 select_reduce_fusion
  59.0 140.2 %all-reduce.2.cloned.1.call-done = bf16[12,1024,512]{2,1,0:T(8,128)(2,1)} async-done(((bf16[12,1024,512]{2,1,0:T(8,128)(2,1)}), bf16[12,1024,512]{2,1,0:T(8,128)(2,1)}) %all-reduce.2.cloned.1.call-update) | async-done | bytes 12582928 | tf_op jit(solution)/shard_map/psum | solution.py:26
  199.1 11.7 %gather_fusion = bf16[16,1024,512]{2,1,0:T(8,128)(2,1)} fusion(bf16[12,1024,512]{2,1,0:T(8,128)(2,1)} %all-reduce.2.cloned.1.call-done, s32[1024]{0:T(1024)S(1)} %pad_clamp_fusion.3), kind=kCustom, calls=%fused_computation | custom fusion | bytes 33554496 | tf_op jit(solution)/shard_map/jit(_take)/gather | solution.py:48
  210.8 21.7 %copy.12 = bf16[4,4,1024,512]{2,3,1,0:T(8,128)(2,1)} copy(bf16[4,4,1024,512]{3,2,1,0:T(8,128)(2,1)} %bitcast.42) | data formatting | bytes 33554432 | tf_op jit(solution)/shard_map/jit(_take)/gather | solution.py:48
  232.5 0.0 collective-permute-done.3
  232.5 0.0 copy-start.1
  232.5 14.5 %convert_reduce_fusion = f32[512,512]{1,0:T(8,128)S(1)} fusion(f32[4,4]{1,0:T(4,128)S(1)} %select_reduce_fusion, f32[4]{0:T(128)S(1)} %gather_fusion.3, f32[4,4]{1,0:T(4,128)S(1)} %reshape.225, f32[512,512]{1,0:T(8,128)} %broadcast_add_fusion, bf16[2,1024,512]{2,1,0:T(8,128)(2,1)} %collective-permute-done.3, bf16[1,1024,512]{2,1,0:T(8,128)(2,1)} %bitcast.46, ...), kind=kOutput, calls=%fused_computation.4 | convolution fusion | flops 8631615488 | bytes 23068832 | tf_op jit(solution)/shard_map/qkxa,qxb->qkab/dot_general | solution.py:51
  247.0 2.0 fusion.23
  249.0 3.0 %fusion.12 = f32[1,512,512]{2,1,0:T(8,128)} fusion(f32[512,512]{1,0:T(8,128)S(1)} %fusion.23, f32[512,512]{1,0:T(8,128)S(1)} %convert_reduce_fusion, f32[512,512]{1,0:T(8,128)S(1)} %copy-done.2, f32[512,512]{0,1:T(8,128)S(1)} %copy.11, f32[512]{0:T(512)S(1)} %copy-done.5), kind=kOutput, calls=%fused_computation.18 | convolution fusion | flops 1612185600 | bytes 5244928 | tf_op jit(solution)/shard_map/dot_general | solution.py:63
  252.0 0.0 copy-done.1
  (13 shorter events, 0.1 us)
Async XLA Ops:
  6.5 46.8 %copy-start = (f32[128]{0:T(128)S(1)}, f32[128]{0:T(128)}, u32[]{:S(2)}) copy-start(f32[128]{0:T(128)} %param.8) | copy-start | bytes 1540
  6.5 192.6 %all-reduce.2.cloned.1.call-start = ((), (), s32[]{:S(2)}) async-start(), calls=%async_computation | async-start | bytes 25165824 | tf_op jit(solution)/shard_map/psum | solution.py:26
  7.3 6.7 %copy-start.3 = (bf16[1,1024,512]{2,1,0:T(8,128)(2,1)S(1)}, bf16[1,1024,512]{2,1,0:T(8,128)(2,1)}, u32[]{:S(2)}) copy-start(bf16[1,1024,512]{2,1,0:T(8,128)(2,1)} %param.7) | copy-start | bytes 3145732
  7.3 11.2 %copy-start.6 = (s32[12,1]{0,1:T(1,128)S(1)}, s32[12,1]{0,1:T(1,128)}, u32[]{:S(2)}) copy-start(s32[12,1]{0,1:T(1,128)} %param.12) | copy-start | bytes 148
  7.3 11.2 %copy-start.7 = (f32[12]{0:T(128)S(1)}, f32[12]{0:T(128)}, u32[]{:S(2)}) copy-start(f32[12]{0:T(128)} %param.13) | copy-start | bytes 148
  7.3 44.9 %copy-start.5 = (f32[512]{0:T(512)S(1)}, f32[512]{0:T(512)}, u32[]{:S(2)}) copy-start(f32[512]{0:T(512)} %param.9) | copy-start | bytes 6148
  14.0 41.0 %copy-start.2 = (f32[512,512]{1,0:T(8,128)S(1)}, f32[512,512]{1,0:T(8,128)}, u32[]{:S(2)}) copy-start(f32[512,512]{1,0:T(8,128)} %param.10) | copy-start | bytes 3145732
  14.0 33.8 %collective-permute-start.2 = (bf16[1024,512]{1,0:T(8,128)(2,1)S(1)}, bf16[1024,512]{1,0:T(8,128)(2,1)S(1)}, u32[]{:S(2)}, u32[]{:S(2)}) collective-permute-start(bf16[1024,512]{1,0:T(8,128)(2,1)S(1)} %bitcast.44), channel_id=1, source_target_pairs={{0,64},{32,96},{64,0},{96,32},{1,65},{33,97},{65,1},{97,33},{2,66}... | collective-permute-start | bytes 3145736 | tf_op jit(solution)/shard_map/ppermute | solution.py:31
  18.6 35.4 %collective-permute-start = (f32[24]{0:T(128)S(1)}, f32[24]{0:T(128)S(1)}, u32[]{:S(2)}, u32[]{:S(2)}) collective-permute-start(f32[24]{0:T(128)S(1)} %pad_maximum_fusion.3), channel_id=1, source_target_pairs={{0,64},{32,96},{64,0},{96,32},{1,65},{33,97},{65,1},{97,33},{2,66}... | collective-permute-start | bytes 296 | tf_op jit(solution)/shard_map/ppermute | solution.py:32
  47.8 6.5 %copy-start.4 = (bf16[1024,512]{1,0:T(8,128)(2,1)}, bf16[1024,512]{1,0:T(8,128)(2,1)S(1)}, u32[]{:S(2)}) copy-start(bf16[1024,512]{1,0:T(8,128)(2,1)S(1)} %collective-permute-done.2) | copy-start | bytes 3145732
  49.5 183.0 %collective-permute-start.3 = (bf16[2,1024,512]{2,1,0:T(8,128)(2,1)}, bf16[2,1024,512]{2,1,0:T(8,128)(2,1)}, u32[]{:S(2)}, u32[]{:S(2)}) collective-permute-start(bf16[2,1024,512]{2,1,0:T(8,128)(2,1)} %pad_maximum_fusion), channel_id=1, source_target_pairs={{0,32},{32,0},{64,96},{96,64},{1,33},{33,1},{65,97},{97,65},{2,34}... | collective-permute-start | bytes 6291464 | tf_op jit(solution)/shard_map/ppermute | solution.py:33
  54.0 3.5 %collective-permute-start.1 = (f32[2,24]{1,0:T(2,128)S(1)}, f32[2,24]{1,0:T(2,128)S(1)}, u32[]{:S(2)}, u32[]{:S(2)}) collective-permute-start(f32[2,24]{1,0:T(2,128)S(1)} %pad_maximum_fusion.2), channel_id=1, source_target_pairs={{0,32},{32,0},{64,96},{96,64},{1,33},{33,1},{65,97},{97,65},{2,34}... | collective-permute-start | bytes 584 | tf_op jit(solution)/shard_map/ppermute | solution.py:34
  232.5 19.5 %copy-start.1 = (f32[128]{0:T(128)S(1)}, f32[128]{0:T(128)}, u32[]{:S(2)}) copy-start(f32[128]{0:T(128)} %param.8) | copy-start | bytes 1540
Sparse Core Ops, SparseCore 0:
  14.2 184.9 all-reduce.1

commit v2 on v1

--- a/solution.py
+++ b/solution.py
@@ -20,8 +20,9 @@
 
     groups_range = jnp.arange(group_count, dtype=jnp.int32)
     i_ids = (groups_range[None, :] * orbit_count + i_plan).reshape(tile_count)
+    own_turned = own_panel.T
     masked = jnp.where(
-        (i_ids == my_orbital)[:, None, None], own_panel[None], jnp.zeros((), own_panel.dtype)
+        (i_ids == my_orbital)[:, None, None], own_turned[None], jnp.zeros((), own_panel.dtype)
     )
     broadcast = lax.psum(masked, ("grp", "orb"))
 
@@ -45,18 +46,17 @@
     slot_tile = jnp.sum(jnp.where(slot_hit, tile_range, 0), axis=2)
     slot_weight = jnp.sum(jnp.where(slot_hit, weights[:, None, :], 0.0), axis=2)
 
-    gathered = jnp.take(broadcast, slot_tile.reshape(-1), axis=0).reshape(
-        group_count, CAP, *own_panel.shape
-    )
-    integral = jnp.einsum(
-        "qkxa,qxb->qkab", gathered, column, preferred_element_type=jnp.float32
-    )
     pair_sum = virt_energy[:, None] + virt_energy[None, :]
     i_energy = occ_energy[i_ids][slot_tile]
     j_energy = occ_energy[source_groups * orbit_count + my_index]
-    denominator = (pair_sum[None, None] - i_energy[:, :, None, None]) - j_energy[:, None, None, None]
-    amplitude = ((integral / denominator) * slot_weight[:, :, None, None]).astype(jnp.bfloat16)
-    summed = jnp.sum(amplitude.astype(jnp.float32), axis=(0, 1))
+    summed = jnp.zeros((NVIR, NVIR), jnp.float32)
+    for q in range(group_count):
+        for k in range(CAP):
+            left_panel = lax.dynamic_index_in_dim(broadcast, slot_tile[q, k], 0, keepdims=False)
+            integral = jnp.dot(left_panel, column[q], preferred_element_type=jnp.float32)
+            denominator = (pair_sum - i_energy[q, k]) - j_energy[q]
+            amplitude = ((integral / denominator) * slot_weight[q, k]).astype(jnp.bfloat16)
+            summed = summed + amplitude.astype(jnp.float32)
 
     fock_matrix = jnp.diag(virt_energy) + 0.5 * (fock_off + fock_off.T)
     left = jnp.dot(fock_matrix, summed, precision=highest)

time: 260 us -> 271 us (1.042)
  matrix products: 19.4 us -> 62.8 us
  waiting for transfers between devices: 171 us -> 137 us
  between operations: 13.5 us -> 44.4 us
  local copies, waits for them, and re-layouts: 36.1 us -> 6.9 us
    dot_general x1 -> x16, matrix products: 14.5 us -> 57.8 us  [shards(): jnp.dot(left_panel, column[q], preferred_element_type=jnp.float32)]
    gather x2 -> x0, local copies, waits for them, and re-layouts: 33.4 us -> none  [shards(): jnp.take(broadcast, slot_tile.reshape(-1), axis=0)]
    psum x1, waiting for transfers between devices: 140 us -> 108 us  [shards(): broadcast = lax.psum(masked, ('grp', 'orb'))]
    ppermute x1, starting transfers between devices: 4.49 us -> 0.09 us  [shards(): far_panel = lax.ppermute(own_panel, 'grp', across)]
    ppermute x1, starting transfers between devices: 0.06 us -> 4.43 us  [shards(): far_meta = lax.ppermute(meta, 'grp', across)]
    slice x0 -> x4, local copies, waits for them, and re-layouts: none -> 2.76 us  [the longest x2 1.33 us: shards(): denominator = pair_sum - i_energy[q, k] - j_energy[q]]
    select_n x2 -> x1, other arithmetic: 6.67 us -> 5.37 us  [shards(): jnp.where((i_ids == my_orbital)[:, None, None], own_turned[None], jnp.zer...]
  transfers between devices with their start and end apart: 5 -> 5, of which waited for: 3 -> 2; matrix products, arithmetic and copies ran while one was open for 15% -> 8% of each run, Pallas kernels for 0% -> 0%
where the time goes in v2:
time: 271 us; the launch traced here: 270 us
  waiting for transfers between devices  137 us (51%)
  matrix products  62.8 us (23%)
  between operations  44.4 us (16%)
  other arithmetic  9.6 us (4%)
  starting transfers between devices  8.84 us (3%)
  local copies, waits for them, and re-layouts  6.9 us (3%)
    psum x1, waiting for transfers between devices, shards(): broadcast = lax.psum(masked, ('grp', 'orb'))  108 us
    dot_general x16, matrix products, shards(): jnp.dot(left_panel, column[q], preferred_element_type=jnp.float32)  57.8 us
    ppermute x1, waiting for transfers between devices, shards(): far_panel = lax.ppermute(own_panel, 'grp', across)  28.9 us
  transfers between devices with their start and end apart: 5, of which 2 were waited for; matrix products, arithmetic and copies ran while one was open for 8% of the time, Pallas kernels for 0%

profile of v2, /device:TPU:1, one launch (start us, length us, event | category | flops | bytes accessed | tf_op | source)
XLA Modules:
  0.0 269.9 jit_solution(11144479260769304966)
XLA Ops:
  6.5 0.0 copy-start
  6.5 0.0 all-reduce.2.cloned.1.call-start
  6.5 0.7 broadcast_compare_fusion
  7.2 0.1 eq.39
  7.3 1.5 copy.13
  8.8 0.0 copy-start.4
  8.8 0.0 copy-start.5
  8.8 0.0 copy-start.1
  8.9 5.4 %broadcast_select_fusion = bf16[12,512,1024]{2,1,0:T(8,128)(2,1)} fusion(pred[12]{0:T(512)(128)(4,1)S(1)} %eq.39, bf16[512,1024]{1,0:T(8,128)(2,1)S(1)} %copy.13), kind=kLoop, calls=%fused_computation.3 | loop fusion | flops 6291456 | bytes 13631500 | tf_op jit(solution)/shard_map/jit(_where)/select_n | solution.py:24
  14.2 0.0 copy-start.3
  14.2 0.0 all-reduce.2.cloned.1.call-update
  14.2 0.0 copy-done.4
  14.3 0.0 copy-done.5
  14.3 0.1 pad_maximum_fusion.3
  14.4 4.4 %collective-permute-start = (f32[24]{0:T(128)S(1)}, f32[24]{0:T(128)S(1)}, u32[]{:S(2)}, u32[]{:S(2)}) collective-permute-start(f32[24]{0:T(128)S(1)} %pad_maximum_fusion.3), channel_id=1, source_target_pairs={{0,64},{32,96},{64,0},{96,32},{1,65},{33,97},{65,1},{97,33},{2,66}... | collective-permute-start | bytes 296 | tf_op jit(solution)/shard_map/ppermute | solution.py:33
  18.8 0.1 collective-permute-start.2
  18.9 0.1 fusion.132
  19.0 0.1 reshape.140
  19.1 0.0 copy-done
  19.1 0.6 gather_fusion.2
  19.7 0.1 fusion.152
  19.8 0.6 fusion.145
  20.4 0.0 collective-permute-done
  20.4 1.0 collective-permute-start.1
  21.4 0.7 gather_fusion
  22.1 0.0 copy-done.1
  22.1 0.3 copy.12
  22.5 0.0 collective-permute-done.1
  22.5 0.1 fusion.141
  22.6 0.2 reduce_window_sum.11
  22.7 28.9 %collective-permute-done.2 = bf16[1024,512]{1,0:T(8,128)(2,1)S(1)} collective-permute-done((bf16[1024,512]{1,0:T(8,128)(2,1)}, bf16[1024,512]{1,0:T(8,128)(2,1)S(1)}, u32[]{:S(2)}, u32[]{:S(2)}) %collective-permute-start.2) | collective-permute-done | bytes 1048608 | tf_op jit(solution)/shard_map/ppermute | solution.py:32
  51.6 2.7 %pad_maximum_fusion = bf16[2,1024,512]{2,1,0:T(8,128)(2,1)} fusion(bf16[1,1024,512]{2,1,0:T(8,128)(2,1)S(1)} %bitcast.158, bf16[1,1024,512]{2,1,0:T(8,128)(2,1)} %param.7), kind=kLoop, calls=%fused_computation.20 | loop fusion | flops 1048576 | bytes 4194304 | tf_op jit(solution)/shard_map/stack | solution.py:34
  54.4 3.3 %collective-permute-start.3 = (bf16[2,1024,512]{2,1,0:T(8,128)(2,1)}, bf16[2,1024,512]{2,1,0:T(8,128)(2,1)}, u32[]{:S(2)}, u32[]{:S(2)}) collective-permute-start(bf16[2,1024,512]{2,1,0:T(8,128)(2,1)} %pad_maximum_fusion), channel_id=1, source_target_pairs={{0,32},{32,0},{64,96},{96,64},{1,33},{33,1},{65,97},{97,65},{2,34}... | collective-permute-start | bytes 6291464 | tf_op jit(solution)/shard_map/ppermute | solution.py:34
  57.7 0.1 select_reduce_fusion.1
  57.8 0.7 fusion.144
  79.0 0.1 reshape.151
  79.1 0.7 gather_fusion.1
  79.8 0.1 reshape.150
  90.1 0.1 select_reduce_fusion
  90.2 0.7 fusion.142
  90.9 0.7 fusion.143
  91.6 108.5 %all-reduce.2.cloned.1.call-done = bf16[12,512,1024]{2,1,0:T(8,128)(2,1)} async-done(((bf16[12,512,1024]{2,1,0:T(8,128)(2,1)}), bf16[12,512,1024]{2,1,0:T(8,128)(2,1)}) %all-reduce.2.cloned.1.call-update) | async-done | bytes 12582928 | tf_op jit(solution)/shard_map/psum | solution.py:27
  200.1 0.0 copy-start.2
  200.1 0.0 copy-done.3
  200.1 4.8 %fusion.23 = f32[512,512]{1,0:T(8,128)S(1)} fusion(bf16[12,512,1024]{2,1,0:T(8,128)(2,1)} %all-reduce.2.cloned.1.call-done, s32[]{:T(128)S(6)} %select_n.104, f32[]{:T(128)} %bitcast.21, f32[]{:T(128)} %bitcast.20, f32[]{:T(128)} %bitcast.16, f32[512]{0:T(512)S(1)} %copy-done.3, bf16[1,1024,512]{2,1,0:T(8,128)(2,1)} %param.7), kind=kOutput, calls=%fused_computation.61 | convolution fusion | flops 538705920 | bytes 3151364 | tf_op jit(solution)/shard_map/dot_general | solution.py:56
  204.9 4.1 %fusion.25 = f32[512,512]{1,0:T(8,128)S(1)} fusion(bf16[12,512,1024]{2,1,0:T(8,128)(2,1)} %all-reduce.2.cloned.1.call-done, s32[]{:T(128)S(6)} %select_n.105, f32[]{:T(128)} %bitcast.25, f32[]{:T(128)} %bitcast.24, f32[]{:T(128)} %bitcast.16, f32[512]{0:T(512)S(1)} %copy-done.3, bf16[1,1024,512]{2,1,0:T(8,128)(2,1)} %param.7), kind=kOutput, calls=%fused_computation.63 | convolution fusion | flops 538705920 | bytes 3151364 | tf_op jit(solution)/shard_map/dot_general | solution.py:56
  209.0 0.0 copy-done.2
  209.0 3.8 %fusion.27 = f32[512,512]{1,0:T(8,128)S(1)} fusion(bf16[12,512,1024]{2,1,0:T(8,128)(2,1)S(1)} %copy-done.2, s32[]{:T(128)S(6)} %select_n.106, f32[]{:T(128)} %bitcast.29, f32[]{:T(128)} %bitcast.28, f32[]{:T(128)} %bitcast.16, f32[512]{0:T(512)S(1)} %copy-done.3, bf16[1,1024,512]{2,1,0:T(8,128)(2,1)} %param.7), kind=kOutput, calls=%fused_computation.65 | convolution fusion | flops 538705920 | bytes 3149840 | tf_op jit(solution)/shard_map/dot_general | solution.py:56
  212.8 0.0 collective-permute-done.3
  212.8 3.9 %fusion.49 = f32[512,512]{1,0:T(8,128)S(1)} fusion(bf16[12,512,1024]{2,1,0:T(8,128)(2,1)S(1)} %copy-done.2, s32[]{:T(128)S(6)} %select_n.111, bf16[2,1024,512]{2,1,0:T(8,128)(2,1)} %collective-permute-done.3, f32[]{:T(128)} %bitcast.53, f32[]{:T(128)} %bitcast.52, f32[]{:T(128)} %bitcast.51, f32[512]{0:T(512)S(1)} %copy-done.3), kind=kOutput, calls=%fused_computation.87 | convolution fusion | flops 538705920 | bytes 3151364 | tf_op jit(solution)/shard_map/dot_general | solution.py:56
  216.7 3.9 %fusion.51 = f32[512,512]{1,0:T(8,128)S(1)} fusion(bf16[12,512,1024]{2,1,0:T(8,128)(2,1)S(1)} %copy-done.2, s32[]{:T(128)S(6)} %select_n.112, bf16[2,1024,512]{2,1,0:T(8,128)(2,1)} %collective-permute-done.3, f32[]{:T(128)} %bitcast.57, f32[]{:T(128)} %bitcast.56, f32[]{:T(128)} %bitcast.52, f32[512]{0:T(512)S(1)} %copy-done.3), kind=kOutput, calls=%fused_computation.89 | convolution fusion | flops 538705920 | bytes 3151364 | tf_op jit(solution)/shard_map/dot_general | solution.py:56
  220.6 3.9 %fusion.53 = f32[512,512]{1,0:T(8,128)S(1)} fusion(bf16[12,512,1024]{2,1,0:T(8,128)(2,1)S(1)} %copy-done.2, s32[]{:T(128)S(6)} %select_n.113, bf16[2,1024,512]{2,1,0:T(8,128)(2,1)} %collective-permute-done.3, f32[]{:T(128)} %bitcast.61, f32[]{:T(128)} %bitcast.60, f32[]{:T(128)} %bitcast.52, f32[512]{0:T(512)S(1)} %copy-done.3), kind=kOutput, calls=%fused_computation.91 | convolution fusion | flops 538705920 | bytes 3151364 | tf_op jit(solution)/shard_map/dot_general | solution.py:56
  224.5 3.9 %fusion.55 = f32[512,512]{1,0:T(8,128)S(1)} fusion(bf16[12,512,1024]{2,1,0:T(8,128)(2,1)S(1)} %copy-done.2, s32[]{:T(128)S(6)} %select_n.114, bf16[2,1024,512]{2,1,0:T(8,128)(2,1)} %collective-permute-done.3, f32[]{:T(128)} %bitcast.65, f32[]{:T(128)} %bitcast.64, f32[]{:T(128)} %bitcast.52, f32[512]{0:T(512)S(1)} %copy-done.3), kind=kOutput, calls=%fused_computation.93 | convolution fusion | flops 538705920 | bytes 3151364 | tf_op jit(solution)/shard_map/dot_general | solution.py:56
  228.4 3.7 %fusion.57 = f32[512,512]{1,0:T(8,128)S(1)} fusion(bf16[12,512,1024]{2,1,0:T(8,128)(2,1)S(1)} %copy-done.2, s32[]{:T(128)S(6)} %select_n.115, bf16[2,1024,512]{2,1,0:T(8,128)(2,1)} %collective-permute-done.3, f32[]{:T(128)} %bitcast.71, f32[]{:T(128)} %bitcast.70, f32[]{:T(128)} %bitcast.69, f32[512]{0:T(512)S(1)} %copy-done.3), kind=kOutput, calls=%fused_computation.95 | convolution fusion | flops 538705920 | bytes 3151364 | tf_op jit(solution)/shard_map/dot_general | solution.py:56
  232.1 3.8 %fusion.59 = f32[512,512]{1,0:T(8,128)S(1)} fusion(bf16[12,512,1024]{2,1,0:T(8,128)(2,1)S(1)} %copy-done.2, s32[]{:T(128)S(6)} %select_n.116, bf16[2,1024,512]{2,1,0:T(8,128)(2,1)} %collective-permute-done.3, f32[]{:T(128)} %bitcast.75, f32[]{:T(128)} %bitcast.74, f32[]{:T(128)} %bitcast.70, f32[512]{0:T(512)S(1)} %copy-done.3), kind=kOutput, calls=%fused_computation.97 | convolution fusion | flops 538705920 | bytes 3151364 | tf_op jit(solution)/shard_map/dot_general | solution.py:56
  235.9 3.7 %fusion.61 = f32[512,512]{1,0:T(8,128)S(1)} fusion(bf16[12,512,1024]{2,1,0:T(8,128)(2,1)S(1)} %copy-done.2, s32[]{:T(128)S(6)} %select_n.117, bf16[2,1024,512]{2,1,0:T(8,128)(2,1)} %collective-permute-done.3, f32[]{:T(128)} %bitcast.79, f32[]{:T(128)} %bitcast.78, f32[]{:T(128)} %bitcast.70, f32[512]{0:T(512)S(1)} %copy-done.3), kind=kOutput, calls=%fused_computation.99 | convolution fusion | flops 538705920 | bytes 3151364 | tf_op jit(solution)/shard_map/dot_general | solution.py:56
  239.7 3.8 %fusion.63 = f32[512,512]{1,0:T(8,128)S(1)} fusion(bf16[12,512,1024]{2,1,0:T(8,128)(2,1)S(1)} %copy-done.2, s32[]{:T(128)S(6)} %select_n.118, bf16[2,1024,512]{2,1,0:T(8,128)(2,1)} %collective-permute-done.3, f32[]{:T(128)} %bitcast.83, f32[]{:T(128)} %bitcast.82, f32[]{:T(128)} %bitcast.70, f32[512]{0:T(512)S(1)} %copy-done.3), kind=kOutput, calls=%fused_computation.101 | convolution fusion | flops 538705920 | bytes 3151364 | tf_op jit(solution)/shard_map/dot_general | solution.py:56
  243.5 2.5 fusion.43
  245.9 2.6 fusion.45
  248.5 2.5 fusion.47
  251.0 4.0 %fusion.21 = f32[512,512]{1,0:T(8,128)S(1)} fusion(f32[512,512]{1,0:T(8,128)S(1)} %fusion.27, f32[512,512]{1,0:T(8,128)S(1)} %fusion.25, f32[512,512]{1,0:T(8,128)S(1)} %fusion.23, bf16[12,512,1024]{2,1,0:T(8,128)(2,1)S(1)} %copy-done.2, s32[]{:T(128)S(6)} %select_n.99, f32[]{:T(128)} %bitcast.17, f32[]{:T(128)} %bitcast.16, f32[]{:T(128)} %bitcast.10, ...), kind=kOutput, calls=%fused_computation.59 | convolution fusion | flops 539492352 | bytes 6295568 | tf_op jit(solution)/shard_map/dot_general | solution.py:56
  255.0 3.1 %fusion.41 = f32[512,512]{1,0:T(8,128)S(1)} fusion(f32[512,512]{1,0:T(8,128)S(1)} %fusion.63, f32[512,512]{1,0:T(8,128)S(1)} %fusion.61, f32[512,512]{1,0:T(8,128)S(1)} %fusion.59, f32[512,512]{1,0:T(8,128)S(1)} %fusion.57, f32[512,512]{1,0:T(8,128)S(1)} %fusion.55, f32[512,512]{1,0:T(8,128)S(1)} %fusion.53, f32[512,512]{1,0:T(8,128)S(1)} %fusion.51, ...), kind=kOutput, calls=%fused_computation.79 | convolution fusion | flops 541851648 | bytes 15732752 | tf_op jit(solution)/shard_map/dot_general | solution.py:56
  258.1 2.0 fusion.139
  260.0 3.0 %fusion = f32[1,512,512]{2,1,0:T(8,128)} fusion(f32[512,512]{1,0:T(8,128)S(1)} %fusion.139, f32[512,512]{1,0:T(8,128)S(1)} %fusion.41, f32[512,512]{1,0:T(8,128)S(1)} %copy-done.1, f32[512,512]{0,1:T(8,128)S(1)} %copy.12, f32[512]{0:T(512)S(1)} %copy-done.3), kind=kOutput, calls=%fused_computation.22 | convolution fusion | flops 1612185600 | bytes 5244928 | tf_op jit(solution)/shard_map/dot_general | solution.py:63
  (10 shorter events, 0.1 us)
Async XLA Ops:
  6.5 12.5 %copy-start = (f32[128]{0:T(128)S(1)}, f32[128]{0:T(128)}, u32[]{:S(2)}) copy-start(f32[128]{0:T(128)} %param.8) | copy-start | bytes 1540
  6.5 193.6 %all-reduce.2.cloned.1.call-start = ((), (), s32[]{:S(2)}) async-start(), calls=%async_computation | async-start | bytes 25165824 | tf_op jit(solution)/shard_map/psum | solution.py:27
  8.8 5.4 %copy-start.4 = (s32[12,1]{0,1:T(1,128)S(1)}, s32[12,1]{0,1:T(1,128)}, u32[]{:S(2)}) copy-start(s32[12,1]{0,1:T(1,128)} %param.12) | copy-start | bytes 148
  8.8 5.4 %copy-start.5 = (f32[12]{0:T(128)S(1)}, f32[12]{0:T(128)}, u32[]{:S(2)}) copy-start(f32[12]{0:T(128)} %param.13) | copy-start | bytes 148
  8.8 13.3 %copy-start.1 = (f32[512,512]{1,0:T(8,128)S(1)}, f32[512,512]{1,0:T(8,128)}, u32[]{:S(2)}) copy-start(f32[512,512]{1,0:T(8,128)} %param.10) | copy-start | bytes 3145732
  14.2 185.9 %copy-start.3 = (f32[512]{0:T(512)S(1)}, f32[512]{0:T(512)}, u32[]{:S(2)}) copy-start(f32[512]{0:T(512)} %param.9) | copy-start | bytes 6148
  14.4 6.0 %collective-permute-start = (f32[24]{0:T(128)S(1)}, f32[24]{0:T(128)S(1)}, u32[]{:S(2)}, u32[]{:S(2)}) collective-permute-start(f32[24]{0:T(128)S(1)} %pad_maximum_fusion.3), channel_id=1, source_target_pairs={{0,64},{32,96},{64,0},{96,32},{1,65},{33,97},{65,1},{97,33},{2,66}... | collective-permute-start | bytes 296 | tf_op jit(solution)/shard_map/ppermute | solution.py:33
  18.8 32.9 %collective-permute-start.2 = (bf16[1024,512]{1,0:T(8,128)(2,1)}, bf16[1024,512]{1,0:T(8,128)(2,1)S(1)}, u32[]{:S(2)}, u32[]{:S(2)}) collective-permute-start(bf16[1024,512]{1,0:T(8,128)(2,1)} %bitcast.1), channel_id=1, source_target_pairs={{0,64},{32,96},{64,0},{96,32},{1,65},{33,97},{65,1},{97,33},{2,66}... | collective-permute-start | bytes 3145736 | tf_op jit(solution)/shard_map/ppermute | solution.py:32
  20.4 2.0 collective-permute-start.1
  54.4 158.4 %collective-permute-start.3 = (bf16[2,1024,512]{2,1,0:T(8,128)(2,1)}, bf16[2,1024,512]{2,1,0:T(8,128)(2,1)}, u32[]{:S(2)}, u32[]{:S(2)}) collective-permute-start(bf16[2,1024,512]{2,1,0:T(8,128)(2,1)} %pad_maximum_fusion), channel_id=1, source_target_pairs={{0,32},{32,0},{64,96},{96,64},{1,33},{33,1},{65,97},{97,65},{2,34}... | collective-permute-start | bytes 6291464 | tf_op jit(solution)/shard_map/ppermute | solution.py:34
  200.1 8.9 %copy-start.2 = (bf16[12,512,1024]{2,1,0:T(8,128)(2,1)S(1)}, bf16[12,512,1024]{2,1,0:T(8,128)(2,1)}, u32[]{:S(2)}) copy-start(bf16[12,512,1024]{2,1,0:T(8,128)(2,1)} %all-reduce.2.cloned.1.call-done) | copy-start | bytes 37748740
Sparse Core Ops, SparseCore 0:
  14.4 185.6 all-reduce.1

commit v3 on v2

--- a/solution.py
+++ b/solution.py
@@ -2,10 +2,51 @@
 import jax.numpy as jnp
 from jax import lax
 from jax.sharding import PartitionSpec as P
+from jax.experimental import pallas as pl
+from jax.experimental.pallas import tpu as pltpu
 
 NVIR = 512
 STEPS = 3
 CAP = 4
+
+
+def slot_kernel(tiles_ref, scalars_ref, left_ref, right_ref, pair_ref, out_ref):
+    step = pl.program_id(0)
+    slots = pl.num_programs(0)
+    integral = jnp.dot(left_ref[...], right_ref[...], preferred_element_type=jnp.float32)
+    denominator = (pair_ref[...] - scalars_ref[step]) - scalars_ref[slots + step]
+    amplitude = ((integral / denominator) * scalars_ref[2 * slots + step]).astype(jnp.bfloat16)
+
+    @pl.when(step == 0)
+    def _():
+        out_ref[...] = amplitude.astype(jnp.float32)
+
+    @pl.when(step > 0)
+    def _():
+        out_ref[...] += amplitude.astype(jnp.float32)
+
+
+def summed_tiles(slot_tile, scalars, broadcast, column, pair_sum):
+    slots = slot_tile.shape[0]
+    per_source = slots // column.shape[0]
+    _, rows, depth = broadcast.shape
+    grid_spec = pltpu.PrefetchScalarGridSpec(
+        num_scalar_prefetch=1,
+        grid=(slots,),
+        in_specs=[
+            pl.BlockSpec(memory_space=pltpu.SMEM),
+            pl.BlockSpec((None, rows, depth), lambda s, tiles: (tiles[s], 0, 0)),
+            pl.BlockSpec((None, depth, rows), lambda s, tiles: (s // per_source, 0, 0)),
+            pl.BlockSpec((rows, rows), lambda s, tiles: (0, 0)),
+        ],
+        out_specs=pl.BlockSpec((rows, rows), lambda s, tiles: (0, 0)),
+    )
+    return pl.pallas_call(
+        slot_kernel,
+        grid_spec=grid_spec,
+        out_shape=jax.ShapeDtypeStruct((rows, rows), jnp.float32),
+        compiler_params=pltpu.CompilerParams(dimension_semantics=("arbitrary",)),
+    )(slot_tile, scalars, broadcast, column, pair_sum)
 
 
 def shards(df_panels, occ_energy, virt_energy, fock_off, i_plan, pair_owner, pair_weight):
@@ -49,14 +90,14 @@
     pair_sum = virt_energy[:, None] + virt_energy[None, :]
     i_energy = occ_energy[i_ids][slot_tile]
     j_energy = occ_energy[source_groups * orbit_count + my_index]
-    summed = jnp.zeros((NVIR, NVIR), jnp.float32)
-    for q in range(group_count):
-        for k in range(CAP):
-            left_panel = lax.dynamic_index_in_dim(broadcast, slot_tile[q, k], 0, keepdims=False)
-            integral = jnp.dot(left_panel, column[q], preferred_element_type=jnp.float32)
-            denominator = (pair_sum - i_energy[q, k]) - j_energy[q]
-            amplitude = ((integral / denominator) * slot_weight[q, k]).astype(jnp.bfloat16)
-            summed = summed + amplitude.astype(jnp.float32)
+    scalars = jnp.concatenate(
+        [
+            i_energy.reshape(-1),
+            jnp.repeat(j_energy, CAP),
+            slot_weight.reshape(-1),
+        ]
+    )
+    summed = summed_tiles(slot_tile.reshape(-1), scalars, broadcast, column, pair_sum)
 
     fock_matrix = jnp.diag(virt_energy) + 0.5 * (fock_off + fock_off.T)
     left = jnp.dot(fock_matrix, summed, precision=highest)

time: 271 us -> 234 us (0.86)
  matrix products: 62.8 us -> 6.25 us
  between operations: 44.4 us -> 13.5 us
  waiting for transfers between devices: 137 us -> 166 us
  Pallas kernels: 0 us -> 20.4 us
  other arithmetic: 9.6 us -> 13.9 us
    dot_general x16 -> x0, matrix products: 57.8 us -> none  [shards(): jnp.dot(left_panel, column[q], preferred_element_type=jnp.float32)]
    psum x1, waiting for transfers between devices: 108 us -> 135 us  [shards(): broadcast = lax.psum(masked, ('grp', 'orb'))]
    pallas_call x0 -> x1, Pallas kernels: none -> 20.4 us  [summed_tiles(): pl.pallas_call(slot_kernel, grid_spec=grid_spec, out_shape=jax.ShapeDtype...]
    ppermute x1, starting transfers between devices: 4.43 us -> 0.03 us  [shards(): far_meta = lax.ppermute(meta, 'grp', across)]
    ppermute x1, starting transfers between devices: 0.09 us -> 4.41 us  [shards(): far_panel = lax.ppermute(own_panel, 'grp', across)]
    another operation x0 -> x1, other arithmetic: none -> 3.62 us  [shards(): column = jnp.stack([own_panel, far_panel, near[0], near[1]])]
    slice x4 -> x0, local copies, waits for them, and re-layouts: 2.76 us -> none  [the longest x2 1.33 us: shards(): denominator = pair_sum - i_energy[q, k] - j_energy[q]]
  transfers between devices with their start and end apart: 5 -> 5, of which waited for: 2 -> 3; matrix products, arithmetic and copies ran while one was open for 8% -> 5% of each run, Pallas kernels for 0% -> 0%
where the time goes in v3:
time: 234 us
  waiting for transfers between devices  166 us (71%)
  Pallas kernels  20.4 us (9%)
  other arithmetic  13.9 us (6%)
  between operations  13.5 us (6%)
  starting transfers between devices  7.21 us (3%)
  matrix products  6.25 us (3%)
  local copies, waits for them, and re-layouts  6.15 us (3%)
    psum x1, waiting for transfers between devices, shards(): broadcast = lax.psum(masked, ('grp', 'orb'))  135 us
    ppermute x1, waiting for transfers between devices, shards(): far_panel = lax.ppermute(own_panel, 'grp', across)  29.6 us
    pallas_call x1, Pallas kernels, summed_tiles(): pl.pallas_call(slot_kernel, grid_spec=grid_spec, out_shape=jax.ShapeDtype...  20.4 us
    select_n x1, other arithmetic, shards(): jnp.where((i_ids == my_orbital)[:, None, None], own_turned[None], jnp.zer...  5.36 us
  transfers between devices with their start and end apart: 5, of which 3 were waited for; matrix products, arithmetic and copies ran while one was open for 5% of the time, Pallas kernels for 0%

profile of v3, /device:TPU:1, one launch (start us, length us, event | category | flops | bytes accessed | tf_op | source)
XLA Modules:
  0.0 233.6 jit_solution(15787143811907092218)
XLA Ops:
  6.5 0.0 copy-start
  6.5 0.0 all-reduce.2.cloned.1.call-start
  6.5 0.7 broadcast_compare_fusion
  7.2 0.1 eq.44
  7.3 1.5 copy.13
  8.8 5.4 %broadcast_select_fusion = bf16[12,512,1024]{2,1,0:T(8,128)(2,1)} fusion(pred[12]{0:T(512)(128)(4,1)S(1)} %eq.44, bf16[512,1024]{1,0:T(8,128)(2,1)S(1)} %copy.13), kind=kLoop, calls=%fused_computation.3 | loop fusion | flops 6291456 | bytes 13631500 | tf_op jit(solution)/shard_map/jit(_where)/select_n | solution.py:65
  14.2 0.0 copy-start.3
  14.2 0.0 copy-start.6
  14.2 0.0 copy-start.7
  14.2 0.0 all-reduce.2.cloned.1.call-update
  14.2 0.0 copy-start.5
  14.2 0.0 copy-start.2
  14.2 1.2 copy-done.3
  15.4 4.4 %collective-permute-start.2 = (bf16[1024,512]{1,0:T(8,128)(2,1)S(1)}, bf16[1024,512]{1,0:T(8,128)(2,1)S(1)}, u32[]{:S(2)}, u32[]{:S(2)}) collective-permute-start(bf16[1024,512]{1,0:T(8,128)(2,1)S(1)} %bitcast.35), channel_id=1, source_target_pairs={{0,64},{32,96},{64,0},{96,32},{1,65},{33,97},{65,1},{97,33},{2,66}... | collective-permute-start | bytes 3145736 | tf_op jit(solution)/shard_map/ppermute | solution.py:73
  19.8 0.0 copy-done.6
  19.8 0.0 copy-done.7
  19.8 0.1 pad_maximum_fusion.4
  19.9 0.0 collective-permute-start
  19.9 0.1 reshape.153
  20.0 29.6 %collective-permute-done.2 = bf16[1024,512]{1,0:T(8,128)(2,1)S(1)} collective-permute-done((bf16[1024,512]{1,0:T(8,128)(2,1)S(1)}, bf16[1024,512]{1,0:T(8,128)(2,1)S(1)}, u32[]{:S(2)}, u32[]{:S(2)}) %collective-permute-start.2) | collective-permute-done | bytes 1048608 | tf_op jit(solution)/shard_map/ppermute | solution.py:73
  49.7 0.0 copy-start.4
  49.7 1.7 pad_maximum_fusion.1
  51.3 2.7 %collective-permute-start.3 = (bf16[2,1024,512]{2,1,0:T(8,128)(2,1)}, bf16[2,1024,512]{2,1,0:T(8,128)(2,1)}, u32[]{:S(2)}, u32[]{:S(2)}) collective-permute-start(bf16[2,1024,512]{2,1,0:T(8,128)(2,1)} %pad_maximum_fusion.1), channel_id=1, source_target_pairs={{0,32},{32,0},{64,96},{96,64},{1,33},{33,1},{65,97},{97,65},{2,34}... | collective-permute-start | bytes 6291464 | tf_op jit(solution)/shard_map/ppermute | solution.py:75
  54.0 0.0 copy-done.4
  54.0 0.0 copy-done
  54.0 0.7 gather_fusion
  54.7 0.1 fusion.13
  54.8 0.1 fusion.5
  54.9 0.0 copy-done.5
  54.9 1.1 broadcast_add_fusion.pair_ref
  56.0 0.6 gather_fusion.2
  56.6 0.0 collective-permute-done
  56.7 0.1 collective-permute-start.1
  56.7 0.1 broadcast_in_dim.80
  56.8 0.1 reshape.155
  56.9 0.0 copy-done.2
  56.9 0.3 copy.12
  57.2 1.8 collective-permute-done.1
  59.1 0.1 fusion.10
  59.1 0.2 reduce_window_sum.11
  59.3 0.1 select_reduce_fusion.1
  59.5 0.7 reshape.152.tiles_ref
  60.2 0.1 reshape.167
  60.3 0.1 select_reduce_fusion
  60.4 0.1 reshape.156
  60.4 0.7 gather_fusion.1
  61.1 0.7 pad_maximum_fusion.5.scalars_ref
  61.8 0.0 collective-permute-done.3
  61.8 3.6 %pad_maximum_fusion.right_ref = bf16[4,1024,512]{2,1,0:T(8,128)(2,1)} fusion(bf16[2,1024,512]{2,1,0:T(8,128)(2,1)} %collective-permute-done.3, bf16[1,1024,512]{2,1,0:T(8,128)(2,1)} %bitcast.37, bf16[1,1024,512]{2,1,0:T(8,128)(2,1)S(1)} %copy-done.3), kind=kLoop, calls=%fused_computation.4 | loop fusion | flops 4194304 | bytes 8388608 | tf_op jit(solution)/shard_map/stack | solution.py:77
  65.4 134.7 %all-reduce.2.cloned.1.call-done.left_ref = bf16[12,512,1024]{2,1,0:T(8,128)(2,1)} async-done(((bf16[12,512,1024]{2,1,0:T(8,128)(2,1)}), bf16[12,512,1024]{2,1,0:T(8,128)(2,1)}) %all-reduce.2.cloned.1.call-update) | async-done | bytes 12582928 | tf_op jit(solution)/shard_map/psum | solution.py:68
  200.0 20.4 %shard_map.73 = f32[512,512]{1,0:T(8,128)} custom-call(s32[16]{0:T(128)} %reshape.152.tiles_ref, f32[48]{0:T(128)} %pad_maximum_fusion.5.scalars_ref, bf16[12,512,1024]{2,1,0:T(8,128)(2,1)} %all-reduce.2.cloned.1.call-done.left_ref, bf16[4,1024,512]{2,1,0:T(8,128)(2,1)} %pad_maximum_fusion.right_ref, f32[512,512]{1,0:T(8,128)} %broadcast_add_fusion.pair_ref), custom_call_target="tpu_custom_call" | custom-call | tf_op jit(solution)/shard_map/pallas_call | solution.py:44
  220.5 0.0 copy-start.1
  220.5 3.3 %fusion.7 = f32[512,512]{1,0:T(8,128)S(1)} fusion(f32[512,512]{1,0:T(8,128)} %shard_map.73, f32[512,512]{1,0:T(8,128)S(1)} %copy-done.2, f32[512,512]{0,1:T(8,128)S(1)} %copy.12, f32[512]{0:T(512)S(1)} %copy-done.5), kind=kOutput, calls=%fused_computation.37 | convolution fusion | flops 1611923456 | bytes 4196352 | tf_op jit(solution)/shard_map/dot_general | solution.py:104
  223.8 0.0 copy-done.1
  223.8 2.9 %fusion = f32[1,512,512]{2,1,0:T(8,128)} fusion(f32[512,512]{1,0:T(8,128)S(1)} %fusion.7, f32[512,512]{1,0:T(8,128)S(1)} %copy-done.1, f32[512,512]{1,0:T(8,128)S(1)} %copy-done.2, f32[512,512]{0,1:T(8,128)S(1)} %copy.12, f32[512]{0:T(512)S(1)} %copy-done.5), kind=kOutput, calls=%fused_computation.7 | convolution fusion | flops 1612185600 | bytes 5244928 | tf_op jit(solution)/shard_map/dot_general | solution.py:103
  (10 shorter events, 0.1 us)
Async XLA Ops:
  6.5 47.5 %copy-start = (f32[128]{0:T(128)S(1)}, f32[128]{0:T(128)}, u32[]{:S(2)}) copy-start(f32[128]{0:T(128)} %param.8) | copy-start | bytes 1540
  6.5 193.5 %all-reduce.2.cloned.1.call-start = ((), (), s32[]{:S(2)}) async-start(), calls=%async_computation | async-start | bytes 25165824 | tf_op jit(solution)/shard_map/psum | solution.py:68
  14.2 1.2 copy-start.3
  14.2 5.6 %copy-start.6 = (s32[12,1]{0,1:T(1,128)S(1)}, s32[12,1]{0,1:T(1,128)}, u32[]{:S(2)}) copy-start(s32[12,1]{0,1:T(1,128)} %param.12) | copy-start | bytes 148
  14.2 5.6 %copy-start.7 = (f32[12]{0:T(128)S(1)}, f32[12]{0:T(128)}, u32[]{:S(2)}) copy-start(f32[12]{0:T(128)} %param.13) | copy-start | bytes 148
  14.2 40.6 %copy-start.5 = (f32[512]{0:T(512)S(1)}, f32[512]{0:T(512)}, u32[]{:S(2)}) copy-start(f32[512]{0:T(512)} %param.9) | copy-start | bytes 6148
  14.2 42.7 %copy-start.2 = (f32[512,512]{1,0:T(8,128)S(1)}, f32[512,512]{1,0:T(8,128)}, u32[]{:S(2)}) copy-start(f32[512,512]{1,0:T(8,128)} %param.10) | copy-start | bytes 3145732
  15.4 34.3 %collective-permute-start.2 = (bf16[1024,512]{1,0:T(8,128)(2,1)S(1)}, bf16[1024,512]{1,0:T(8,128)(2,1)S(1)}, u32[]{:S(2)}, u32[]{:S(2)}) collective-permute-start(bf16[1024,512]{1,0:T(8,128)(2,1)S(1)} %bitcast.35), channel_id=1, source_target_pairs={{0,64},{32,96},{64,0},{96,32},{1,65},{33,97},{65,1},{97,33},{2,66}... | collective-permute-start | bytes 3145736 | tf_op jit(solution)/shard_map/ppermute | solution.py:73
  19.9 36.7 %collective-permute-start = (f32[24]{0:T(128)S(1)}, f32[24]{0:T(128)S(1)}, u32[]{:S(2)}, u32[]{:S(2)}) collective-permute-start(f32[24]{0:T(128)S(1)} %pad_maximum_fusion.4), channel_id=1, source_target_pairs={{0,64},{32,96},{64,0},{96,32},{1,65},{33,97},{65,1},{97,33},{2,66}... | collective-permute-start | bytes 296 | tf_op jit(solution)/shard_map/ppermute | solution.py:74
  49.7 4.3 %copy-start.4 = (bf16[1024,512]{1,0:T(8,128)(2,1)}, bf16[1024,512]{1,0:T(8,128)(2,1)S(1)}, u32[]{:S(2)}) copy-start(bf16[1024,512]{1,0:T(8,128)(2,1)S(1)} %collective-permute-done.2) | copy-start | bytes 3145732
  51.3 10.4 %collective-permute-start.3 = (bf16[2,1024,512]{2,1,0:T(8,128)(2,1)}, bf16[2,1024,512]{2,1,0:T(8,128)(2,1)}, u32[]{:S(2)}, u32[]{:S(2)}) collective-permute-start(bf16[2,1024,512]{2,1,0:T(8,128)(2,1)} %pad_maximum_fusion.1), channel_id=1, source_target_pairs={{0,32},{32,0},{64,96},{96,64},{1,33},{33,1},{65,97},{97,65},{2,34}... | collective-permute-start | bytes 6291464 | tf_op jit(solution)/shard_map/ppermute | solution.py:75
  56.7 2.4 %collective-permute-start.1 = (f32[2,24]{1,0:T(2,128)S(1)}, f32[2,24]{1,0:T(2,128)S(1)}, u32[]{:S(2)}, u32[]{:S(2)}) collective-permute-start(f32[2,24]{1,0:T(2,128)S(1)} %pad_maximum_fusion.3), channel_id=1, source_target_pairs={{0,32},{32,0},{64,96},{96,64},{1,33},{33,1},{65,97},{97,65},{2,34}... | collective-permute-start | bytes 584 | tf_op jit(solution)/shard_map/ppermute | solution.py:76
  220.5 3.3 %copy-start.1 = (f32[512,512]{1,0:T(8,128)S(1)}, f32[512,512]{1,0:T(8,128)}, u32[]{:S(2)}) copy-start(f32[512,512]{1,0:T(8,128)} %shard_map.73) | copy-start | bytes 3145732
Sparse Core Ops, SparseCore 0:
  14.3 185.6 all-reduce.1

commit v4 on v3

--- a/solution.py
+++ b/solution.py
@@ -1,7 +1,7 @@
 import jax
 import jax.numpy as jnp
 from jax import lax
-from jax.sharding import PartitionSpec as P
+from jax.sharding import Mesh, PartitionSpec as P
 from jax.experimental import pallas as pl
 from jax.experimental.pallas import tpu as pltpu
 
@@ -51,9 +51,12 @@
 
 def shards(df_panels, occ_energy, virt_energy, fock_off, i_plan, pair_owner, pair_weight):
     highest = lax.Precision.HIGHEST
-    group_count = lax.axis_size("grp")
+    halves = lax.axis_size("zh")
+    cores = lax.axis_size("core")
+    group_count = halves * cores
     orbit_count = lax.axis_size("orb")
-    my_group = lax.axis_index("grp")
+    my_core = lax.axis_index("core")
+    my_group = lax.axis_index("zh") * cores + my_core
     my_index = lax.axis_index("orb")
     my_orbital = my_group * orbit_count + my_index
     own_panel = df_panels[0]
@@ -62,18 +65,23 @@
     groups_range = jnp.arange(group_count, dtype=jnp.int32)
     i_ids = (groups_range[None, :] * orbit_count + i_plan).reshape(tile_count)
     own_turned = own_panel.T
+    core_ids = lax.dynamic_index_in_dim(
+        i_ids.reshape(STEPS, halves, cores), my_core, axis=2, keepdims=False
+    ).reshape(-1)
     masked = jnp.where(
-        (i_ids == my_orbital)[:, None, None], own_turned[None], jnp.zeros((), own_panel.dtype)
+        (core_ids == my_orbital)[:, None, None], own_turned[None], jnp.zeros((), own_panel.dtype)
     )
-    broadcast = lax.psum(masked, ("grp", "orb"))
+    mine = lax.psum(masked, ("zh", "orb"))
+    theirs = lax.ppermute(mine, "core", [(c, c ^ 1) for c in range(cores)])
+    broadcast = jnp.concatenate([mine, theirs])
 
     meta = jnp.concatenate([pair_weight, pair_owner[:, 0].astype(jnp.float32)])
-    across = [(g, g ^ 2) for g in range(group_count)]
-    beside = [(g, g ^ 1) for g in range(group_count)]
-    far_panel = lax.ppermute(own_panel, "grp", across)
-    far_meta = lax.ppermute(meta, "grp", across)
-    near = lax.ppermute(jnp.stack([own_panel, far_panel]), "grp", beside)
-    near_meta = lax.ppermute(jnp.stack([meta, far_meta]), "grp", beside)
+    across = [(z, z ^ 1) for z in range(halves)]
+    beside = [(c, c ^ 1) for c in range(cores)]
+    far_panel = lax.ppermute(own_panel, "zh", across)
+    far_meta = lax.ppermute(meta, "zh", across)
+    near = lax.ppermute(jnp.stack([own_panel, far_panel]), "core", beside)
+    near_meta = lax.ppermute(jnp.stack([meta, far_meta]), "core", beside)
     column = jnp.stack([own_panel, far_panel, near[0], near[1]])
     column_meta = jnp.stack([meta, far_meta, near_meta[0], near_meta[1]])
     source_groups = jnp.stack([my_group, my_group ^ 2, my_group ^ 1, my_group ^ 3])
@@ -97,7 +105,13 @@
             slot_weight.reshape(-1),
         ]
     )
-    summed = summed_tiles(slot_tile.reshape(-1), scalars, broadcast, column, pair_sum)
+    step_of, group_of = slot_tile // group_count, slot_tile % group_count
+    position = (
+        jnp.where(group_of % cores == my_core, 0, tile_count // cores)
+        + step_of * halves
+        + group_of // cores
+    )
+    summed = summed_tiles(position.reshape(-1), scalars, broadcast, column, pair_sum)
 
     fock_matrix = jnp.diag(virt_energy) + 0.5 * (fock_off + fock_off.T)
     left = jnp.dot(fock_matrix, summed, precision=highest)
@@ -106,15 +120,18 @@
 
 
 def solution(mesh):
+    group_count, orbit_count = mesh.devices.shape
+    split = Mesh(mesh.devices.reshape(2, group_count // 2, orbit_count), ("zh", "core", "orb"))
+    spread = ("zh", "core", "orb")
     placed = (
-        P(("grp", "orb"), None, None),
+        P(spread, None, None),
         P(),
         P(),
         P(),
         P(),
-        P(("grp", "orb"), None),
-        P(("grp", "orb")),
+        P(spread, None),
+        P(spread),
     )
     return jax.shard_map(
-        shards, mesh=mesh, in_specs=placed, out_specs=P(("grp", "orb"), None, None), check_vma=False
+        shards, mesh=split, in_specs=placed, out_specs=P(spread, None, None), check_vma=False
     )

time: 234 us -> 248 us (1.060)
  waiting for transfers between devices: 166 us -> 175 us
  other arithmetic: 13.9 us -> 22.7 us
    psum x1, waiting for transfers between devices: 135 us -> 151 us  [shards(): mine = lax.psum(masked, ('zh', 'orb'))]
    concatenate x0 -> x1, other arithmetic: none -> 10.6 us  [shards(): broadcast = jnp.concatenate([mine, theirs])]
    ppermute x4 -> x5, waiting for transfers between devices: 31.5 us -> 23.9 us  [the longest x1 23 us: shards(): far_panel = lax.ppermute(own_panel, 'zh', across)]
    ppermute x4 -> x5, starting transfers between devices: 7.21 us -> 5.41 us  [the longest x1 2.41 us: shards(): far_panel = lax.ppermute(own_panel, 'zh', across)]
  transfers between devices with their start and end apart: 5 -> 6, of which waited for: 3 -> 3; matrix products, arithmetic and copies ran while one was open for 5% -> 4% of each run, Pallas kernels for 0% -> 0%
where the time goes in v4:
time: 248 us
  waiting for transfers between devices  175 us (71%)
  other arithmetic  22.7 us (9%)
  Pallas kernels  20.6 us (8%)
  between operations  13.5 us (5%)
  matrix products  6.22 us (3%)
  starting transfers between devices  5.41 us (2%)
  local copies, waits for them, and re-layouts  4.61 us (2%)
    psum x1, waiting for transfers between devices, shards(): mine = lax.psum(masked, ('zh', 'orb'))  151 us
    ppermute x1, waiting for transfers between devices, shards(): far_panel = lax.ppermute(own_panel, 'zh', across)  23 us
    pallas_call x1, Pallas kernels, summed_tiles(): pl.pallas_call(slot_kernel, grid_spec=grid_spec, out_shape=jax.ShapeDtype...  20.6 us
    concatenate x1, other arithmetic, shards(): broadcast = jnp.concatenate([mine, theirs])  10.6 us
  transfers between devices with their start and end apart: 6, of which 3 were waited for; matrix products, arithmetic and copies ran while one was open for 4% of the time, Pallas kernels for 0%

profile of v4, /device:TPU:1, one launch (start us, length us, event | category | flops | bytes accessed | tf_op | source)
XLA Modules:
  0.0 247.7 jit_solution(10531030559197876255)
XLA Ops:
  6.5 0.0 copy-start
  6.5 0.0 all-reduce.2.cloned.1.call-start
  6.5 0.7 broadcast_add_fusion.1
  7.2 0.1 copy.21
  7.3 0.1 copy.23
  7.5 0.1 eq.56
  7.5 1.5 copy.24
  9.0 3.1 %broadcast_select_fusion = bf16[6,512,1024]{2,1,0:T(8,128)(2,1)} fusion(pred[6]{0:T(512)(128)(4,1)S(1)} %eq.56, bf16[512,1024]{1,0:T(8,128)(2,1)S(1)} %copy.24), kind=kLoop, calls=%fused_computation.4 | loop fusion | flops 3145728 | bytes 7340038 | tf_op jit(solution)/shard_map/jit(_where)/select_n | solution.py:71
  12.2 0.0 copy-start.3
  12.2 0.0 copy-start.6
  12.2 0.0 copy-start.7
  12.2 0.0 copy-start.5
  12.2 0.0 all-reduce.2.cloned.1.call-update
  12.2 0.0 copy-start.2
  12.2 150.8 %all-reduce.2.cloned.1.call-done = bf16[6,512,1024]{2,1,0:T(8,128)(2,1)} async-done(((bf16[6,512,1024]{2,1,0:T(8,128)(2,1)}), bf16[6,512,1024]{2,1,0:T(8,128)(2,1)}) %all-reduce.2.cloned.1.call-update) | async-done | bytes 6291472 | tf_op jit(solution)/shard_map/psum | solution.py:74
  163.0 1.5 collective-permute-start.2
  164.5 0.0 copy-done.3
  164.5 2.4 collective-permute-start.3
  166.9 0.0 copy-done.6
  166.9 0.0 copy-done.7
  166.9 0.1 pad_maximum_fusion.5
  167.0 0.6 collective-permute-start
  167.5 0.1 reshape.153
  167.6 0.1 fusion.7
  167.7 23.0 %collective-permute-done.3 = bf16[1024,512]{1,0:T(8,128)(2,1)S(1)} collective-permute-done((bf16[1024,512]{1,0:T(8,128)(2,1)S(1)}, bf16[1024,512]{1,0:T(8,128)(2,1)S(1)}, u32[]{:S(2)}, u32[]{:S(2)}) %collective-permute-start.3) | collective-permute-done | bytes 1048608 | tf_op jit(solution)/shard_map/ppermute | solution.py:81
  190.7 0.0 copy-start.4
  190.7 1.6 pad_maximum_fusion.2
  192.3 0.9 collective-permute-start.4
  193.2 0.0 copy-done
  193.2 0.6 gather_fusion.2
  193.8 0.1 fusion.15
  193.9 0.0 copy-done.5
  193.9 1.2 broadcast_add_fusion.pair_ref
  195.1 0.1 broadcast_in_dim.87
  195.1 0.1 reshape.155
  195.2 0.0 collective-permute-done
  195.2 0.1 collective-permute-start.1
  195.3 0.0 copy-done.4
  195.3 0.7 gather_fusion
  196.0 0.0 copy-done.2
  196.0 0.3 copy.20
  196.4 0.9 collective-permute-done.1
  197.3 0.1 fusion.12
  197.4 0.2 reduce_window_sum.11
  197.6 0.1 select_reduce_fusion.1
  197.7 0.1 reduce_sum.23
  197.8 0.1 select_reduce_fusion
  197.9 0.1 reshape.156
  198.0 0.1 reshape.167
  198.1 0.7 gather_fusion.1
  198.8 0.7 pad_maximum_fusion.6.scalars_ref
  199.4 0.6 fusion.5.tiles_ref
  200.0 0.0 collective-permute-done.4
  200.0 3.5 %pad_maximum_fusion.1.right_ref = bf16[4,1024,512]{2,1,0:T(8,128)(2,1)} fusion(bf16[2,1024,512]{2,1,0:T(8,128)(2,1)} %collective-permute-done.4, bf16[1,1024,512]{2,1,0:T(8,128)(2,1)} %bitcast.41, bf16[1,1024,512]{2,1,0:T(8,128)(2,1)S(1)} %copy-done.3), kind=kLoop, calls=%fused_computation.5 | loop fusion | flops 4194304 | bytes 8388608 | tf_op jit(solution)/shard_map/stack | solution.py:85
  203.5 0.0 collective-permute-done.2
  203.5 10.6 %pad_maximum_fusion.left_ref = bf16[12,512,1024]{2,1,0:T(8,128)(2,1)} fusion(bf16[6,512,1024]{2,1,0:T(8,128)(2,1)} %collective-permute-done.2, bf16[6,512,1024]{2,1,0:T(8,128)(2,1)} %all-reduce.2.cloned.1.call-done), kind=kLoop, calls=%fused_computation.3 | loop fusion | flops 6291456 | bytes 25165824 | tf_op jit(solution)/shard_map/concatenate | solution.py:76
  214.1 20.6 %shard_map.73 = f32[512,512]{1,0:T(8,128)} custom-call(s32[16]{0:T(128)} %fusion.5.tiles_ref, f32[48]{0:T(128)} %pad_maximum_fusion.6.scalars_ref, bf16[12,512,1024]{2,1,0:T(8,128)(2,1)} %pad_maximum_fusion.left_ref, bf16[4,1024,512]{2,1,0:T(8,128)(2,1)} %pad_maximum_fusion.1.right_ref, f32[512,512]{1,0:T(8,128)} %broadcast_add_fusion.pair_ref), custom_call_target="tpu_custom_call" | custom-call | tf_op jit(solution)/shard_map/pallas_call | solution.py:44
  234.7 0.0 copy-start.1
  234.7 3.3 %fusion.9 = f32[512,512]{1,0:T(8,128)S(1)} fusion(f32[512,512]{1,0:T(8,128)} %shard_map.73, f32[512,512]{1,0:T(8,128)S(1)} %copy-done.2, f32[512,512]{0,1:T(8,128)S(1)} %copy.20, f32[512]{0:T(512)S(1)} %copy-done.5), kind=kOutput, calls=%fused_computation.52 | convolution fusion | flops 1611923456 | bytes 4196352 | tf_op jit(solution)/shard_map/dot_general | solution.py:118
  238.0 0.0 copy-done.1
  238.0 2.9 %fusion = f32[1,512,512]{2,1,0:T(8,128)} fusion(f32[512,512]{1,0:T(8,128)S(1)} %fusion.9, f32[512,512]{1,0:T(8,128)S(1)} %copy-done.1, f32[512,512]{1,0:T(8,128)S(1)} %copy-done.2, f32[512,512]{0,1:T(8,128)S(1)} %copy.20, f32[512]{0:T(512)S(1)} %copy-done.5), kind=kOutput, calls=%fused_computation.8 | convolution fusion | flops 1612185600 | bytes 5244928 | tf_op jit(solution)/shard_map/dot_general | solution.py:117
  (12 shorter events, 0.1 us)
Async XLA Ops:
  6.5 186.6 %copy-start = (f32[128]{0:T(128)S(1)}, f32[128]{0:T(128)}, u32[]{:S(2)}) copy-start(f32[128]{0:T(128)} %param.8) | copy-start | bytes 1540
  6.5 156.5 %all-reduce.2.cloned.1.call-start = ((), (), s32[]{:S(2)}) async-start(), calls=%async_computation | async-start | bytes 12582912 | tf_op jit(solution)/shard_map/psum | solution.py:74
  12.2 152.3 %copy-start.3 = (bf16[1,1024,512]{2,1,0:T(8,128)(2,1)S(1)}, bf16[1,1024,512]{2,1,0:T(8,128)(2,1)}, u32[]{:S(2)}) copy-start(bf16[1,1024,512]{2,1,0:T(8,128)(2,1)} %param.7) | copy-start | bytes 3145732
  12.2 154.7 %copy-start.6 = (s32[12,1]{0,1:T(1,128)S(1)}, s32[12,1]{0,1:T(1,128)}, u32[]{:S(2)}) copy-start(s32[12,1]{0,1:T(1,128)} %param.12) | copy-start | bytes 148
  12.2 154.7 %copy-start.7 = (f32[12]{0:T(128)S(1)}, f32[12]{0:T(128)}, u32[]{:S(2)}) copy-start(f32[12]{0:T(128)} %param.13) | copy-start | bytes 148
  12.2 181.7 %copy-start.5 = (f32[512]{0:T(512)S(1)}, f32[512]{0:T(512)}, u32[]{:S(2)}) copy-start(f32[512]{0:T(512)} %param.9) | copy-start | bytes 6148
  12.2 183.8 %copy-start.2 = (f32[512,512]{1,0:T(8,128)S(1)}, f32[512,512]{1,0:T(8,128)}, u32[]{:S(2)}) copy-start(f32[512,512]{1,0:T(8,128)} %param.10) | copy-start | bytes 3145732
  163.0 40.5 %collective-permute-start.2 = (bf16[6,512,1024]{2,1,0:T(8,128)(2,1)}, bf16[6,512,1024]{2,1,0:T(8,128)(2,1)}, u32[]{:S(2)}, u32[]{:S(2)}) collective-permute-start(bf16[6,512,1024]{2,1,0:T(8,128)(2,1)} %all-reduce.2.cloned.1.call-done), channel_id=1, source_target_pairs={{0,32},{32,0},{1,33},{33,1},{2,34},{34,2},{3,35},{35,3},{4,36},{36... | collective-permute-start | bytes 18874376 | tf_op jit(solution)/shard_map/ppermute | solution.py:75
  164.5 26.2 %collective-permute-start.3 = (bf16[1024,512]{1,0:T(8,128)(2,1)S(1)}, bf16[1024,512]{1,0:T(8,128)(2,1)S(1)}, u32[]{:S(2)}, u32[]{:S(2)}) collective-permute-start(bf16[1024,512]{1,0:T(8,128)(2,1)S(1)} %bitcast.39), channel_id=1, source_target_pairs={{0,64},{64,0},{1,65},{65,1},{2,66},{66,2},{3,67},{67,3},{4,68},{68... | collective-permute-start | bytes 3145736 | tf_op jit(solution)/shard_map/ppermute | solution.py:81
  167.0 28.3 %collective-permute-start = (f32[24]{0:T(128)S(1)}, f32[24]{0:T(128)S(1)}, u32[]{:S(2)}, u32[]{:S(2)}) collective-permute-start(f32[24]{0:T(128)S(1)} %pad_maximum_fusion.5), channel_id=1, source_target_pairs={{0,64},{64,0},{1,65},{65,1},{2,66},{66,2},{3,67},{67,3},{4,68},{68... | collective-permute-start | bytes 296 | tf_op jit(solution)/shard_map/ppermute | solution.py:82
  190.7 4.7 %copy-start.4 = (bf16[1024,512]{1,0:T(8,128)(2,1)}, bf16[1024,512]{1,0:T(8,128)(2,1)S(1)}, u32[]{:S(2)}) copy-start(bf16[1024,512]{1,0:T(8,128)(2,1)S(1)} %collective-permute-done.3) | copy-start | bytes 3145732
  192.3 7.7 %collective-permute-start.4 = (bf16[2,1024,512]{2,1,0:T(8,128)(2,1)}, bf16[2,1024,512]{2,1,0:T(8,128)(2,1)}, u32[]{:S(2)}, u32[]{:S(2)}) collective-permute-start(bf16[2,1024,512]{2,1,0:T(8,128)(2,1)} %pad_maximum_fusion.2), channel_id=1, source_target_pairs={{0,32},{32,0},{1,33},{33,1},{2,34},{34,2},{3,35},{35,3},{4,36},{36... | collective-permute-start | bytes 6291464 | tf_op jit(solution)/shard_map/ppermute | solution.py:83
  195.2 2.1 collective-permute-start.1
  234.7 3.3 %copy-start.1 = (f32[512,512]{1,0:T(8,128)S(1)}, f32[512,512]{1,0:T(8,128)}, u32[]{:S(2)}) copy-start(f32[512,512]{1,0:T(8,128)} %shard_map.73) | copy-start | bytes 3145732
Sparse Core Ops, SparseCore 0:
  12.3 150.6 all-reduce.1

commit v5 on v4

--- a/solution.py
+++ b/solution.py
@@ -5,37 +5,63 @@
 from jax.experimental import pallas as pl
 from jax.experimental.pallas import tpu as pltpu
 
-NVIR = 512
 STEPS = 3
 CAP = 4
 
 
-def slot_kernel(tiles_ref, scalars_ref, left_ref, right_ref, pair_ref, out_ref):
+def slot_kernel(tiles_ref, scalars_ref, mine_ref, theirs_ref, right_ref, pair_ref, out_ref):
     step = pl.program_id(0)
     slots = pl.num_programs(0)
-    integral = jnp.dot(left_ref[...], right_ref[...], preferred_element_type=jnp.float32)
-    denominator = (pair_ref[...] - scalars_ref[step]) - scalars_ref[slots + step]
-    amplitude = ((integral / denominator) * scalars_ref[2 * slots + step]).astype(jnp.bfloat16)
 
-    @pl.when(step == 0)
+    def accumulate(left_ref):
+        integral = jnp.dot(left_ref[...], right_ref[...], preferred_element_type=jnp.float32)
+        denominator = (pair_ref[...] - scalars_ref[step]) - scalars_ref[slots + step]
+        amplitude = ((integral / denominator) * scalars_ref[2 * slots + step]).astype(jnp.bfloat16)
+
+        @pl.when(step == 0)
+        def _():
+            out_ref[...] = amplitude.astype(jnp.float32)
+
+        @pl.when(step > 0)
+        def _():
+            out_ref[...] += amplitude.astype(jnp.float32)
+
+    @pl.when(tiles_ref[step] == 0)
     def _():
-        out_ref[...] = amplitude.astype(jnp.float32)
+        accumulate(mine_ref)
 
-    @pl.when(step > 0)
+    @pl.when(tiles_ref[step] != 0)
     def _():
-        out_ref[...] += amplitude.astype(jnp.float32)
+        accumulate(theirs_ref)
 
 
-def summed_tiles(slot_tile, scalars, broadcast, column, pair_sum):
-    slots = slot_tile.shape[0]
+def held_index(present, local):
+    steps = jnp.arange(present.shape[0], dtype=jnp.int32)
+    last = lax.cummax(jnp.where(present, steps, -1))
+    first = jnp.argmax(present)
+    return jnp.where(last >= 0, local[jnp.maximum(last, 0)], local[first])
+
+
+def summed_tiles(position, scalars, mine, theirs, column, pair_sum):
+    slots = position.shape[0]
     per_source = slots // column.shape[0]
-    _, rows, depth = broadcast.shape
+    half, rows, depth = mine.shape
+    in_theirs = position >= half
+    local = position % half
+    tables = jnp.concatenate(
+        [
+            in_theirs.astype(jnp.int32),
+            held_index(~in_theirs, local),
+            held_index(in_theirs, local),
+        ]
+    )
     grid_spec = pltpu.PrefetchScalarGridSpec(
         num_scalar_prefetch=1,
         grid=(slots,),
         in_specs=[
             pl.BlockSpec(memory_space=pltpu.SMEM),
-            pl.BlockSpec((None, rows, depth), lambda s, tiles: (tiles[s], 0, 0)),
+            pl.BlockSpec((None, rows, depth), lambda s, tiles: (tiles[slots + s], 0, 0)),
+            pl.BlockSpec((None, rows, depth), lambda s, tiles: (tiles[2 * slots + s], 0, 0)),
             pl.BlockSpec((None, depth, rows), lambda s, tiles: (s // per_source, 0, 0)),
             pl.BlockSpec((rows, rows), lambda s, tiles: (0, 0)),
         ],
@@ -46,10 +72,10 @@
         grid_spec=grid_spec,
         out_shape=jax.ShapeDtypeStruct((rows, rows), jnp.float32),
         compiler_params=pltpu.CompilerParams(dimension_semantics=("arbitrary",)),
-    )(slot_tile, scalars, broadcast, column, pair_sum)
+    )(tables, scalars, mine, theirs, column, pair_sum)
 
 
-def shards(df_panels, occ_energy, virt_energy, fock_off, i_plan, pair_owner, pair_weight):
+def layer(df_panels, occ_energy, virt_energy, fock_off, i_plan, pair_owner, pair_weight):
     highest = lax.Precision.HIGHEST
     halves = lax.axis_size("zh")
     cores = lax.axis_size("core")
@@ -71,9 +97,8 @@
     masked = jnp.where(
         (core_ids == my_orbital)[:, None, None], own_turned[None], jnp.zeros((), own_panel.dtype)
     )
-    mine = lax.psum(masked, ("zh", "orb"))
-    theirs = lax.ppermute(mine, "core", [(c, c ^ 1) for c in range(cores)])
-    broadcast = jnp.concatenate([mine, theirs])
+    own_half = lax.psum(masked, ("zh", "orb"))
+    other_half = lax.ppermute(own_half, "core", [(c, c ^ 1) for c in range(cores)])
 
     meta = jnp.concatenate([pair_weight, pair_owner[:, 0].astype(jnp.float32)])
     across = [(z, z ^ 1) for z in range(halves)]
@@ -111,7 +136,7 @@
         + step_of * halves
         + group_of // cores
     )
-    summed = summed_tiles(position.reshape(-1), scalars, broadcast, column, pair_sum)
+    summed = summed_tiles(position.reshape(-1), scalars, own_half, other_half, column, pair_sum)
 
     fock_matrix = jnp.diag(virt_energy) + 0.5 * (fock_off + fock_off.T)
     left = jnp.dot(fock_matrix, summed, precision=highest)
@@ -133,5 +158,5 @@
         P(spread),
     )
     return jax.shard_map(
-        shards, mesh=split, in_specs=placed, out_specs=P(spread, None, None), check_vma=False
+        layer, mesh=split, in_specs=placed, out_specs=P(spread, None, None), check_vma=False
     )

time: 248 us -> 241 us (0.972)
  waiting for transfers between devices: 175 us -> 168 us
  other arithmetic: 22.7 us -> 16.6 us
  between operations: 13.5 us -> 17.5 us
    concatenate x3, other arithmetic: 11.4 us -> 1.23 us  [the longest x1 0.59 us: layer(): jnp.concatenate([i_energy.reshape(-1), jnp.repeat(j_energy, CAP), slot_we...]
    ppermute x5, waiting for transfers between devices: 23.9 us -> 16.7 us  [the longest x1 13.5 us: layer(): far_panel = lax.ppermute(own_panel, 'zh', across)]
    another operation x6 -> x10, other arithmetic: 5.4 us -> 8.1 us  [the longest x1 3.52 us: layer(): column = jnp.stack([own_panel, far_panel, near[0], near[1]])]
  transfers between devices with their start and end apart: 6 -> 6, of which waited for: 3 -> 3; matrix products, arithmetic and copies ran while one was open for 4% -> 7% of each run, Pallas kernels for 0% -> 0%
where the time goes in v5:
time: 241 us; the launch traced here: 240 us
  waiting for transfers between devices  168 us (70%)
  Pallas kernels  19.4 us (8%)
  between operations  17.5 us (7%)
  other arithmetic  16.6 us (7%)
  local copies, waits for them, and re-layouts  6.67 us (3%)
  starting transfers between devices  6.23 us (3%)
  matrix products  6.22 us (3%)
    psum x1, waiting for transfers between devices, layer(): own_half = lax.psum(masked, ('zh', 'orb'))  151 us
    pallas_call x1, Pallas kernels, summed_tiles(): pl.pallas_call(slot_kernel, grid_spec=grid_spec, out_shape=jax.ShapeDtype...  19.4 us
    ppermute x1, waiting for transfers between devices, layer(): far_panel = lax.ppermute(own_panel, 'zh', across)  13.5 us
  transfers between devices with their start and end apart: 6, of which 3 were waited for; matrix products, arithmetic and copies ran while one was open for 7% of the time, Pallas kernels for 0%

profile of v5, /device:TPU:1, one launch (start us, length us, event | category | flops | bytes accessed | tf_op | source)
XLA Modules:
  0.0 240.2 jit_solution(14961330984205647762)
XLA Ops:
  6.5 0.0 copy-start
  6.5 0.0 all-reduce.2.cloned.1.call-start
  6.5 0.7 broadcast_add_fusion.1
  7.2 0.1 copy.37
  7.3 0.1 copy.39
  7.5 0.1 eq.78
  7.5 1.5 copy.40
  9.0 3.1 %broadcast_select_fusion = bf16[6,512,1024]{2,1,0:T(8,128)(2,1)} fusion(pred[6]{0:T(512)(128)(4,1)S(1)} %eq.78, bf16[512,1024]{1,0:T(8,128)(2,1)S(1)} %copy.40), kind=kLoop, calls=%fused_computation.5 | loop fusion | flops 3145728 | bytes 7340038 | tf_op jit(solution)/shard_map/jit(_where)/select_n | solution.py:97
  12.2 0.0 copy-start.2
  12.2 0.0 all-reduce.2.cloned.1.call-update
  12.2 150.8 %all-reduce.2.cloned.1.call-done.mine_ref = bf16[6,512,1024]{2,1,0:T(8,128)(2,1)} async-done(((bf16[6,512,1024]{2,1,0:T(8,128)(2,1)}), bf16[6,512,1024]{2,1,0:T(8,128)(2,1)}) %all-reduce.2.cloned.1.call-update) | async-done | bytes 6291472 | tf_op jit(solution)/shard_map/psum | solution.py:100
  163.0 1.4 collective-permute-start.2
  164.5 0.0 copy-done.5
  164.5 0.0 copy-done.6
  164.5 0.1 pad_maximum_fusion.4
  164.5 2.4 %collective-permute-start = (f32[24]{0:T(128)S(1)}, f32[24]{0:T(128)S(1)}, u32[]{:S(2)}, u32[]{:S(2)}) collective-permute-start(f32[24]{0:T(128)S(1)} %pad_maximum_fusion.4), channel_id=1, source_target_pairs={{0,64},{64,0},{1,65},{65,1},{2,66},{66,2},{3,67},{67,3},{4,68},{68... | collective-permute-start | bytes 296 | tf_op jit(solution)/shard_map/ppermute | solution.py:107
  167.0 0.0 copy-done.3
  167.0 0.6 collective-permute-start.3
  167.5 0.1 reshape.380
  167.6 0.0 copy-done
  167.6 0.7 gather_fusion.2
  168.3 0.1 fusion.28
  168.4 0.1 fusion.16
  168.5 0.0 copy-done.4
  168.5 1.1 broadcast_add_fusion.pair_ref
  169.6 0.6 gather_fusion.4
  170.2 0.0 collective-permute-done
  170.2 0.6 collective-permute-start.1
  170.9 0.1 broadcast_in_dim.104
  171.0 0.1 reshape.382
  171.0 0.0 copy-done.2
  171.1 0.3 copy.32
  171.4 3.2 %collective-permute-done.1 = f32[2,24]{1,0:T(2,128)S(1)} collective-permute-done((f32[2,24]{1,0:T(2,128)S(1)}, f32[2,24]{1,0:T(2,128)S(1)}, u32[]{:S(2)}, u32[]{:S(2)}) %collective-permute-start.1) | collective-permute-done | bytes 224 | tf_op jit(solution)/shard_map/ppermute | solution.py:109
  174.6 0.1 fusion.24
  174.7 0.2 reduce_window_sum.11
  174.9 0.1 select_reduce_fusion.1
  175.0 0.1 reduce_sum.25
  175.1 0.7 iota_reduce_fusion
  177.1 0.7 not_reduce_fusion
  179.3 0.1 reduce_sum.29
  179.3 0.1 select_reduce_fusion
  179.4 0.1 reshape.383
  179.5 13.5 %collective-permute-done.3 = bf16[1024,512]{1,0:T(8,128)(2,1)} collective-permute-done((bf16[1024,512]{1,0:T(8,128)(2,1)S(1)}, bf16[1024,512]{1,0:T(8,128)(2,1)}, u32[]{:S(2)}, u32[]{:S(2)}) %collective-permute-start.3) | collective-permute-done | bytes 1048608 | tf_op jit(solution)/shard_map/ppermute | solution.py:106
  193.0 2.8 %pad_maximum_fusion.1 = bf16[2,1024,512]{2,1,0:T(8,128)(2,1)} fusion(bf16[1,1024,512]{2,1,0:T(8,128)(2,1)} %bitcast.16, bf16[1,1024,512]{2,1,0:T(8,128)(2,1)S(1)} %copy-done.3), kind=kLoop, calls=%fused_computation.7 | loop fusion | flops 1048576 | bytes 4194304 | tf_op jit(solution)/shard_map/stack | solution.py:108
  195.8 1.1 collective-permute-start.4
  197.0 0.1 reshape.410
  197.1 0.1 maximum_reduce_fusion.1
  197.3 0.7 gather_fusion
  197.9 0.1 maximum_reduce_fusion
  198.1 0.7 gather_fusion.1
  200.1 0.7 gather_fusion.3
  200.7 0.7 fusion.25
  201.4 0.6 pad_maximum_fusion.5.scalars_ref
  202.0 0.1 compare_reduce_fusion.1
  202.1 0.1 compare_reduce_fusion
  202.3 1.3 broadcast_select_fusion.1
  203.6 0.6 pad_add_fusion.tiles_ref
  204.2 0.0 collective-permute-done.4
  204.2 3.5 %pad_maximum_fusion.right_ref = bf16[4,1024,512]{2,1,0:T(8,128)(2,1)} fusion(bf16[2,1024,512]{2,1,0:T(8,128)(2,1)} %collective-permute-done.4, bf16[1,1024,512]{2,1,0:T(8,128)(2,1)} %bitcast.16, bf16[1,1024,512]{2,1,0:T(8,128)(2,1)S(1)} %copy-done.3), kind=kLoop, calls=%fused_computation.6 | loop fusion | flops 4194304 | bytes 8388608 | tf_op jit(solution)/shard_map/stack | solution.py:110
  207.7 0.0 collective-permute-done.2.theirs_ref
  207.7 19.4 %shard_map.73 = f32[512,512]{1,0:T(8,128)} custom-call(s32[48]{0:T(128)} %pad_add_fusion.tiles_ref, f32[48]{0:T(128)} %pad_maximum_fusion.5.scalars_ref, bf16[6,512,1024]{2,1,0:T(8,128)(2,1)} %all-reduce.2.cloned.1.call-done.mine_ref, bf16[6,512,1024]{2,1,0:T(8,128)(2,1)} %collective-permute-done.2.theirs_ref, ...), custom_call_target="tpu_custom_call" | custom-call | tf_op jit(solution)/shard_map/pallas_call | solution.py:70
  227.1 3.3 %fusion.19 = f32[512,512]{1,0:T(8,128)S(1)} fusion(f32[512,512]{1,0:T(8,128)} %shard_map.73, f32[512,512]{1,0:T(8,128)S(1)} %copy-done.2, f32[512,512]{0,1:T(8,128)S(1)} %copy.32, f32[512]{0:T(512)S(1)} %copy-done.4), kind=kOutput, calls=%fused_computation.90 | convolution fusion | flops 1611923456 | bytes 4196352 | tf_op jit(solution)/shard_map/dot_general | solution.py:143
  230.4 0.0 copy-done.1
  230.4 2.9 %fusion = f32[1,512,512]{2,1,0:T(8,128)} fusion(f32[512,512]{1,0:T(8,128)S(1)} %fusion.19, f32[512,512]{1,0:T(8,128)S(1)} %copy-done.1, f32[512,512]{1,0:T(8,128)S(1)} %copy-done.2, f32[512,512]{0,1:T(8,128)S(1)} %copy.32, f32[512]{0:T(512)S(1)} %copy-done.4), kind=kOutput, calls=%fused_computation.9 | convolution fusion | flops 1612185600 | bytes 5244928 | tf_op jit(solution)/shard_map/dot_general | solution.py:142
  (25 shorter events, 0.2 us)
Async XLA Ops:
  6.5 161.1 %copy-start = (f32[128]{0:T(128)S(1)}, f32[128]{0:T(128)}, u32[]{:S(2)}) copy-start(f32[128]{0:T(128)} %param.8) | copy-start | bytes 1540
  6.5 156.5 %all-reduce.2.cloned.1.call-start = ((), (), s32[]{:S(2)}) async-start(), calls=%async_computation | async-start | bytes 12582912 | tf_op jit(solution)/shard_map/psum | solution.py:100
  12.2 152.3 %copy-start.5 = (s32[12,1]{0,1:T(1,128)S(1)}, s32[12,1]{0,1:T(1,128)}, u32[]{:S(2)}) copy-start(s32[12,1]{0,1:T(1,128)} %param.12) | copy-start | bytes 148
  12.2 152.3 %copy-start.6 = (f32[12]{0:T(128)S(1)}, f32[12]{0:T(128)}, u32[]{:S(2)}) copy-start(f32[12]{0:T(128)} %param.13) | copy-start | bytes 148
  12.2 154.8 %copy-start.3 = (bf16[1,1024,512]{2,1,0:T(8,128)(2,1)S(1)}, bf16[1,1024,512]{2,1,0:T(8,128)(2,1)}, u32[]{:S(2)}) copy-start(bf16[1,1024,512]{2,1,0:T(8,128)(2,1)} %param.7) | copy-start | bytes 3145732
  12.2 156.3 %copy-start.4 = (f32[512]{0:T(512)S(1)}, f32[512]{0:T(512)}, u32[]{:S(2)}) copy-start(f32[512]{0:T(512)} %param.9) | copy-start | bytes 6148
  12.2 158.9 %copy-start.2 = (f32[512,512]{1,0:T(8,128)S(1)}, f32[512,512]{1,0:T(8,128)}, u32[]{:S(2)}) copy-start(f32[512,512]{1,0:T(8,128)} %param.10) | copy-start | bytes 3145732
  163.0 44.7 %collective-permute-start.2 = (bf16[6,512,1024]{2,1,0:T(8,128)(2,1)}, bf16[6,512,1024]{2,1,0:T(8,128)(2,1)}, u32[]{:S(2)}, u32[]{:S(2)}) collective-permute-start(bf16[6,512,1024]{2,1,0:T(8,128)(2,1)} %all-reduce.2.cloned.1.call-done.mine_ref), channel_id=1, source_target_pairs={{0,32},{32,0},{1,33},{33,1},{2,34},{34,2},{3,35},{35,3},{4,36},{36... | collective-permute-start | bytes 18874376 | tf_op jit(solution)/shard_map/ppermute | solution.py:101
  164.5 5.7 %collective-permute-start = (f32[24]{0:T(128)S(1)}, f32[24]{0:T(128)S(1)}, u32[]{:S(2)}, u32[]{:S(2)}) collective-permute-start(f32[24]{0:T(128)S(1)} %pad_maximum_fusion.4), channel_id=1, source_target_pairs={{0,64},{64,0},{1,65},{65,1},{2,66},{66,2},{3,67},{67,3},{4,68},{68... | collective-permute-start | bytes 296 | tf_op jit(solution)/shard_map/ppermute | solution.py:107
  167.0 26.0 %collective-permute-start.3 = (bf16[1024,512]{1,0:T(8,128)(2,1)S(1)}, bf16[1024,512]{1,0:T(8,128)(2,1)}, u32[]{:S(2)}, u32[]{:S(2)}) collective-permute-start(bf16[1024,512]{1,0:T(8,128)(2,1)S(1)} %bitcast.41), channel_id=1, source_target_pairs={{0,64},{64,0},{1,65},{65,1},{2,66},{66,2},{3,67},{67,3},{4,68},{68... | collective-permute-start | bytes 3145736 | tf_op jit(solution)/shard_map/ppermute | solution.py:106
  170.2 4.3 %collective-permute-start.1 = (f32[2,24]{1,0:T(2,128)S(1)}, f32[2,24]{1,0:T(2,128)S(1)}, u32[]{:S(2)}, u32[]{:S(2)}) collective-permute-start(f32[2,24]{1,0:T(2,128)S(1)} %pad_maximum_fusion.3), channel_id=1, source_target_pairs={{0,32},{32,0},{1,33},{33,1},{2,34},{34,2},{3,35},{35,3},{4,36},{36... | collective-permute-start | bytes 584 | tf_op jit(solution)/shard_map/ppermute | solution.py:109
  195.8 8.4 %collective-permute-start.4 = (bf16[2,1024,512]{2,1,0:T(8,128)(2,1)}, bf16[2,1024,512]{2,1,0:T(8,128)(2,1)}, u32[]{:S(2)}, u32[]{:S(2)}) collective-permute-start(bf16[2,1024,512]{2,1,0:T(8,128)(2,1)} %pad_maximum_fusion.1), channel_id=1, source_target_pairs={{0,32},{32,0},{1,33},{33,1},{2,34},{34,2},{3,35},{35,3},{4,36},{36... | collective-permute-start | bytes 6291464 | tf_op jit(solution)/shard_map/ppermute | solution.py:108
  227.1 3.3 %copy-start.1 = (f32[512,512]{1,0:T(8,128)S(1)}, f32[512,512]{1,0:T(8,128)}, u32[]{:S(2)}) copy-start(f32[512,512]{1,0:T(8,128)} %shard_map.73) | copy-start | bytes 3145732
Sparse Core Ops, SparseCore 0:
  12.3 150.6 all-reduce.1

commit v6 on v5

--- a/solution.py
+++ b/solution.py
@@ -49,11 +49,7 @@
     in_theirs = position >= half
     local = position % half
     tables = jnp.concatenate(
-        [
-            in_theirs.astype(jnp.int32),
-            held_index(~in_theirs, local),
-            held_index(in_theirs, local),
-        ]
+        [in_theirs.astype(jnp.int32), held_index(~in_theirs, local), held_index(in_theirs, local)]
     )
     grid_spec = pltpu.PrefetchScalarGridSpec(
         num_scalar_prefetch=1,

time: 241 us -> 241 us (level)
  no operation moved by 1% of the time
where the time goes in v6:
time: 241 us; the launch traced here: 240 us
  waiting for transfers between devices  168 us (70%)
  Pallas kernels  19.4 us (8%)
  between operations  17.5 us (7%)
  other arithmetic  16.6 us (7%)
  local copies, waits for them, and re-layouts  6.67 us (3%)
  starting transfers between devices  6.23 us (3%)
  matrix products  6.22 us (3%)
    psum x1, waiting for transfers between devices, layer(): own_half = lax.psum(masked, ('zh', 'orb'))  151 us
    pallas_call x1, Pallas kernels, summed_tiles(): pl.pallas_call(slot_kernel, grid_spec=grid_spec, out_shape=jax.ShapeDtype...  19.4 us
    ppermute x1, waiting for transfers between devices, layer(): far_panel = lax.ppermute(own_panel, 'zh', across)  13.5 us
  transfers between devices with their start and end apart: 6, of which 3 were waited for; matrix products, arithmetic and copies ran while one was open for 7% of the time, Pallas kernels for 0%

profile of v6, /device:TPU:1, one launch (start us, length us, event | category | flops | bytes accessed | tf_op | source)
XLA Modules:
  0.0 240.2 jit_solution(14961330984205647762)
XLA Ops:
  6.5 0.0 copy-start
  6.5 0.0 all-reduce.2.cloned.1.call-start
  6.5 0.7 broadcast_add_fusion.1
  7.2 0.1 copy.37
  7.3 0.1 copy.39
  7.5 0.1 eq.78
  7.5 1.5 copy.40
  9.0 3.1 %broadcast_select_fusion = bf16[6,512,1024]{2,1,0:T(8,128)(2,1)} fusion(pred[6]{0:T(512)(128)(4,1)S(1)} %eq.78, bf16[512,1024]{1,0:T(8,128)(2,1)S(1)} %copy.40), kind=kLoop, calls=%fused_computation.5 | loop fusion | flops 3145728 | bytes 7340038 | tf_op jit(solution)/shard_map/jit(_where)/select_n | solution.py:93
  12.2 0.0 copy-start.2
  12.2 0.0 all-reduce.2.cloned.1.call-update
  12.2 150.8 %all-reduce.2.cloned.1.call-done.mine_ref = bf16[6,512,1024]{2,1,0:T(8,128)(2,1)} async-done(((bf16[6,512,1024]{2,1,0:T(8,128)(2,1)}), bf16[6,512,1024]{2,1,0:T(8,128)(2,1)}) %all-reduce.2.cloned.1.call-update) | async-done | bytes 6291472 | tf_op jit(solution)/shard_map/psum | solution.py:96
  163.0 1.4 collective-permute-start.2
  164.5 0.0 copy-done.5
  164.5 0.0 copy-done.6
  164.5 0.1 pad_maximum_fusion.4
  164.5 2.4 %collective-permute-start = (f32[24]{0:T(128)S(1)}, f32[24]{0:T(128)S(1)}, u32[]{:S(2)}, u32[]{:S(2)}) collective-permute-start(f32[24]{0:T(128)S(1)} %pad_maximum_fusion.4), channel_id=1, source_target_pairs={{0,64},{64,0},{1,65},{65,1},{2,66},{66,2},{3,67},{67,3},{4,68},{68... | collective-permute-start | bytes 296 | tf_op jit(solution)/shard_map/ppermute | solution.py:103
  167.0 0.0 copy-done.3
  167.0 0.6 collective-permute-start.3
  167.5 0.1 reshape.380
  167.6 0.0 copy-done
  167.6 0.7 gather_fusion.2
  168.3 0.1 fusion.28
  168.4 0.1 fusion.16
  168.5 0.0 copy-done.4
  168.5 1.1 broadcast_add_fusion.pair_ref
  169.6 0.6 gather_fusion.4
  170.2 0.0 collective-permute-done
  170.2 0.6 collective-permute-start.1
  170.9 0.1 broadcast_in_dim.104
  171.0 0.1 reshape.382
  171.0 0.0 copy-done.2
  171.1 0.3 copy.32
  171.4 3.2 %collective-permute-done.1 = f32[2,24]{1,0:T(2,128)S(1)} collective-permute-done((f32[2,24]{1,0:T(2,128)S(1)}, f32[2,24]{1,0:T(2,128)S(1)}, u32[]{:S(2)}, u32[]{:S(2)}) %collective-permute-start.1) | collective-permute-done | bytes 224 | tf_op jit(solution)/shard_map/ppermute | solution.py:105
  174.6 0.1 fusion.24
  174.7 0.2 reduce_window_sum.11
  174.9 0.1 select_reduce_fusion.1
  175.0 0.1 reduce_sum.25
  175.1 0.7 iota_reduce_fusion
  177.1 0.7 not_reduce_fusion
  179.3 0.1 reduce_sum.29
  179.3 0.1 select_reduce_fusion
  179.4 0.1 reshape.383
  179.5 13.5 %collective-permute-done.3 = bf16[1024,512]{1,0:T(8,128)(2,1)} collective-permute-done((bf16[1024,512]{1,0:T(8,128)(2,1)S(1)}, bf16[1024,512]{1,0:T(8,128)(2,1)}, u32[]{:S(2)}, u32[]{:S(2)}) %collective-permute-start.3) | collective-permute-done | bytes 1048608 | tf_op jit(solution)/shard_map/ppermute | solution.py:102
  193.0 2.8 %pad_maximum_fusion.1 = bf16[2,1024,512]{2,1,0:T(8,128)(2,1)} fusion(bf16[1,1024,512]{2,1,0:T(8,128)(2,1)} %bitcast.16, bf16[1,1024,512]{2,1,0:T(8,128)(2,1)S(1)} %copy-done.3), kind=kLoop, calls=%fused_computation.7 | loop fusion | flops 1048576 | bytes 4194304 | tf_op jit(solution)/shard_map/stack | solution.py:104
  195.8 1.1 collective-permute-start.4
  197.0 0.1 reshape.410
  197.1 0.1 maximum_reduce_fusion.1
  197.3 0.7 gather_fusion
  197.9 0.1 maximum_reduce_fusion
  198.1 0.7 gather_fusion.1
  200.1 0.7 gather_fusion.3
  200.7 0.7 fusion.25
  201.4 0.6 pad_maximum_fusion.5.scalars_ref
  202.0 0.1 compare_reduce_fusion.1
  202.1 0.1 compare_reduce_fusion
  202.3 1.3 broadcast_select_fusion.1
  203.6 0.6 pad_add_fusion.tiles_ref
  204.2 0.0 collective-permute-done.4
  204.2 3.5 %pad_maximum_fusion.right_ref = bf16[4,1024,512]{2,1,0:T(8,128)(2,1)} fusion(bf16[2,1024,512]{2,1,0:T(8,128)(2,1)} %collective-permute-done.4, bf16[1,1024,512]{2,1,0:T(8,128)(2,1)} %bitcast.16, bf16[1,1024,512]{2,1,0:T(8,128)(2,1)S(1)} %copy-done.3), kind=kLoop, calls=%fused_computation.6 | loop fusion | flops 4194304 | bytes 8388608 | tf_op jit(solution)/shard_map/stack | solution.py:106
  207.7 0.0 collective-permute-done.2.theirs_ref
  207.7 19.4 %shard_map.73 = f32[512,512]{1,0:T(8,128)} custom-call(s32[48]{0:T(128)} %pad_add_fusion.tiles_ref, f32[48]{0:T(128)} %pad_maximum_fusion.5.scalars_ref, bf16[6,512,1024]{2,1,0:T(8,128)(2,1)} %all-reduce.2.cloned.1.call-done.mine_ref, bf16[6,512,1024]{2,1,0:T(8,128)(2,1)} %collective-permute-done.2.theirs_ref, ...), custom_call_target="tpu_custom_call" | custom-call | tf_op jit(solution)/shard_map/pallas_call | solution.py:66
  227.1 3.3 %fusion.19 = f32[512,512]{1,0:T(8,128)S(1)} fusion(f32[512,512]{1,0:T(8,128)} %shard_map.73, f32[512,512]{1,0:T(8,128)S(1)} %copy-done.2, f32[512,512]{0,1:T(8,128)S(1)} %copy.32, f32[512]{0:T(512)S(1)} %copy-done.4), kind=kOutput, calls=%fused_computation.90 | convolution fusion | flops 1611923456 | bytes 4196352 | tf_op jit(solution)/shard_map/dot_general | solution.py:139
  230.4 0.0 copy-done.1
  230.4 2.9 %fusion = f32[1,512,512]{2,1,0:T(8,128)} fusion(f32[512,512]{1,0:T(8,128)S(1)} %fusion.19, f32[512,512]{1,0:T(8,128)S(1)} %copy-done.1, f32[512,512]{1,0:T(8,128)S(1)} %copy-done.2, f32[512,512]{0,1:T(8,128)S(1)} %copy.32, f32[512]{0:T(512)S(1)} %copy-done.4), kind=kOutput, calls=%fused_computation.9 | convolution fusion | flops 1612185600 | bytes 5244928 | tf_op jit(solution)/shard_map/dot_general | solution.py:138
  (25 shorter events, 0.2 us)
Async XLA Ops:
  6.5 161.1 %copy-start = (f32[128]{0:T(128)S(1)}, f32[128]{0:T(128)}, u32[]{:S(2)}) copy-start(f32[128]{0:T(128)} %param.8) | copy-start | bytes 1540
  6.5 156.5 %all-reduce.2.cloned.1.call-start = ((), (), s32[]{:S(2)}) async-start(), calls=%async_computation | async-start | bytes 12582912 | tf_op jit(solution)/shard_map/psum | solution.py:96
  12.2 152.3 %copy-start.5 = (s32[12,1]{0,1:T(1,128)S(1)}, s32[12,1]{0,1:T(1,128)}, u32[]{:S(2)}) copy-start(s32[12,1]{0,1:T(1,128)} %param.12) | copy-start | bytes 148
  12.2 152.3 %copy-start.6 = (f32[12]{0:T(128)S(1)}, f32[12]{0:T(128)}, u32[]{:S(2)}) copy-start(f32[12]{0:T(128)} %param.13) | copy-start | bytes 148
  12.2 154.8 %copy-start.3 = (bf16[1,1024,512]{2,1,0:T(8,128)(2,1)S(1)}, bf16[1,1024,512]{2,1,0:T(8,128)(2,1)}, u32[]{:S(2)}) copy-start(bf16[1,1024,512]{2,1,0:T(8,128)(2,1)} %param.7) | copy-start | bytes 3145732
  12.2 156.3 %copy-start.4 = (f32[512]{0:T(512)S(1)}, f32[512]{0:T(512)}, u32[]{:S(2)}) copy-start(f32[512]{0:T(512)} %param.9) | copy-start | bytes 6148
  12.2 158.9 %copy-start.2 = (f32[512,512]{1,0:T(8,128)S(1)}, f32[512,512]{1,0:T(8,128)}, u32[]{:S(2)}) copy-start(f32[512,512]{1,0:T(8,128)} %param.10) | copy-start | bytes 3145732
  163.0 44.7 %collective-permute-start.2 = (bf16[6,512,1024]{2,1,0:T(8,128)(2,1)}, bf16[6,512,1024]{2,1,0:T(8,128)(2,1)}, u32[]{:S(2)}, u32[]{:S(2)}) collective-permute-start(bf16[6,512,1024]{2,1,0:T(8,128)(2,1)} %all-reduce.2.cloned.1.call-done.mine_ref), channel_id=1, source_target_pairs={{0,32},{32,0},{1,33},{33,1},{2,34},{34,2},{3,35},{35,3},{4,36},{36... | collective-permute-start | bytes 18874376 | tf_op jit(solution)/shard_map/ppermute | solution.py:97
  164.5 5.7 %collective-permute-start = (f32[24]{0:T(128)S(1)}, f32[24]{0:T(128)S(1)}, u32[]{:S(2)}, u32[]{:S(2)}) collective-permute-start(f32[24]{0:T(128)S(1)} %pad_maximum_fusion.4), channel_id=1, source_target_pairs={{0,64},{64,0},{1,65},{65,1},{2,66},{66,2},{3,67},{67,3},{4,68},{68... | collective-permute-start | bytes 296 | tf_op jit(solution)/shard_map/ppermute | solution.py:103
  167.0 26.0 %collective-permute-start.3 = (bf16[1024,512]{1,0:T(8,128)(2,1)S(1)}, bf16[1024,512]{1,0:T(8,128)(2,1)}, u32[]{:S(2)}, u32[]{:S(2)}) collective-permute-start(bf16[1024,512]{1,0:T(8,128)(2,1)S(1)} %bitcast.41), channel_id=1, source_target_pairs={{0,64},{64,0},{1,65},{65,1},{2,66},{66,2},{3,67},{67,3},{4,68},{68... | collective-permute-start | bytes 3145736 | tf_op jit(solution)/shard_map/ppermute | solution.py:102
  170.2 4.3 %collective-permute-start.1 = (f32[2,24]{1,0:T(2,128)S(1)}, f32[2,24]{1,0:T(2,128)S(1)}, u32[]{:S(2)}, u32[]{:S(2)}) collective-permute-start(f32[2,24]{1,0:T(2,128)S(1)} %pad_maximum_fusion.3), channel_id=1, source_target_pairs={{0,32},{32,0},{1,33},{33,1},{2,34},{34,2},{3,35},{35,3},{4,36},{36... | collective-permute-start | bytes 584 | tf_op jit(solution)/shard_map/ppermute | solution.py:105
  195.8 8.4 %collective-permute-start.4 = (bf16[2,1024,512]{2,1,0:T(8,128)(2,1)}, bf16[2,1024,512]{2,1,0:T(8,128)(2,1)}, u32[]{:S(2)}, u32[]{:S(2)}) collective-permute-start(bf16[2,1024,512]{2,1,0:T(8,128)(2,1)} %pad_maximum_fusion.1), channel_id=1, source_target_pairs={{0,32},{32,0},{1,33},{33,1},{2,34},{34,2},{3,35},{35,3},{4,36},{36... | collective-permute-start | bytes 6291464 | tf_op jit(solution)/shard_map/ppermute | solution.py:104
  227.1 3.3 %copy-start.1 = (f32[512,512]{1,0:T(8,128)S(1)}, f32[512,512]{1,0:T(8,128)}, u32[]{:S(2)}) copy-start(f32[512,512]{1,0:T(8,128)} %shard_map.73) | copy-start | bytes 3145732
Sparse Core Ops, SparseCore 0:
  12.3 150.6 all-reduce.1

commit v7 on v6

--- a/solution.py
+++ b/solution.py
@@ -9,30 +9,37 @@
 CAP = 4
 
 
-def slot_kernel(tiles_ref, scalars_ref, mine_ref, theirs_ref, right_ref, pair_ref, out_ref):
+def amplitude_of(step, slots, scalars_ref, left_ref, right_ref, pair_ref):
+    integral = jnp.dot(left_ref[...], right_ref[...], preferred_element_type=jnp.float32)
+    denominator = (pair_ref[...] - scalars_ref[step]) - scalars_ref[slots + step]
+    amplitude = ((integral / denominator) * scalars_ref[2 * slots + step]).astype(jnp.bfloat16)
+    return amplitude.astype(jnp.float32)
+
+
+def own_kernel(tiles_ref, scalars_ref, left_ref, right_ref, pair_ref, out_ref):
     step = pl.program_id(0)
     slots = pl.num_programs(0)
 
-    def accumulate(left_ref):
-        integral = jnp.dot(left_ref[...], right_ref[...], preferred_element_type=jnp.float32)
-        denominator = (pair_ref[...] - scalars_ref[step]) - scalars_ref[slots + step]
-        amplitude = ((integral / denominator) * scalars_ref[2 * slots + step]).astype(jnp.bfloat16)
-
-        @pl.when(step == 0)
-        def _():
-            out_ref[...] = amplitude.astype(jnp.float32)
-
-        @pl.when(step > 0)
-        def _():
-            out_ref[...] += amplitude.astype(jnp.float32)
+    @pl.when(step == 0)
+    def _():
+        out_ref[...] = jnp.zeros(out_ref.shape, out_ref.dtype)
 
     @pl.when(tiles_ref[step] == 0)
     def _():
-        accumulate(mine_ref)
+        out_ref[...] += amplitude_of(step, slots, scalars_ref, left_ref, right_ref, pair_ref)
+
+
+def other_kernel(tiles_ref, scalars_ref, left_ref, right_ref, pair_ref, acc_ref, out_ref):
+    step = pl.program_id(0)
+    slots = pl.num_programs(0)
+
+    @pl.when(step == 0)
+    def _():
+        out_ref[...] = acc_ref[...]
 
     @pl.when(tiles_ref[step] != 0)
     def _():
-        accumulate(theirs_ref)
+        out_ref[...] += amplitude_of(step, slots, scalars_ref, left_ref, right_ref, pair_ref)
 
 
 def held_index(present, local):
@@ -51,24 +58,33 @@
     tables = jnp.concatenate(
         [in_theirs.astype(jnp.int32), held_index(~in_theirs, local), held_index(in_theirs, local)]
     )
-    grid_spec = pltpu.PrefetchScalarGridSpec(
-        num_scalar_prefetch=1,
-        grid=(slots,),
-        in_specs=[
-            pl.BlockSpec(memory_space=pltpu.SMEM),
-            pl.BlockSpec((None, rows, depth), lambda s, tiles: (tiles[slots + s], 0, 0)),
-            pl.BlockSpec((None, rows, depth), lambda s, tiles: (tiles[2 * slots + s], 0, 0)),
-            pl.BlockSpec((None, depth, rows), lambda s, tiles: (s // per_source, 0, 0)),
-            pl.BlockSpec((rows, rows), lambda s, tiles: (0, 0)),
-        ],
-        out_specs=pl.BlockSpec((rows, rows), lambda s, tiles: (0, 0)),
-    )
+
+    def specs(offset, extra):
+        return pltpu.PrefetchScalarGridSpec(
+            num_scalar_prefetch=1,
+            grid=(slots,),
+            in_specs=[
+                pl.BlockSpec(memory_space=pltpu.SMEM),
+                pl.BlockSpec((None, rows, depth), lambda s, tiles: (tiles[offset + s], 0, 0)),
+                pl.BlockSpec((None, depth, rows), lambda s, tiles: (s // per_source, 0, 0)),
+                pl.BlockSpec((rows, rows), lambda s, tiles: (0, 0)),
+            ]
+            + [pl.BlockSpec((rows, rows), lambda s, tiles: (0, 0))] * extra,
+            out_specs=pl.BlockSpec((rows, rows), lambda s, tiles: (0, 0)),
+        )
+
+    params = pltpu.CompilerParams(dimension_semantics=("arbitrary",))
+    out_shape = jax.ShapeDtypeStruct((rows, rows), jnp.float32)
+    partial = pl.pallas_call(
+        own_kernel, grid_spec=specs(slots, 0), out_shape=out_shape, compiler_params=params
+    )(tables, scalars, mine, column, pair_sum)
     return pl.pallas_call(
-        slot_kernel,
-        grid_spec=grid_spec,
-        out_shape=jax.ShapeDtypeStruct((rows, rows), jnp.float32),
-        compiler_params=pltpu.CompilerParams(dimension_semantics=("arbitrary",)),
-    )(tables, scalars, mine, theirs, column, pair_sum)
+        other_kernel,
+        grid_spec=specs(2 * slots, 1),
+        out_shape=out_shape,
+        compiler_params=params,
+        input_output_aliases={5: 0},
+    )(tables, scalars, theirs, column, pair_sum, partial)
 
 
 def layer(df_panels, occ_energy, virt_energy, fock_off, i_plan, pair_owner, pair_weight):

time: 241 us -> 254 us (1.054)
  the two profiles are of different devices: /device:TPU:1 before, /device:TPU:83 now
where the time goes in v7:
time: 254 us; the launch traced here: 253 us
  waiting for transfers between devices  164 us (65%)
  Pallas kernels  36.7 us (14%)
  between operations  17.5 us (7%)
  other arithmetic  16.6 us (7%)
  local copies, waits for them, and re-layouts  6.67 us (3%)
  matrix products  6.21 us (2%)
  starting transfers between devices  5.62 us (2%)
    psum x1, waiting for transfers between devices, layer(): own_half = lax.psum(masked, ('zh', 'orb'))  148 us
    pallas_call x1, Pallas kernels, summed_tiles(): pl.pallas_call(other_kernel, grid_spec=specs(2 * slots, 1), out_shape=out...  19.5 us
    pallas_call x1, Pallas kernels, summed_tiles(): pl.pallas_call(own_kernel, grid_spec=specs(slots, 0), out_shape=out_shape...  17.2 us
    ppermute x1, waiting for transfers between devices, layer(): far_panel = lax.ppermute(own_panel, 'zh', across)  12.8 us
  transfers between devices with their start and end apart: 6, of which 3 were waited for; matrix products, arithmetic and copies ran while one was open for 7% of the time, Pallas kernels for 7%

profile of v7, /device:TPU:83, one launch (start us, length us, event | category | flops | bytes accessed | tf_op | source)
XLA Modules:
  0.0 253.3 jit_solution(6124117374910971624)
XLA Ops:
  6.5 0.0 copy-start
  6.5 0.0 all-reduce.2.cloned.1.call-start
  6.5 0.7 broadcast_add_fusion.1
  7.2 0.1 copy.38
  7.3 0.1 copy.40
  7.5 0.1 eq.78
  7.5 1.5 copy.41
  9.0 3.1 %broadcast_select_fusion = bf16[6,512,1024]{2,1,0:T(8,128)(2,1)} fusion(pred[6]{0:T(512)(128)(4,1)S(1)} %eq.78, bf16[512,1024]{1,0:T(8,128)(2,1)S(1)} %copy.41), kind=kLoop, calls=%fused_computation.5 | loop fusion | flops 3145728 | bytes 7340038 | tf_op jit(solution)/shard_map/jit(_where)/select_n | solution.py:109
  12.2 0.0 copy-start.2
  12.2 0.0 all-reduce.2.cloned.1.call-update
  12.2 147.9 %all-reduce.2.cloned.1.call-done.left_ref = bf16[6,512,1024]{2,1,0:T(8,128)(2,1)} async-done(((bf16[6,512,1024]{2,1,0:T(8,128)(2,1)}), bf16[6,512,1024]{2,1,0:T(8,128)(2,1)}) %all-reduce.2.cloned.1.call-update) | async-done | bytes 6291472 | tf_op jit(solution)/shard_map/psum | solution.py:112
  160.1 0.8 collective-permute-start.2
  161.0 0.0 copy-done.5
  161.0 0.0 copy-done.6
  161.0 0.1 pad_maximum_fusion.4
  161.1 1.7 collective-permute-start
  162.8 0.0 copy-done.3
  162.8 1.2 collective-permute-start.3
  164.0 0.1 reshape.380
  164.1 0.1 fusion.16
  164.2 0.0 copy-done
  164.2 0.6 gather_fusion.4
  164.9 0.1 fusion.28
  164.9 0.0 copy-done.4
  165.0 1.1 broadcast_add_fusion.pair_ref
  166.1 0.1 broadcast_in_dim.104
  166.1 0.1 reshape.382
  166.2 0.0 collective-permute-done
  166.2 0.7 collective-permute-start.1
  166.9 0.7 gather_fusion.2
  167.5 0.0 copy-done.2
  167.6 0.3 copy.33
  167.9 3.2 %collective-permute-done.1 = f32[2,24]{1,0:T(2,128)S(1)} collective-permute-done((f32[2,24]{1,0:T(2,128)S(1)}, f32[2,24]{1,0:T(2,128)S(1)}, u32[]{:S(2)}, u32[]{:S(2)}) %collective-permute-start.1) | collective-permute-done | bytes 224 | tf_op jit(solution)/shard_map/ppermute | solution.py:121
  171.1 0.1 fusion.24
  171.2 0.2 reduce_window_sum.11
  171.4 0.1 select_reduce_fusion.1
  171.5 0.1 reduce_sum.25
  171.6 0.7 iota_reduce_fusion
  173.6 0.7 not_reduce_fusion
  175.8 0.1 reduce_sum.29
  175.8 0.1 select_reduce_fusion
  175.9 0.1 reshape.383
  176.0 12.8 %collective-permute-done.3 = bf16[1024,512]{1,0:T(8,128)(2,1)} collective-permute-done((bf16[1024,512]{1,0:T(8,128)(2,1)S(1)}, bf16[1024,512]{1,0:T(8,128)(2,1)}, u32[]{:S(2)}, u32[]{:S(2)}) %collective-permute-start.3) | collective-permute-done | bytes 1048608 | tf_op jit(solution)/shard_map/ppermute | solution.py:118
  188.8 2.8 %pad_maximum_fusion.1 = bf16[2,1024,512]{2,1,0:T(8,128)(2,1)} fusion(bf16[1,1024,512]{2,1,0:T(8,128)(2,1)} %bitcast.16, bf16[1,1024,512]{2,1,0:T(8,128)(2,1)S(1)} %copy-done.3), kind=kLoop, calls=%fused_computation.7 | loop fusion | flops 1048576 | bytes 4194304 | tf_op jit(solution)/shard_map/stack | solution.py:120
  191.6 1.1 collective-permute-start.4
  192.8 0.1 reshape.410
  193.0 0.1 maximum_reduce_fusion.1
  193.1 0.7 gather_fusion
  193.8 0.1 maximum_reduce_fusion
  193.9 0.7 gather_fusion.1
  194.6 0.7 gather_fusion.3
  196.6 0.7 fusion.25
  197.2 0.6 pad_maximum_fusion.5.scalars_ref
  197.8 0.1 compare_reduce_fusion
  197.9 0.1 compare_reduce_fusion.1
  198.1 1.3 broadcast_select_fusion.1
  199.4 0.6 pad_add_fusion.tiles_ref
  200.0 0.0 collective-permute-done.4
  200.0 3.5 %pad_maximum_fusion.right_ref = bf16[4,1024,512]{2,1,0:T(8,128)(2,1)} fusion(bf16[2,1024,512]{2,1,0:T(8,128)(2,1)} %collective-permute-done.4, bf16[1,1024,512]{2,1,0:T(8,128)(2,1)} %bitcast.16, bf16[1,1024,512]{2,1,0:T(8,128)(2,1)S(1)} %copy-done.3), kind=kLoop, calls=%fused_computation.6 | loop fusion | flops 4194304 | bytes 8388608 | tf_op jit(solution)/shard_map/stack | solution.py:122
  203.5 17.2 %shard_map.73.acc_ref = f32[512,512]{1,0:T(8,128)} custom-call(s32[48]{0:T(128)} %pad_add_fusion.tiles_ref, f32[48]{0:T(128)} %pad_maximum_fusion.5.scalars_ref, bf16[6,512,1024]{2,1,0:T(8,128)(2,1)} %all-reduce.2.cloned.1.call-done.left_ref, bf16[4,1024,512]{2,1,0:T(8,128)(2,1)} %pad_maximum_fusion.right_ref, f32[512,512]{1,0:T(8,128)} %broadcast_add_fusion.pair_ref), custom_call_target="tpu_custom_call" | custom-call | tf_op jit(solution)/shard_map/pallas_call | solution.py:78
  220.7 0.0 collective-permute-done.2.left_ref
  220.7 19.5 %shard_map.74 = f32[512,512]{1,0:T(8,128)} custom-call(s32[48]{0:T(128)} %pad_add_fusion.tiles_ref, f32[48]{0:T(128)} %pad_maximum_fusion.5.scalars_ref, bf16[6,512,1024]{2,1,0:T(8,128)(2,1)} %collective-permute-done.2.left_ref, bf16[4,1024,512]{2,1,0:T(8,128)(2,1)} %pad_maximum_fusion.right_ref, ...), custom_call_target="tpu_custom_call", output_to_operand_aliasing={{}: (5, {})} | custom-call | tf_op jit(solution)/shard_map/pallas_call | solution.py:81
  240.2 3.3 %fusion.19 = f32[512,512]{1,0:T(8,128)S(1)} fusion(f32[512,512]{1,0:T(8,128)} %shard_map.74, f32[512,512]{1,0:T(8,128)S(1)} %copy-done.2, f32[512,512]{0,1:T(8,128)S(1)} %copy.33, f32[512]{0:T(512)S(1)} %copy-done.4), kind=kOutput, calls=%fused_computation.90 | convolution fusion | flops 1611923456 | bytes 4196352 | tf_op jit(solution)/shard_map/dot_general | solution.py:155
  243.5 2.9 %fusion = f32[1,512,512]{2,1,0:T(8,128)} fusion(f32[512,512]{1,0:T(8,128)S(1)} %fusion.19, f32[512,512]{1,0:T(8,128)S(1)} %copy-done.1, f32[512,512]{1,0:T(8,128)S(1)} %copy-done.2, f32[512,512]{0,1:T(8,128)S(1)} %copy.33, f32[512]{0:T(512)S(1)} %copy-done.4), kind=kOutput, calls=%fused_computation.9 | convolution fusion | flops 1612185600 | bytes 5244928 | tf_op jit(solution)/shard_map/dot_general | solution.py:154
  (26 shorter events, 0.2 us)
Async XLA Ops:
  6.5 157.7 %copy-start = (f32[128]{0:T(128)S(1)}, f32[128]{0:T(128)}, u32[]{:S(2)}) copy-start(f32[128]{0:T(128)} %param.8) | copy-start | bytes 1540
  6.5 153.6 %all-reduce.2.cloned.1.call-start = ((), (), s32[]{:S(2)}) async-start(), calls=%async_computation | async-start | bytes 12582912 | tf_op jit(solution)/shard_map/psum | solution.py:112
  12.2 148.8 %copy-start.5 = (s32[12,1]{0,1:T(1,128)S(1)}, s32[12,1]{0,1:T(1,128)}, u32[]{:S(2)}) copy-start(s32[12,1]{0,1:T(1,128)} %param.12) | copy-start | bytes 148
  12.2 148.8 %copy-start.6 = (f32[12]{0:T(128)S(1)}, f32[12]{0:T(128)}, u32[]{:S(2)}) copy-start(f32[12]{0:T(128)} %param.13) | copy-start | bytes 148
  12.2 150.6 %copy-start.3 = (bf16[1,1024,512]{2,1,0:T(8,128)(2,1)S(1)}, bf16[1,1024,512]{2,1,0:T(8,128)(2,1)}, u32[]{:S(2)}) copy-start(bf16[1,1024,512]{2,1,0:T(8,128)(2,1)} %param.7) | copy-start | bytes 3145732
  12.2 152.8 %copy-start.4 = (f32[512]{0:T(512)S(1)}, f32[512]{0:T(512)}, u32[]{:S(2)}) copy-start(f32[512]{0:T(512)} %param.9) | copy-start | bytes 6148
  12.2 155.4 %copy-start.2 = (f32[512,512]{1,0:T(8,128)S(1)}, f32[512,512]{1,0:T(8,128)}, u32[]{:S(2)}) copy-start(f32[512,512]{1,0:T(8,128)} %param.10) | copy-start | bytes 3145732
  160.1 60.6 %collective-permute-start.2 = (bf16[6,512,1024]{2,1,0:T(8,128)(2,1)}, bf16[6,512,1024]{2,1,0:T(8,128)(2,1)}, u32[]{:S(2)}, u32[]{:S(2)}) collective-permute-start(bf16[6,512,1024]{2,1,0:T(8,128)(2,1)} %all-reduce.2.cloned.1.call-done.left_ref), channel_id=1, source_target_pairs={{0,32},{32,0},{1,33},{33,1},{2,34},{34,2},{3,35},{35,3},{4,36},{36... | collective-permute-start | bytes 18874376 | tf_op jit(solution)/shard_map/ppermute | solution.py:113
  161.1 5.2 %collective-permute-start = (f32[24]{0:T(128)S(1)}, f32[24]{0:T(128)S(1)}, u32[]{:S(2)}, u32[]{:S(2)}) collective-permute-start(f32[24]{0:T(128)S(1)} %pad_maximum_fusion.4), channel_id=1, source_target_pairs={{0,64},{64,0},{1,65},{65,1},{2,66},{66,2},{3,67},{67,3},{4,68},{68... | collective-permute-start | bytes 296 | tf_op jit(solution)/shard_map/ppermute | solution.py:119
  162.8 26.0 %collective-permute-start.3 = (bf16[1024,512]{1,0:T(8,128)(2,1)S(1)}, bf16[1024,512]{1,0:T(8,128)(2,1)}, u32[]{:S(2)}, u32[]{:S(2)}) collective-permute-start(bf16[1024,512]{1,0:T(8,128)(2,1)S(1)} %bitcast.41), channel_id=1, source_target_pairs={{0,64},{64,0},{1,65},{65,1},{2,66},{66,2},{3,67},{67,3},{4,68},{68... | collective-permute-start | bytes 3145736 | tf_op jit(solution)/shard_map/ppermute | solution.py:118
  166.2 4.9 %collective-permute-start.1 = (f32[2,24]{1,0:T(2,128)S(1)}, f32[2,24]{1,0:T(2,128)S(1)}, u32[]{:S(2)}, u32[]{:S(2)}) collective-permute-start(f32[2,24]{1,0:T(2,128)S(1)} %pad_maximum_fusion.3), channel_id=1, source_target_pairs={{0,32},{32,0},{1,33},{33,1},{2,34},{34,2},{3,35},{35,3},{4,36},{36... | collective-permute-start | bytes 584 | tf_op jit(solution)/shard_map/ppermute | solution.py:121
  191.6 8.3 %collective-permute-start.4 = (bf16[2,1024,512]{2,1,0:T(8,128)(2,1)}, bf16[2,1024,512]{2,1,0:T(8,128)(2,1)}, u32[]{:S(2)}, u32[]{:S(2)}) collective-permute-start(bf16[2,1024,512]{2,1,0:T(8,128)(2,1)} %pad_maximum_fusion.1), channel_id=1, source_target_pairs={{0,32},{32,0},{1,33},{33,1},{2,34},{34,2},{3,35},{35,3},{4,36},{36... | collective-permute-start | bytes 6291464 | tf_op jit(solution)/shard_map/ppermute | solution.py:120
  240.2 3.3 %copy-start.1 = (f32[512,512]{1,0:T(8,128)S(1)}, f32[512,512]{1,0:T(8,128)}, u32[]{:S(2)}) copy-start(f32[512,512]{1,0:T(8,128)} %shard_map.74) | copy-start | bytes 3145732
Sparse Core Ops, SparseCore 0:
  12.3 147.7 all-reduce.1

commit v8 on v6

--- a/solution.py
+++ b/solution.py
@@ -135,9 +135,12 @@
     summed = summed_tiles(position.reshape(-1), scalars, own_half, other_half, column, pair_sum)
 
     fock_matrix = jnp.diag(virt_energy) + 0.5 * (fock_off + fock_off.T)
-    left = jnp.dot(fock_matrix, summed, precision=highest)
-    right = jnp.dot(summed, fock_matrix, precision=highest)
-    return (left + right)[None]
+    paired = jnp.dot(
+        jnp.concatenate([fock_matrix, summed], axis=1),
+        jnp.concatenate([summed, fock_matrix], axis=0),
+        precision=highest,
+    )
+    return paired[None]
 
 
 def solution(mesh):

time: 241 us -> 241 us (level)
  waiting for transfers between devices: 168 us -> 165 us
    dot_general x2 -> x1, matrix products: 6.22 us -> 6.09 us  [layer(): jnp.dot(jnp.concatenate([fock_matrix, summed], axis=1), jnp.concatenate([...]
  transfers between devices with their start and end apart: 6 -> 6, of which waited for: 3 -> 3; matrix products, arithmetic and copies ran while one was open for 7% -> 8% of each run, Pallas kernels for 0% -> 0%
where the time goes in v8:
time: 241 us; the launch traced here: 240 us
  waiting for transfers between devices  165 us (68%)
  Pallas kernels  19.4 us (8%)
  other arithmetic  17.9 us (7%)
  between operations  17.5 us (7%)
  local copies, waits for them, and re-layouts  7.64 us (3%)
  starting transfers between devices  6.23 us (3%)
  matrix products  6.09 us (3%)
    psum x1, waiting for transfers between devices, layer(): own_half = lax.psum(masked, ('zh', 'orb'))  151 us
    pallas_call x1, Pallas kernels, summed_tiles(): pl.pallas_call(slot_kernel, grid_spec=grid_spec, out_shape=jax.ShapeDtype...  19.4 us
    ppermute x1, waiting for transfers between devices, layer(): far_panel = lax.ppermute(own_panel, 'zh', across)  13.5 us
    dot_general x1, matrix products, layer(): jnp.dot(jnp.concatenate([fock_matrix, summed], axis=1), jnp.concatenate([...  6.09 us
  transfers between devices with their start and end apart: 6, of which 3 were waited for; matrix products, arithmetic and copies ran while one was open for 8% of the time, Pallas kernels for 0%

profile of v8, /device:TPU:1, one launch (start us, length us, event | category | flops | bytes accessed | tf_op | source)
XLA Modules:
  0.0 240.0 jit_solution(11074253071574817198)
XLA Ops:
  6.5 0.0 copy-start
  6.5 0.0 all-reduce.2.cloned.1.call-start
  6.5 0.7 broadcast_add_fusion.1
  7.2 0.1 copy.37
  7.3 0.1 copy.39
  7.5 0.1 eq.78
  7.5 1.5 copy.40
  9.0 3.1 %broadcast_select_fusion = bf16[6,512,1024]{2,1,0:T(8,128)(2,1)} fusion(pred[6]{0:T(512)(128)(4,1)S(1)} %eq.78, bf16[512,1024]{1,0:T(8,128)(2,1)S(1)} %copy.40), kind=kLoop, calls=%fused_computation.5 | loop fusion | flops 3145728 | bytes 7340038 | tf_op jit(solution)/shard_map/jit(_where)/select_n | solution.py:93
  12.2 0.0 copy-start.4
  12.2 0.0 copy-start.5
  12.2 0.0 all-reduce.2.cloned.1.call-update
  12.2 0.0 copy-start.3
  12.2 150.8 %all-reduce.2.cloned.1.call-done.mine_ref = bf16[6,512,1024]{2,1,0:T(8,128)(2,1)} async-done(((bf16[6,512,1024]{2,1,0:T(8,128)(2,1)}), bf16[6,512,1024]{2,1,0:T(8,128)(2,1)}) %all-reduce.2.cloned.1.call-update) | async-done | bytes 6291472 | tf_op jit(solution)/shard_map/psum | solution.py:96
  163.0 1.4 collective-permute-start.2
  164.5 0.0 copy-done.4
  164.5 0.0 copy-done.5
  164.5 0.1 pad_maximum_fusion.4
  164.5 2.4 %collective-permute-start = (f32[24]{0:T(128)S(1)}, f32[24]{0:T(128)S(1)}, u32[]{:S(2)}, u32[]{:S(2)}) collective-permute-start(f32[24]{0:T(128)S(1)} %pad_maximum_fusion.4), channel_id=1, source_target_pairs={{0,64},{64,0},{1,65},{65,1},{2,66},{66,2},{3,67},{67,3},{4,68},{68... | collective-permute-start | bytes 296 | tf_op jit(solution)/shard_map/ppermute | solution.py:103
  167.0 0.0 copy-done.1
  167.0 0.6 collective-permute-start.3
  167.5 0.1 reshape.380
  167.6 0.0 copy-done.2
  167.6 1.3 copy.32
  168.9 0.1 fusion.35
  169.0 0.1 fusion.27
  169.1 0.0 copy-done.3
  169.1 2.4 %broadcast_add_fusion = (f32[512,512]{1,0:T(8,128)}, f32[512,512]{1,0:T(8,128)S(1)}) fusion(f32[512]{0:T(512)S(1)} %copy-done.3, f32[512,512]{1,0:T(8,128)S(1)} %copy-done.2, f32[512,512]{0,1:T(8,128)} %copy.32), kind=kLoop, calls=%fused_computation.20 | loop fusion | flops 1572864 | bytes 4196352 | tf_op jit(solution)/shard_map/add | solution.py:119
  171.5 0.0 copy-done
  171.5 0.7 gather_fusion.2
  172.2 0.0 collective-permute-done
  172.2 0.6 collective-permute-start.1
  172.9 0.6 gather_fusion.4
  173.5 0.1 broadcast_in_dim.104
  173.6 0.1 reshape.382
  173.7 0.9 collective-permute-done.1
  174.6 0.1 fusion.33
  174.7 0.2 reduce_window_sum.11
  174.9 0.1 select_reduce_fusion.1
  175.0 0.1 reduce_sum.25
  175.1 0.7 iota_reduce_fusion
  177.1 0.7 not_reduce_fusion
  179.2 0.1 reduce_sum.29
  179.3 0.1 select_reduce_fusion
  179.4 0.1 reshape.383
  179.5 13.5 %collective-permute-done.3 = bf16[1024,512]{1,0:T(8,128)(2,1)} collective-permute-done((bf16[1024,512]{1,0:T(8,128)(2,1)S(1)}, bf16[1024,512]{1,0:T(8,128)(2,1)}, u32[]{:S(2)}, u32[]{:S(2)}) %collective-permute-start.3) | collective-permute-done | bytes 1048608 | tf_op jit(solution)/shard_map/ppermute | solution.py:102
  193.0 2.8 %pad_maximum_fusion.1 = bf16[2,1024,512]{2,1,0:T(8,128)(2,1)} fusion(bf16[1,1024,512]{2,1,0:T(8,128)(2,1)} %bitcast.16, bf16[1,1024,512]{2,1,0:T(8,128)(2,1)S(1)} %copy-done.1), kind=kLoop, calls=%fused_computation.7 | loop fusion | flops 1048576 | bytes 4194304 | tf_op jit(solution)/shard_map/stack | solution.py:104
  195.8 1.1 collective-permute-start.4
  196.9 0.1 reshape.410
  197.1 0.1 maximum_reduce_fusion.1
  197.3 0.7 gather_fusion
  197.9 0.1 maximum_reduce_fusion
  198.1 0.7 gather_fusion.1
  200.1 0.7 gather_fusion.3
  200.7 0.7 fusion.34
  201.4 0.6 pad_maximum_fusion.5.scalars_ref
  202.0 0.1 compare_reduce_fusion.1
  202.1 0.1 compare_reduce_fusion
  202.2 1.3 broadcast_select_fusion.1
  203.6 0.6 pad_add_fusion.tiles_ref
  204.1 0.0 collective-permute-done.4
  204.1 3.5 %pad_maximum_fusion.right_ref = bf16[4,1024,512]{2,1,0:T(8,128)(2,1)} fusion(bf16[2,1024,512]{2,1,0:T(8,128)(2,1)} %collective-permute-done.4, bf16[1,1024,512]{2,1,0:T(8,128)(2,1)} %bitcast.16, bf16[1,1024,512]{2,1,0:T(8,128)(2,1)S(1)} %copy-done.1), kind=kLoop, calls=%fused_computation.6 | loop fusion | flops 4194304 | bytes 8388608 | tf_op jit(solution)/shard_map/stack | solution.py:106
  207.7 0.0 collective-permute-done.2.theirs_ref
  207.7 19.4 %shard_map.73 = f32[512,512]{1,0:T(8,128)} custom-call(s32[48]{0:T(128)} %pad_add_fusion.tiles_ref, f32[48]{0:T(128)} %pad_maximum_fusion.5.scalars_ref, bf16[6,512,1024]{2,1,0:T(8,128)(2,1)} %all-reduce.2.cloned.1.call-done.mine_ref, bf16[6,512,1024]{2,1,0:T(8,128)(2,1)} %collective-permute-done.2.theirs_ref, ...), custom_call_target="tpu_custom_call" | custom-call | tf_op jit(solution)/shard_map/pallas_call | solution.py:66
  227.1 6.1 %fusion.7 = f32[1,512,512]{2,1,0:T(8,128)} fusion(f32[512,512]{1,0:T(8,128)S(1)} %get-tuple-element.16, f32[512,512]{1,0:T(8,128)} %shard_map.73), kind=kOutput, calls=%fused_computation.15 | convolution fusion | flops 3222274048 | bytes 3145728 | tf_op jit(solution)/shard_map/dot_general | solution.py:138
  (22 shorter events, 0.2 us)
Async XLA Ops:
  6.5 165.0 %copy-start = (f32[128]{0:T(128)S(1)}, f32[128]{0:T(128)}, u32[]{:S(2)}) copy-start(f32[128]{0:T(128)} %param.8) | copy-start | bytes 1540
  6.5 156.5 %all-reduce.2.cloned.1.call-start = ((), (), s32[]{:S(2)}) async-start(), calls=%async_computation | async-start | bytes 12582912 | tf_op jit(solution)/shard_map/psum | solution.py:96
  12.2 152.3 %copy-start.4 = (s32[12,1]{0,1:T(1,128)S(1)}, s32[12,1]{0,1:T(1,128)}, u32[]{:S(2)}) copy-start(s32[12,1]{0,1:T(1,128)} %param.12) | copy-start | bytes 148
  12.2 152.3 %copy-start.5 = (f32[12]{0:T(128)S(1)}, f32[12]{0:T(128)}, u32[]{:S(2)}) copy-start(f32[12]{0:T(128)} %param.13) | copy-start | bytes 148
  12.2 154.8 %copy-start.1 = (bf16[1,1024,512]{2,1,0:T(8,128)(2,1)S(1)}, bf16[1,1024,512]{2,1,0:T(8,128)(2,1)}, u32[]{:S(2)}) copy-start(bf16[1,1024,512]{2,1,0:T(8,128)(2,1)} %param.7) | copy-start | bytes 3145732
  12.2 155.4 %copy-start.2 = (f32[512,512]{1,0:T(8,128)S(1)}, f32[512,512]{1,0:T(8,128)}, u32[]{:S(2)}) copy-start(f32[512,512]{1,0:T(8,128)} %param.10) | copy-start | bytes 3145732
  12.2 156.9 %copy-start.3 = (f32[512]{0:T(512)S(1)}, f32[512]{0:T(512)}, u32[]{:S(2)}) copy-start(f32[512]{0:T(512)} %param.9) | copy-start | bytes 6148
  163.0 44.7 %collective-permute-start.2 = (bf16[6,512,1024]{2,1,0:T(8,128)(2,1)}, bf16[6,512,1024]{2,1,0:T(8,128)(2,1)}, u32[]{:S(2)}, u32[]{:S(2)}) collective-permute-start(bf16[6,512,1024]{2,1,0:T(8,128)(2,1)} %all-reduce.2.cloned.1.call-done.mine_ref), channel_id=1, source_target_pairs={{0,32},{32,0},{1,33},{33,1},{2,34},{34,2},{3,35},{35,3},{4,36},{36... | collective-permute-start | bytes 18874376 | tf_op jit(solution)/shard_map/ppermute | solution.py:97
  164.5 7.7 %collective-permute-start = (f32[24]{0:T(128)S(1)}, f32[24]{0:T(128)S(1)}, u32[]{:S(2)}, u32[]{:S(2)}) collective-permute-start(f32[24]{0:T(128)S(1)} %pad_maximum_fusion.4), channel_id=1, source_target_pairs={{0,64},{64,0},{1,65},{65,1},{2,66},{66,2},{3,67},{67,3},{4,68},{68... | collective-permute-start | bytes 296 | tf_op jit(solution)/shard_map/ppermute | solution.py:103
  167.0 26.0 %collective-permute-start.3 = (bf16[1024,512]{1,0:T(8,128)(2,1)S(1)}, bf16[1024,512]{1,0:T(8,128)(2,1)}, u32[]{:S(2)}, u32[]{:S(2)}) collective-permute-start(bf16[1024,512]{1,0:T(8,128)(2,1)S(1)} %bitcast.37), channel_id=1, source_target_pairs={{0,64},{64,0},{1,65},{65,1},{2,66},{66,2},{3,67},{67,3},{4,68},{68... | collective-permute-start | bytes 3145736 | tf_op jit(solution)/shard_map/ppermute | solution.py:102
  172.2 2.4 collective-permute-start.1
  195.8 8.4 %collective-permute-start.4 = (bf16[2,1024,512]{2,1,0:T(8,128)(2,1)}, bf16[2,1024,512]{2,1,0:T(8,128)(2,1)}, u32[]{:S(2)}, u32[]{:S(2)}) collective-permute-start(bf16[2,1024,512]{2,1,0:T(8,128)(2,1)} %pad_maximum_fusion.1), channel_id=1, source_target_pairs={{0,32},{32,0},{1,33},{33,1},{2,34},{34,2},{3,35},{35,3},{4,36},{36... | collective-permute-start | bytes 6291464 | tf_op jit(solution)/shard_map/ppermute | solution.py:104
Sparse Core Ops, SparseCore 0:
  12.3 150.6 all-reduce.1

commit v9 on v6

--- a/solution.py
+++ b/solution.py
@@ -14,17 +14,21 @@
     slots = pl.num_programs(0)
 
     def accumulate(left_ref):
-        integral = jnp.dot(left_ref[...], right_ref[...], preferred_element_type=jnp.float32)
-        denominator = (pair_ref[...] - scalars_ref[step]) - scalars_ref[slots + step]
-        amplitude = ((integral / denominator) * scalars_ref[2 * slots + step]).astype(jnp.bfloat16)
+        band = left_ref.shape[0] // 2
+        for lo in (0, band):
+            rows = pl.ds(lo, band)
+            integral = jnp.dot(left_ref[rows, :], right_ref[...], preferred_element_type=jnp.float32)
+            denominator = (pair_ref[rows, :] - scalars_ref[step]) - scalars_ref[slots + step]
+            scaled = (integral / denominator) * scalars_ref[2 * slots + step]
+            amplitude = scaled.astype(jnp.bfloat16).astype(jnp.float32)
 
-        @pl.when(step == 0)
-        def _():
-            out_ref[...] = amplitude.astype(jnp.float32)
+            @pl.when(step == 0)
+            def _():
+                out_ref[rows, :] = amplitude
 
-        @pl.when(step > 0)
-        def _():
-            out_ref[...] += amplitude.astype(jnp.float32)
+            @pl.when(step > 0)
+            def _():
+                out_ref[rows, :] += amplitude
 
     @pl.when(tiles_ref[step] == 0)
     def _():

time: 241 us -> 243 us (level)
  no operation moved by 1% of the time
where the time goes in v9:
time: 243 us; the launch traced here: 242 us
  waiting for transfers between devices  168 us (69%)
  Pallas kernels  21.4 us (9%)
  between operations  17.5 us (7%)
  other arithmetic  16.6 us (7%)
  local copies, waits for them, and re-layouts  6.67 us (3%)
  starting transfers between devices  6.23 us (3%)
  matrix products  6.21 us (3%)
    psum x1, waiting for transfers between devices, layer(): own_half = lax.psum(masked, ('zh', 'orb'))  151 us
    pallas_call x1, Pallas kernels, summed_tiles(): pl.pallas_call(slot_kernel, grid_spec=grid_spec, out_shape=jax.ShapeDtype...  21.4 us
    ppermute x1, waiting for transfers between devices, layer(): far_panel = lax.ppermute(own_panel, 'zh', across)  13.5 us
  transfers between devices with their start and end apart: 6, of which 3 were waited for; matrix products, arithmetic and copies ran while one was open for 7% of the time, Pallas kernels for 0%

profile of v9, /device:TPU:1, one launch (start us, length us, event | category | flops | bytes accessed | tf_op | source)
XLA Modules:
  0.0 242.1 jit_solution(18338709646291579206)
XLA Ops:
  6.5 0.0 copy-start
  6.5 0.0 all-reduce.2.cloned.1.call-start
  6.5 0.7 broadcast_add_fusion.1
  7.2 0.1 copy.37
  7.3 0.1 copy.39
  7.5 0.1 eq.78
  7.5 1.5 copy.40
  9.0 3.1 %broadcast_select_fusion = bf16[6,512,1024]{2,1,0:T(8,128)(2,1)} fusion(pred[6]{0:T(512)(128)(4,1)S(1)} %eq.78, bf16[512,1024]{1,0:T(8,128)(2,1)S(1)} %copy.40), kind=kLoop, calls=%fused_computation.5 | loop fusion | flops 3145728 | bytes 7340038 | tf_op jit(solution)/shard_map/jit(_where)/select_n | solution.py:97
  12.2 0.0 copy-start.2
  12.2 0.0 all-reduce.2.cloned.1.call-update
  12.2 150.8 %all-reduce.2.cloned.1.call-done.mine_ref = bf16[6,512,1024]{2,1,0:T(8,128)(2,1)} async-done(((bf16[6,512,1024]{2,1,0:T(8,128)(2,1)}), bf16[6,512,1024]{2,1,0:T(8,128)(2,1)}) %all-reduce.2.cloned.1.call-update) | async-done | bytes 6291472 | tf_op jit(solution)/shard_map/psum | solution.py:100
  163.0 1.4 collective-permute-start.2
  164.5 0.0 copy-done.5
  164.5 0.0 copy-done.6
  164.5 0.1 pad_maximum_fusion.4
  164.5 2.4 %collective-permute-start = (f32[24]{0:T(128)S(1)}, f32[24]{0:T(128)S(1)}, u32[]{:S(2)}, u32[]{:S(2)}) collective-permute-start(f32[24]{0:T(128)S(1)} %pad_maximum_fusion.4), channel_id=1, source_target_pairs={{0,64},{64,0},{1,65},{65,1},{2,66},{66,2},{3,67},{67,3},{4,68},{68... | collective-permute-start | bytes 296 | tf_op jit(solution)/shard_map/ppermute | solution.py:107
  167.0 0.0 copy-done.3
  167.0 0.6 collective-permute-start.3
  167.5 0.1 reshape.380
  167.6 0.0 copy-done
  167.6 0.7 gather_fusion.2
  168.3 0.1 fusion.28
  168.4 0.1 fusion.16
  168.5 0.0 copy-done.4
  168.5 1.1 broadcast_add_fusion.pair_ref
  169.6 0.6 gather_fusion.4
  170.2 0.0 collective-permute-done
  170.2 0.6 collective-permute-start.1
  170.9 0.1 broadcast_in_dim.104
  171.0 0.1 reshape.382
  171.0 0.0 copy-done.2
  171.1 0.3 copy.32
  171.4 3.2 %collective-permute-done.1 = f32[2,24]{1,0:T(2,128)S(1)} collective-permute-done((f32[2,24]{1,0:T(2,128)S(1)}, f32[2,24]{1,0:T(2,128)S(1)}, u32[]{:S(2)}, u32[]{:S(2)}) %collective-permute-start.1) | collective-permute-done | bytes 224 | tf_op jit(solution)/shard_map/ppermute | solution.py:109
  174.6 0.1 fusion.24
  174.7 0.2 reduce_window_sum.11
  174.9 0.1 select_reduce_fusion.1
  175.0 0.1 reduce_sum.25
  175.1 0.7 iota_reduce_fusion
  177.1 0.7 not_reduce_fusion
  179.3 0.1 reduce_sum.29
  179.3 0.1 select_reduce_fusion
  179.4 0.1 reshape.383
  179.5 13.5 %collective-permute-done.3 = bf16[1024,512]{1,0:T(8,128)(2,1)} collective-permute-done((bf16[1024,512]{1,0:T(8,128)(2,1)S(1)}, bf16[1024,512]{1,0:T(8,128)(2,1)}, u32[]{:S(2)}, u32[]{:S(2)}) %collective-permute-start.3) | collective-permute-done | bytes 1048608 | tf_op jit(solution)/shard_map/ppermute | solution.py:106
  193.0 2.8 %pad_maximum_fusion.1 = bf16[2,1024,512]{2,1,0:T(8,128)(2,1)} fusion(bf16[1,1024,512]{2,1,0:T(8,128)(2,1)} %bitcast.16, bf16[1,1024,512]{2,1,0:T(8,128)(2,1)S(1)} %copy-done.3), kind=kLoop, calls=%fused_computation.7 | loop fusion | flops 1048576 | bytes 4194304 | tf_op jit(solution)/shard_map/stack | solution.py:108
  195.8 1.1 collective-permute-start.4
  197.0 0.1 reshape.410
  197.1 0.1 maximum_reduce_fusion.1
  197.3 0.7 gather_fusion
  197.9 0.1 maximum_reduce_fusion
  198.1 0.7 gather_fusion.1
  200.1 0.7 gather_fusion.3
  200.7 0.7 fusion.25
  201.4 0.6 pad_maximum_fusion.5.scalars_ref
  202.0 0.1 compare_reduce_fusion.1
  202.1 0.1 compare_reduce_fusion
  202.3 1.3 broadcast_select_fusion.1
  203.6 0.6 pad_add_fusion.tiles_ref
  204.2 0.0 collective-permute-done.4
  204.2 3.5 %pad_maximum_fusion.right_ref = bf16[4,1024,512]{2,1,0:T(8,128)(2,1)} fusion(bf16[2,1024,512]{2,1,0:T(8,128)(2,1)} %collective-permute-done.4, bf16[1,1024,512]{2,1,0:T(8,128)(2,1)} %bitcast.16, bf16[1,1024,512]{2,1,0:T(8,128)(2,1)S(1)} %copy-done.3), kind=kLoop, calls=%fused_computation.6 | loop fusion | flops 4194304 | bytes 8388608 | tf_op jit(solution)/shard_map/stack | solution.py:110
  207.7 0.0 collective-permute-done.2.theirs_ref
  207.7 21.4 %shard_map.73 = f32[512,512]{1,0:T(8,128)} custom-call(s32[48]{0:T(128)} %pad_add_fusion.tiles_ref, f32[48]{0:T(128)} %pad_maximum_fusion.5.scalars_ref, bf16[6,512,1024]{2,1,0:T(8,128)(2,1)} %all-reduce.2.cloned.1.call-done.mine_ref, bf16[6,512,1024]{2,1,0:T(8,128)(2,1)} %collective-permute-done.2.theirs_ref, ...), custom_call_target="tpu_custom_call" | custom-call | tf_op jit(solution)/shard_map/pallas_call | solution.py:70
  229.1 3.3 %fusion.19 = f32[512,512]{1,0:T(8,128)S(1)} fusion(f32[512,512]{1,0:T(8,128)} %shard_map.73, f32[512,512]{1,0:T(8,128)S(1)} %copy-done.2, f32[512,512]{0,1:T(8,128)S(1)} %copy.32, f32[512]{0:T(512)S(1)} %copy-done.4), kind=kOutput, calls=%fused_computation.90 | convolution fusion | flops 1611923456 | bytes 4196352 | tf_op jit(solution)/shard_map/dot_general | solution.py:143
  232.4 0.0 copy-done.1
  232.4 2.9 %fusion = f32[1,512,512]{2,1,0:T(8,128)} fusion(f32[512,512]{1,0:T(8,128)S(1)} %fusion.19, f32[512,512]{1,0:T(8,128)S(1)} %copy-done.1, f32[512,512]{1,0:T(8,128)S(1)} %copy-done.2, f32[512,512]{0,1:T(8,128)S(1)} %copy.32, f32[512]{0:T(512)S(1)} %copy-done.4), kind=kOutput, calls=%fused_computation.9 | convolution fusion | flops 1612185600 | bytes 5244928 | tf_op jit(solution)/shard_map/dot_general | solution.py:142
  (25 shorter events, 0.2 us)
Async XLA Ops:
  6.5 161.1 %copy-start = (f32[128]{0:T(128)S(1)}, f32[128]{0:T(128)}, u32[]{:S(2)}) copy-start(f32[128]{0:T(128)} %param.8) | copy-start | bytes 1540
  6.5 156.5 %all-reduce.2.cloned.1.call-start = ((), (), s32[]{:S(2)}) async-start(), calls=%async_computation | async-start | bytes 12582912 | tf_op jit(solution)/shard_map/psum | solution.py:100
  12.2 152.3 %copy-start.5 = (s32[12,1]{0,1:T(1,128)S(1)}, s32[12,1]{0,1:T(1,128)}, u32[]{:S(2)}) copy-start(s32[12,1]{0,1:T(1,128)} %param.12) | copy-start | bytes 148
  12.2 152.3 %copy-start.6 = (f32[12]{0:T(128)S(1)}, f32[12]{0:T(128)}, u32[]{:S(2)}) copy-start(f32[12]{0:T(128)} %param.13) | copy-start | bytes 148
  12.2 154.8 %copy-start.3 = (bf16[1,1024,512]{2,1,0:T(8,128)(2,1)S(1)}, bf16[1,1024,512]{2,1,0:T(8,128)(2,1)}, u32[]{:S(2)}) copy-start(bf16[1,1024,512]{2,1,0:T(8,128)(2,1)} %param.7) | copy-start | bytes 3145732
  12.2 156.3 %copy-start.4 = (f32[512]{0:T(512)S(1)}, f32[512]{0:T(512)}, u32[]{:S(2)}) copy-start(f32[512]{0:T(512)} %param.9) | copy-start | bytes 6148
  12.2 158.9 %copy-start.2 = (f32[512,512]{1,0:T(8,128)S(1)}, f32[512,512]{1,0:T(8,128)}, u32[]{:S(2)}) copy-start(f32[512,512]{1,0:T(8,128)} %param.10) | copy-start | bytes 3145732
  163.0 44.7 %collective-permute-start.2 = (bf16[6,512,1024]{2,1,0:T(8,128)(2,1)}, bf16[6,512,1024]{2,1,0:T(8,128)(2,1)}, u32[]{:S(2)}, u32[]{:S(2)}) collective-permute-start(bf16[6,512,1024]{2,1,0:T(8,128)(2,1)} %all-reduce.2.cloned.1.call-done.mine_ref), channel_id=1, source_target_pairs={{0,32},{32,0},{1,33},{33,1},{2,34},{34,2},{3,35},{35,3},{4,36},{36... | collective-permute-start | bytes 18874376 | tf_op jit(solution)/shard_map/ppermute | solution.py:101
  164.5 5.7 %collective-permute-start = (f32[24]{0:T(128)S(1)}, f32[24]{0:T(128)S(1)}, u32[]{:S(2)}, u32[]{:S(2)}) collective-permute-start(f32[24]{0:T(128)S(1)} %pad_maximum_fusion.4), channel_id=1, source_target_pairs={{0,64},{64,0},{1,65},{65,1},{2,66},{66,2},{3,67},{67,3},{4,68},{68... | collective-permute-start | bytes 296 | tf_op jit(solution)/shard_map/ppermute | solution.py:107
  167.0 26.0 %collective-permute-start.3 = (bf16[1024,512]{1,0:T(8,128)(2,1)S(1)}, bf16[1024,512]{1,0:T(8,128)(2,1)}, u32[]{:S(2)}, u32[]{:S(2)}) collective-permute-start(bf16[1024,512]{1,0:T(8,128)(2,1)S(1)} %bitcast.41), channel_id=1, source_target_pairs={{0,64},{64,0},{1,65},{65,1},{2,66},{66,2},{3,67},{67,3},{4,68},{68... | collective-permute-start | bytes 3145736 | tf_op jit(solution)/shard_map/ppermute | solution.py:106
  170.2 4.3 %collective-permute-start.1 = (f32[2,24]{1,0:T(2,128)S(1)}, f32[2,24]{1,0:T(2,128)S(1)}, u32[]{:S(2)}, u32[]{:S(2)}) collective-permute-start(f32[2,24]{1,0:T(2,128)S(1)} %pad_maximum_fusion.3), channel_id=1, source_target_pairs={{0,32},{32,0},{1,33},{33,1},{2,34},{34,2},{3,35},{35,3},{4,36},{36... | collective-permute-start | bytes 584 | tf_op jit(solution)/shard_map/ppermute | solution.py:109
  195.8 8.4 %collective-permute-start.4 = (bf16[2,1024,512]{2,1,0:T(8,128)(2,1)}, bf16[2,1024,512]{2,1,0:T(8,128)(2,1)}, u32[]{:S(2)}, u32[]{:S(2)}) collective-permute-start(bf16[2,1024,512]{2,1,0:T(8,128)(2,1)} %pad_maximum_fusion.1), channel_id=1, source_target_pairs={{0,32},{32,0},{1,33},{33,1},{2,34},{34,2},{3,35},{35,3},{4,36},{36... | collective-permute-start | bytes 6291464 | tf_op jit(solution)/shard_map/ppermute | solution.py:108
  229.1 3.3 %copy-start.1 = (f32[512,512]{1,0:T(8,128)S(1)}, f32[512,512]{1,0:T(8,128)}, u32[]{:S(2)}) copy-start(f32[512,512]{1,0:T(8,128)} %shard_map.73) | copy-start | bytes 3145732
Sparse Core Ops, SparseCore 0:
  12.3 150.6 all-reduce.1

commit v10 on v5

--- a/solution.py
+++ b/solution.py
@@ -9,30 +9,31 @@
 CAP = 4
 
 
-def slot_kernel(tiles_ref, scalars_ref, mine_ref, theirs_ref, right_ref, pair_ref, out_ref):
+def slot_kernel(tiles_ref, scalars_ref, *refs):
+    *lefts, right_ref, pair_ref, out_ref = refs
     step = pl.program_id(0)
-    slots = pl.num_programs(0)
+    steps = pl.num_programs(0)
+    streams = len(lefts) // 2
+    slots = streams * steps
+    total = None
+    for stream in range(streams):
+        slot = streams * step + stream
+        mine_ref, theirs_ref = lefts[2 * stream], lefts[2 * stream + 1]
+        from_theirs = tiles_ref[3 * stream * steps + step] != 0
+        left = jnp.where(from_theirs, theirs_ref[...], mine_ref[...])
+        integral = jnp.dot(left, right_ref[...], preferred_element_type=jnp.float32)
+        denominator = (pair_ref[...] - scalars_ref[slot]) - scalars_ref[slots + slot]
+        scaled = (integral / denominator) * scalars_ref[2 * slots + slot]
+        amplitude = scaled.astype(jnp.bfloat16).astype(jnp.float32)
+        total = amplitude if total is None else total + amplitude
 
-    def accumulate(left_ref):
-        integral = jnp.dot(left_ref[...], right_ref[...], preferred_element_type=jnp.float32)
-        denominator = (pair_ref[...] - scalars_ref[step]) - scalars_ref[slots + step]
-        amplitude = ((integral / denominator) * scalars_ref[2 * slots + step]).astype(jnp.bfloat16)
+    @pl.when(step == 0)
+    def _():
+        out_ref[...] = total
 
-        @pl.when(step == 0)
-        def _():
-            out_ref[...] = amplitude.astype(jnp.float32)
-
-        @pl.when(step > 0)
-        def _():
-            out_ref[...] += amplitude.astype(jnp.float32)
-
-    @pl.when(tiles_ref[step] == 0)
+    @pl.when(step > 0)
     def _():
-        accumulate(mine_ref)
-
-    @pl.when(tiles_ref[step] != 0)
-    def _():
-        accumulate(theirs_ref)
+        out_ref[...] += total
 
 
 def held_index(present, local):
@@ -44,35 +45,44 @@
 
 def summed_tiles(position, scalars, mine, theirs, column, pair_sum):
     slots = position.shape[0]
+    streams = 4
+    steps = slots // streams
     per_source = slots // column.shape[0]
     half, rows, depth = mine.shape
-    in_theirs = position >= half
-    local = position % half
-    tables = jnp.concatenate(
-        [
+    parts = []
+    for stream in range(streams):
+        picked = position[stream::streams]
+        in_theirs = picked >= half
+        local = picked % half
+        parts += [
             in_theirs.astype(jnp.int32),
             held_index(~in_theirs, local),
             held_index(in_theirs, local),
         ]
-    )
+    tables = jnp.concatenate(parts)
+
+    def left_spec(stream, kind):
+        offset = (3 * stream + kind) * steps
+        return pl.BlockSpec((None, rows, depth), lambda p, tiles: (tiles[offset + p], 0, 0))
+
     grid_spec = pltpu.PrefetchScalarGridSpec(
         num_scalar_prefetch=1,
-        grid=(slots,),
-        in_specs=[
-            pl.BlockSpec(memory_space=pltpu.SMEM),
-            pl.BlockSpec((None, rows, depth), lambda s, tiles: (tiles[slots + s], 0, 0)),
-            pl.BlockSpec((None, rows, depth), lambda s, tiles: (tiles[2 * slots + s], 0, 0)),
-            pl.BlockSpec((None, depth, rows), lambda s, tiles: (s // per_source, 0, 0)),
-            pl.BlockSpec((rows, rows), lambda s, tiles: (0, 0)),
+        grid=(steps,),
+        in_specs=[pl.BlockSpec(memory_space=pltpu.SMEM)]
+        + [left_spec(stream, kind) for stream in range(streams) for kind in (1, 2)]
+        + [
+            pl.BlockSpec((None, depth, rows), lambda p, tiles: (p * streams // per_source, 0, 0)),
+            pl.BlockSpec((rows, rows), lambda p, tiles: (0, 0)),
         ],
-        out_specs=pl.BlockSpec((rows, rows), lambda s, tiles: (0, 0)),
+        out_specs=pl.BlockSpec((rows, rows), lambda p, tiles: (0, 0)),
     )
+    lefts = [mine, theirs] * streams
     return pl.pallas_call(
         slot_kernel,
         grid_spec=grid_spec,
         out_shape=jax.ShapeDtypeStruct((rows, rows), jnp.float32),
         compiler_params=pltpu.CompilerParams(dimension_semantics=("arbitrary",)),
-    )(tables, scalars, mine, theirs, column, pair_sum)
+    )(tables, scalars, *lefts, column, pair_sum)
 
 
 def layer(df_panels, occ_energy, virt_energy, fock_off, i_plan, pair_owner, pair_weight):

time: 241 us -> 245 us (1.017)
  waiting for transfers between devices: 168 us -> 144 us
  between operations: 17.5 us -> 29.4 us
  other arithmetic: 16.6 us -> 25.2 us
  local copies, waits for them, and re-layouts: 6.67 us -> 14 us
    ppermute x1, waiting for transfers between devices: 13.5 us -> 0.01 us  [layer(): far_panel = lax.ppermute(own_panel, 'zh', across)]
    psum x1, waiting for transfers between devices: 151 us -> 144 us  [layer(): own_half = lax.psum(masked, ('zh', 'orb'))]
    another operation x2 -> x8, other arithmetic: 1.45 us -> 5.73 us  [held_index(): first = jnp.argmax(present)]
    select_n x1 -> x4, other arithmetic: 1.33 us -> 5.25 us  [held_index(): return jnp.where(last >= 0, local[jnp.maximum(last, 0)], local[first])]
    gather x2 -> x8, local copies, waits for them, and re-layouts: 1.32 us -> 5.12 us  [held_index(): return jnp.where(last >= 0, local[jnp.maximum(last, 0)], local[first])]
    ppermute x1, waiting for transfers between devices: 3.2 us -> 0.32 us  [layer(): near_meta = lax.ppermute(jnp.stack([meta, far_meta]), 'core', beside)]
  transfers between devices with their start and end apart: 6 -> 6, of which waited for: 3 -> 2; matrix products, arithmetic and copies ran while one was open for 7% -> 13% of each run, Pallas kernels for 0% -> 0%
where the time goes in v10:
time: 245 us
  waiting for transfers between devices  144 us (59%)
  between operations  29.4 us (12%)
  other arithmetic  25.2 us (10%)
  Pallas kernels  18.5 us (8%)
  local copies, waits for them, and re-layouts  14 us (6%)
  starting transfers between devices  7.41 us (3%)
  matrix products  6.23 us (3%)
    psum x1, waiting for transfers between devices, layer(): own_half = lax.psum(masked, ('zh', 'orb'))  144 us
    pallas_call x1, Pallas kernels, summed_tiles(): pl.pallas_call(slot_kernel, grid_spec=grid_spec, out_shape=jax.ShapeDtype...  18.5 us
    another operation x8, other arithmetic, held_index(): first = jnp.argmax(present)  5.73 us
    select_n x4, other arithmetic, held_index(): return jnp.where(last >= 0, local[jnp.maximum(last, 0)], local[first])  5.25 us
    gather x8, local copies, waits for them, and re-layouts, held_index(): return jnp.where(last >= 0, local[jnp.maximum(last, 0)], local[first])  5.12 us
  transfers between devices with their start and end apart: 6, of which 2 were waited for; matrix products, arithmetic and copies ran while one was open for 13% of the time, Pallas kernels for 0%

profile of v10, /device:TPU:1, one launch (start us, length us, event | category | flops | bytes accessed | tf_op | source)
XLA Modules:
  0.0 244.8 jit_solution(17138967150487707172)
XLA Ops:
  6.5 0.7 broadcast_add_fusion.1
  7.2 0.1 copy.21
  7.3 0.1 copy.23
  7.5 0.1 eq.70
  7.5 1.5 copy.24
  9.0 3.1 %broadcast_select_fusion = bf16[6,512,1024]{2,1,0:T(8,128)(2,1)} fusion(pred[6]{0:T(512)(128)(4,1)S(1)} %eq.70, bf16[512,1024]{1,0:T(8,128)(2,1)S(1)} %copy.24), kind=kLoop, calls=%fused_computation.11 | loop fusion | flops 3145728 | bytes 7340038 | tf_op jit(solution)/shard_map/jit(_where)/select_n | solution.py:107
  12.2 0.6 copy-done.5
  12.9 4.4 %collective-permute-start = (f32[24]{0:T(128)S(1)}, f32[24]{0:T(128)S(1)}, u32[]{:S(2)}, u32[]{:S(2)}) collective-permute-start(f32[24]{0:T(128)S(1)} %pad_maximum_fusion.4), channel_id=1, source_target_pairs={{0,64},{64,0},{1,65},{65,1},{2,66},{66,2},{3,67},{67,3},{4,68},{68... | collective-permute-start | bytes 296 | tf_op jit(solution)/shard_map/ppermute | solution.py:117
  17.3 0.5 collective-permute-start.3
  17.9 0.7 gather_fusion.8
  18.8 1.1 broadcast_add_fusion.refs_9_
  19.9 0.6 gather_fusion.10
  20.6 1.0 collective-permute-start.1
  21.7 0.3 copy.20
  22.1 0.3 collective-permute-done.1
  22.5 0.2 reduce_window_sum.11
  22.7 0.1 select_reduce_fusion.1
  23.0 0.1 slice.28
  23.1 0.1 slice.27
  23.1 0.1 slice.26
  23.2 0.1 slice.25
  23.3 0.7 iota_reduce_fusion.3
  25.3 0.7 not_reduce_fusion.3
  27.5 0.7 iota_reduce_fusion.2
  29.4 0.7 not_reduce_fusion.2
  31.5 0.7 iota_reduce_fusion.1
  33.6 0.7 not_reduce_fusion.1
  35.6 143.8 %all-reduce.2.cloned.1.call-done.refs_0_.refs_2_.refs_4_.refs_6_ = bf16[6,512,1024]{2,1,0:T(8,128)(2,1)} async-done(((bf16[6,512,1024]{2,1,0:T(8,128)(2,1)}), bf16[6,512,1024]{2,1,0:T(8,128)(2,1)}) %all-reduce.2.cloned.1.call-update) | async-done | bytes 6291472 | tf_op jit(solution)/shard_map/psum | solution.py:110
  179.4 1.4 collective-permute-start.2
  180.8 0.7 iota_reduce_fusion
  182.9 0.7 not_reduce_fusion
  184.9 0.1 select_reduce_fusion
  185.1 0.2 reduce-window.29
  185.3 0.2 reduce-window.26
  185.5 0.2 reduce-window.31
  185.7 0.2 reduce-window.30
  185.9 0.2 reduce-window.35
  186.1 0.2 reduce-window.34
  186.2 0.2 reduce-window.39
  186.4 0.2 reduce-window.36
  186.6 0.6 gather_fusion.7
  187.3 0.6 gather_fusion.6
  187.9 0.6 gather_fusion.5
  188.6 0.6 gather_fusion.4
  189.2 0.6 gather_fusion.3
  189.9 2.8 %pad_maximum_fusion.1 = bf16[2,1024,512]{2,1,0:T(8,128)(2,1)} fusion(bf16[1,1024,512]{2,1,0:T(8,128)(2,1)} %bitcast.46, bf16[1,1024,512]{2,1,0:T(8,128)(2,1)S(1)} %copy-done.2), kind=kLoop, calls=%fused_computation.13 | loop fusion | flops 1048576 | bytes 4194304 | tf_op jit(solution)/shard_map/stack | solution.py:118
  192.7 0.6 gather_fusion.2
  193.3 0.6 gather_fusion.1
  194.0 0.6 gather_fusion
  199.9 0.7 gather_fusion.9
  200.5 0.7 fusion.20
  201.2 0.7 fusion.19
  201.9 0.7 fusion.18
  202.5 0.7 fusion.17
  203.2 1.3 bitcast_select_fusion
  204.5 1.3 bitcast_select_fusion.2
  205.8 1.3 bitcast_select_fusion.4
  207.2 1.3 bitcast_select_fusion.6
  208.5 0.6 concatenate.17.tiles_ref
  209.1 0.6 pad_maximum_fusion.5.scalars_ref
  209.7 3.5 %pad_maximum_fusion.refs_8_ = bf16[4,1024,512]{2,1,0:T(8,128)(2,1)} fusion(bf16[2,1024,512]{2,1,0:T(8,128)(2,1)} %collective-permute-done.4, bf16[1,1024,512]{2,1,0:T(8,128)(2,1)} %bitcast.46, bf16[1,1024,512]{2,1,0:T(8,128)(2,1)S(1)} %copy-done.2), kind=kLoop, calls=%fused_computation.12 | loop fusion | flops 4194304 | bytes 8388608 | tf_op jit(solution)/shard_map/stack | solution.py:120
  213.2 18.5 %shard_map.73 = f32[512,512]{1,0:T(8,128)} custom-call(s32[48]{0:T(128)} %concatenate.17.tiles_ref, f32[48]{0:T(128)} %pad_maximum_fusion.5.scalars_ref, bf16[6,512,1024]{2,1,0:T(8,128)(2,1)} %all-reduce.2.cloned.1.call-done.refs_0_.refs_2_.refs_4_.refs_6_, bf16[6,512,1024]{2,1,0:T(8,128)(2,1)} %collective-permute-done.2.refs_1_.refs_3_.refs_5_.refs_7_, ...), custom_call_target="tpu_custom_call" | custom-call | tf_op jit(solution)/shard_map/pallas_call | solution.py:80
  231.7 3.3 %fusion.13 = f32[512,512]{1,0:T(8,128)S(1)} fusion(f32[512,512]{1,0:T(8,128)} %shard_map.73, f32[512,512]{1,0:T(8,128)S(1)} %copy-done.1, f32[512,512]{0,1:T(8,128)S(1)} %copy.20, f32[512]{0:T(512)S(1)} %copy-done.4), kind=kOutput, calls=%fused_computation.111 | convolution fusion | flops 1611923456 | bytes 4196352 | tf_op jit(solution)/shard_map/dot_general | solution.py:153
  235.0 2.9 %fusion = f32[1,512,512]{2,1,0:T(8,128)} fusion(f32[512,512]{1,0:T(8,128)S(1)} %fusion.13, f32[512,512]{1,0:T(8,128)S(1)} %copy-done.3, f32[512,512]{1,0:T(8,128)S(1)} %copy-done.1, f32[512,512]{0,1:T(8,128)S(1)} %copy.20, f32[512]{0:T(512)S(1)} %copy-done.4), kind=kOutput, calls=%fused_computation.15 | convolution fusion | flops 1612185600 | bytes 5244928 | tf_op jit(solution)/shard_map/dot_general | solution.py:152
  (65 shorter events, 1.1 us)
Async XLA Ops:
  6.5 11.4 %copy-start = (f32[128]{0:T(128)S(1)}, f32[128]{0:T(128)}, u32[]{:S(2)}) copy-start(f32[128]{0:T(128)} %param.8) | copy-start | bytes 1540
  6.5 172.8 %all-reduce.2.cloned.1.call-start = ((), (), s32[]{:S(2)}) async-start(), calls=%async_computation | async-start | bytes 12582912 | tf_op jit(solution)/shard_map/psum | solution.py:110
  12.2 0.7 copy-start.5
  12.2 0.7 copy-start.6
  12.2 5.2 %copy-start.2 = (bf16[1,1024,512]{2,1,0:T(8,128)(2,1)S(1)}, bf16[1,1024,512]{2,1,0:T(8,128)(2,1)}, u32[]{:S(2)}) copy-start(bf16[1,1024,512]{2,1,0:T(8,128)(2,1)} %param.7) | copy-start | bytes 3145732
  12.2 6.6 %copy-start.4 = (f32[512]{0:T(512)S(1)}, f32[512]{0:T(512)}, u32[]{:S(2)}) copy-start(f32[512]{0:T(512)} %param.9) | copy-start | bytes 6148
  12.2 9.6 %copy-start.1 = (f32[512,512]{1,0:T(8,128)S(1)}, f32[512,512]{1,0:T(8,128)}, u32[]{:S(2)}) copy-start(f32[512,512]{1,0:T(8,128)} %param.10) | copy-start | bytes 3145732
  12.9 7.6 %collective-permute-start = (f32[24]{0:T(128)S(1)}, f32[24]{0:T(128)S(1)}, u32[]{:S(2)}, u32[]{:S(2)}) collective-permute-start(f32[24]{0:T(128)S(1)} %pad_maximum_fusion.4), channel_id=1, source_target_pairs={{0,64},{64,0},{1,65},{65,1},{2,66},{66,2},{3,67},{67,3},{4,68},{68... | collective-permute-start | bytes 296 | tf_op jit(solution)/shard_map/ppermute | solution.py:117
  17.3 172.5 %collective-permute-start.3 = (bf16[1024,512]{1,0:T(8,128)(2,1)S(1)}, bf16[1024,512]{1,0:T(8,128)(2,1)}, u32[]{:S(2)}, u32[]{:S(2)}) collective-permute-start(bf16[1024,512]{1,0:T(8,128)(2,1)S(1)} %bitcast.95), channel_id=1, source_target_pairs={{0,64},{64,0},{1,65},{65,1},{2,66},{66,2},{3,67},{67,3},{4,68},{68... | collective-permute-start | bytes 3145736 | tf_op jit(solution)/shard_map/ppermute | solution.py:116
  20.6 1.9 collective-permute-start.1
  179.4 33.8 %collective-permute-start.2 = (bf16[6,512,1024]{2,1,0:T(8,128)(2,1)}, bf16[6,512,1024]{2,1,0:T(8,128)(2,1)}, u32[]{:S(2)}, u32[]{:S(2)}) collective-permute-start(bf16[6,512,1024]{2,1,0:T(8,128)(2,1)} %all-reduce.2.cloned.1.call-done.refs_0_.refs_2_.refs_4_.refs_6_), channel_id=1, source_target_pairs={{0,32},{32,0},{1,33},{33,1},{2,34},{34,2},{3,35},{35,3},{4,36},{36... | collective-permute-start | bytes 18874376 | tf_op jit(solution)/shard_map/ppermute | solution.py:111
  192.7 17.0 %collective-permute-start.4 = (bf16[2,1024,512]{2,1,0:T(8,128)(2,1)}, bf16[2,1024,512]{2,1,0:T(8,128)(2,1)}, u32[]{:S(2)}, u32[]{:S(2)}) collective-permute-start(bf16[2,1024,512]{2,1,0:T(8,128)(2,1)} %pad_maximum_fusion.1), channel_id=1, source_target_pairs={{0,32},{32,0},{1,33},{33,1},{2,34},{34,2},{3,35},{35,3},{4,36},{36... | collective-permute-start | bytes 6291464 | tf_op jit(solution)/shard_map/ppermute | solution.py:118
  231.7 3.3 %copy-start.3 = (f32[512,512]{1,0:T(8,128)S(1)}, f32[512,512]{1,0:T(8,128)}, u32[]{:S(2)}) copy-start(f32[512,512]{1,0:T(8,128)} %shard_map.73) | copy-start | bytes 3145732
Sparse Core Ops, SparseCore 0:
  12.3 166.9 all-reduce.1

commit v11 on v10

--- a/solution.py
+++ b/solution.py
@@ -45,7 +45,7 @@
 
 def summed_tiles(position, scalars, mine, theirs, column, pair_sum):
     slots = position.shape[0]
-    streams = 4
+    streams = 2
     steps = slots // streams
     per_source = slots // column.shape[0]
     half, rows, depth = mine.shape
@@ -86,7 +86,6 @@
 
 
 def layer(df_panels, occ_energy, virt_energy, fock_off, i_plan, pair_owner, pair_weight):
-    highest = lax.Precision.HIGHEST
     halves = lax.axis_size("zh")
     cores = lax.axis_size("core")
     group_count = halves * cores
@@ -149,8 +148,19 @@
     summed = summed_tiles(position.reshape(-1), scalars, own_half, other_half, column, pair_sum)
 
     fock_matrix = jnp.diag(virt_energy) + 0.5 * (fock_off + fock_off.T)
-    left = jnp.dot(fock_matrix, summed, precision=highest)
-    right = jnp.dot(summed, fock_matrix, precision=highest)
+
+    def split(value):
+        high = value.astype(jnp.bfloat16)
+        return high, (value - high.astype(jnp.float32)).astype(jnp.bfloat16)
+
+    fock_high, fock_low = split(fock_matrix)
+    sum_high, sum_low = split(summed)
+
+    def product(a, b):
+        return jnp.dot(a, b, preferred_element_type=jnp.float32)
+
+    left = product(fock_high, sum_high) + (product(fock_high, sum_low) + product(fock_low, sum_high))
+    right = product(sum_high, fock_high) + (product(sum_high, fock_low) + product(sum_low, fock_high))
     return (left + right)[None]
 
 

time: 245 us -> 250 us (1.020)
  waiting for transfers between devices: 144 us -> 166 us
  between operations: 29.4 us -> 21.6 us
  other arithmetic: 25.2 us -> 20.2 us
  local copies, waits for them, and re-layouts: 14 us -> 10.9 us
    psum x1, waiting for transfers between devices: 144 us -> 162 us  [layer(): own_half = lax.psum(masked, ('zh', 'orb'))]
    ppermute x1, waiting for transfers between devices: 0.32 us -> 4.55 us  [layer(): near_meta = lax.ppermute(jnp.stack([meta, far_meta]), 'core', beside)]
    another operation x8 -> x4, other arithmetic: 5.73 us -> 2.87 us  [held_index(): first = jnp.argmax(present)]
    select_n x4 -> x2, other arithmetic: 5.25 us -> 2.64 us  [held_index(): return jnp.where(last >= 0, local[jnp.maximum(last, 0)], local[first])]
    gather x8 -> x4, local copies, waits for them, and re-layouts: 5.12 us -> 2.57 us  [held_index(): return jnp.where(last >= 0, local[jnp.maximum(last, 0)], local[first])]
    dot_general x2 -> x6, matrix products: 6.23 us -> 6.57 us  [product(): return jnp.dot(a, b, preferred_element_type=jnp.float32)]
  transfers between devices with their start and end apart: 6 -> 6, of which waited for: 2 -> 2; matrix products, arithmetic and copies ran while one was open for 13% -> 10% of each run, Pallas kernels for 0% -> 0%
where the time goes in v11:
time: 250 us
  waiting for transfers between devices  166 us (66%)
  between operations  21.6 us (9%)
  other arithmetic  20.2 us (8%)
  Pallas kernels  17.4 us (7%)
  local copies, waits for them, and re-layouts  10.9 us (4%)
  starting transfers between devices  6.83 us (3%)
  matrix products  6.57 us (3%)
    psum x1, waiting for transfers between devices, layer(): own_half = lax.psum(masked, ('zh', 'orb'))  162 us
    pallas_call x1, Pallas kernels, summed_tiles(): pl.pallas_call(slot_kernel, grid_spec=grid_spec, out_shape=jax.ShapeDtype...  17.4 us
    dot_general x6, matrix products, product(): return jnp.dot(a, b, preferred_element_type=jnp.float32)  6.57 us
  transfers between devices with their start and end apart: 6, of which 2 were waited for; matrix products, arithmetic and copies ran while one was open for 10% of the time, Pallas kernels for 0%

profile of v11, /device:TPU:1, one launch (start us, length us, event | category | flops | bytes accessed | tf_op | source)
XLA Modules:
  0.0 249.6 jit_solution(15479430100929346628)
XLA Ops:
  6.5 0.7 broadcast_add_fusion.1
  7.2 0.1 copy.21
  7.3 0.1 copy.23
  7.5 0.1 eq.64
  7.5 1.5 copy.24
  9.0 3.1 %broadcast_select_fusion = bf16[6,512,1024]{2,1,0:T(8,128)(2,1)} fusion(pred[6]{0:T(512)(128)(4,1)S(1)} %eq.64, bf16[512,1024]{1,0:T(8,128)(2,1)S(1)} %copy.24), kind=kLoop, calls=%fused_computation.7 | loop fusion | flops 3145728 | bytes 7340038 | tf_op jit(solution)/shard_map/jit(_where)/select_n | solution.py:106
  12.2 0.0 copy-start.4
  12.2 0.0 all-reduce.2.cloned.1.call-update
  12.2 0.6 copy-done.5
  12.8 0.0 copy-done.6
  12.8 0.1 pad_maximum_fusion.4
  12.9 4.4 %collective-permute-start = (f32[24]{0:T(128)S(1)}, f32[24]{0:T(128)S(1)}, u32[]{:S(2)}, u32[]{:S(2)}) collective-permute-start(f32[24]{0:T(128)S(1)} %pad_maximum_fusion.4), channel_id=1, source_target_pairs={{0,64},{64,0},{1,65},{65,1},{2,66},{66,2},{3,67},{67,3},{4,68},{68... | collective-permute-start | bytes 296 | tf_op jit(solution)/shard_map/ppermute | solution.py:116
  17.3 0.5 collective-permute-start.3
  17.8 161.5 %all-reduce.2.cloned.1.call-done.refs_0_.refs_2_ = bf16[6,512,1024]{2,1,0:T(8,128)(2,1)} async-done(((bf16[6,512,1024]{2,1,0:T(8,128)(2,1)}), bf16[6,512,1024]{2,1,0:T(8,128)(2,1)}) %all-reduce.2.cloned.1.call-update) | async-done | bytes 6291472 | tf_op jit(solution)/shard_map/psum | solution.py:109
  179.4 1.4 collective-permute-start.2
  180.8 0.1 fusion.31
  180.9 0.1 reshape.205
  181.0 1.3 copy.20
  182.3 0.1 fusion.8
  182.4 2.4 subtract_convert_fusion
  184.9 0.7 gather_fusion.4
  185.5 0.1 collective-permute-start.1
  185.6 0.6 gather_fusion.6
  186.3 0.1 broadcast_in_dim.116
  186.3 0.1 reshape.207
  186.4 4.5 %collective-permute-done.1 = f32[2,24]{1,0:T(2,128)S(1)} collective-permute-done((f32[2,24]{1,0:T(2,128)S(1)}, f32[2,24]{1,0:T(2,128)S(1)}, u32[]{:S(2)}, u32[]{:S(2)}) %collective-permute-start.1) | collective-permute-done | bytes 224 | tf_op jit(solution)/shard_map/ppermute | solution.py:118
  191.0 0.1 fusion.22
  191.1 0.2 reduce_window_sum.11
  191.3 0.1 select_reduce_fusion.1
  191.4 0.1 reduce_sum.23
  191.5 0.1 slice.20
  191.6 0.1 slice.19
  191.7 0.7 iota_reduce_fusion.1
  193.7 0.7 not_reduce_fusion.1
  195.8 0.7 iota_reduce_fusion
  197.8 0.7 not_reduce_fusion
  199.9 0.2 reduce-window.19
  200.1 2.8 %pad_maximum_fusion.1 = bf16[2,1024,512]{2,1,0:T(8,128)(2,1)} fusion(bf16[1,1024,512]{2,1,0:T(8,128)(2,1)} %bitcast.30, bf16[1,1024,512]{2,1,0:T(8,128)(2,1)S(1)} %copy-done.2), kind=kLoop, calls=%fused_computation.9 | loop fusion | flops 1048576 | bytes 4194304 | tf_op jit(solution)/shard_map/stack | solution.py:117
  202.9 0.4 collective-permute-start.4
  203.3 0.1 select_reduce_fusion
  203.4 0.1 reshape.208
  203.5 0.1 reshape.251
  203.5 0.2 reduce-window.15
  203.7 0.2 reduce-window.14
  203.9 0.2 reduce-window.16
  204.1 0.6 gather_fusion.3
  204.8 0.6 gather_fusion.2
  205.4 0.6 gather_fusion.1
  206.1 0.6 gather_fusion
  209.4 0.7 gather_fusion.5
  210.0 0.7 fusion.24
  210.7 0.7 fusion.23
  211.4 1.3 bitcast_select_fusion
  212.7 1.3 bitcast_select_fusion.2
  214.1 0.6 concatenate.17.tiles_ref
  214.7 0.6 pad_maximum_fusion.5.scalars_ref
  215.2 3.5 %pad_maximum_fusion.refs_4_ = bf16[4,1024,512]{2,1,0:T(8,128)(2,1)} fusion(bf16[2,1024,512]{2,1,0:T(8,128)(2,1)} %collective-permute-done.4, bf16[1,1024,512]{2,1,0:T(8,128)(2,1)} %bitcast.30, bf16[1,1024,512]{2,1,0:T(8,128)(2,1)S(1)} %copy-done.2), kind=kLoop, calls=%fused_computation.8 | loop fusion | flops 4194304 | bytes 8388608 | tf_op jit(solution)/shard_map/stack | solution.py:119
  218.7 17.4 %shard_map.73 = f32[512,512]{1,0:T(8,128)} custom-call(s32[48]{0:T(128)} %concatenate.17.tiles_ref, f32[48]{0:T(128)} %pad_maximum_fusion.5.scalars_ref, bf16[6,512,1024]{2,1,0:T(8,128)(2,1)} %all-reduce.2.cloned.1.call-done.refs_0_.refs_2_, bf16[6,512,1024]{2,1,0:T(8,128)(2,1)} %collective-permute-done.2.refs_1_.refs_3_, ...), custom_call_target="tpu_custom_call" | custom-call | tf_op jit(solution)/shard_map/pallas_call | solution.py:80
  236.1 1.8 fusion.17
  237.9 2.1 fusion.13
  240.0 0.4 convolution_add_fusion.2
  240.4 0.4 convolution_add_fusion
  240.9 0.4 convolution_add_fusion.1
  241.3 1.4 fusion.1
  (40 shorter events, 0.2 us)
Async XLA Ops:
  6.5 178.3 %copy-start = (f32[128]{0:T(128)S(1)}, f32[128]{0:T(128)}, u32[]{:S(2)}) copy-start(f32[128]{0:T(128)} %param.8) | copy-start | bytes 1540
  6.5 172.9 %all-reduce.2.cloned.1.call-start = ((), (), s32[]{:S(2)}) async-start(), calls=%async_computation | async-start | bytes 12582912 | tf_op jit(solution)/shard_map/psum | solution.py:109
  12.2 0.7 copy-start.5
  12.2 0.7 copy-start.6
  12.2 5.2 %copy-start.2 = (bf16[1,1024,512]{2,1,0:T(8,128)(2,1)S(1)}, bf16[1,1024,512]{2,1,0:T(8,128)(2,1)}, u32[]{:S(2)}) copy-start(bf16[1,1024,512]{2,1,0:T(8,128)(2,1)} %param.7) | copy-start | bytes 3145732
  12.2 168.8 %copy-start.3 = (f32[512,512]{1,0:T(8,128)S(1)}, f32[512,512]{1,0:T(8,128)}, u32[]{:S(2)}) copy-start(f32[512,512]{1,0:T(8,128)} %param.10) | copy-start | bytes 3145732
  12.2 170.2 %copy-start.4 = (f32[512]{0:T(512)S(1)}, f32[512]{0:T(512)}, u32[]{:S(2)}) copy-start(f32[512]{0:T(512)} %param.9) | copy-start | bytes 6148
  12.9 172.6 %collective-permute-start = (f32[24]{0:T(128)S(1)}, f32[24]{0:T(128)S(1)}, u32[]{:S(2)}, u32[]{:S(2)}) collective-permute-start(f32[24]{0:T(128)S(1)} %pad_maximum_fusion.4), channel_id=1, source_target_pairs={{0,64},{64,0},{1,65},{65,1},{2,66},{66,2},{3,67},{67,3},{4,68},{68... | collective-permute-start | bytes 296 | tf_op jit(solution)/shard_map/ppermute | solution.py:116
  17.3 182.8 %collective-permute-start.3 = (bf16[1024,512]{1,0:T(8,128)(2,1)S(1)}, bf16[1024,512]{1,0:T(8,128)(2,1)}, u32[]{:S(2)}, u32[]{:S(2)}) collective-permute-start(bf16[1024,512]{1,0:T(8,128)(2,1)S(1)} %bitcast.74), channel_id=1, source_target_pairs={{0,64},{64,0},{1,65},{65,1},{2,66},{66,2},{3,67},{67,3},{4,68},{68... | collective-permute-start | bytes 3145736 | tf_op jit(solution)/shard_map/ppermute | solution.py:115
  179.4 39.4 %collective-permute-start.2 = (bf16[6,512,1024]{2,1,0:T(8,128)(2,1)}, bf16[6,512,1024]{2,1,0:T(8,128)(2,1)}, u32[]{:S(2)}, u32[]{:S(2)}) collective-permute-start(bf16[6,512,1024]{2,1,0:T(8,128)(2,1)} %all-reduce.2.cloned.1.call-done.refs_0_.refs_2_), channel_id=1, source_target_pairs={{0,32},{32,0},{1,33},{33,1},{2,34},{34,2},{3,35},{35,3},{4,36},{36... | collective-permute-start | bytes 18874376 | tf_op jit(solution)/shard_map/ppermute | solution.py:110
  185.5 5.4 %collective-permute-start.1 = (f32[2,24]{1,0:T(2,128)S(1)}, f32[2,24]{1,0:T(2,128)S(1)}, u32[]{:S(2)}, u32[]{:S(2)}) collective-permute-start(f32[2,24]{1,0:T(2,128)S(1)} %pad_maximum_fusion.3), channel_id=1, source_target_pairs={{0,32},{32,0},{1,33},{33,1},{2,34},{34,2},{3,35},{35,3},{4,36},{36... | collective-permute-start | bytes 584 | tf_op jit(solution)/shard_map/ppermute | solution.py:118
  202.9 12.3 %collective-permute-start.4 = (bf16[2,1024,512]{2,1,0:T(8,128)(2,1)}, bf16[2,1024,512]{2,1,0:T(8,128)(2,1)}, u32[]{:S(2)}, u32[]{:S(2)}) collective-permute-start(bf16[2,1024,512]{2,1,0:T(8,128)(2,1)} %pad_maximum_fusion.1), channel_id=1, source_target_pairs={{0,32},{32,0},{1,33},{33,1},{2,34},{34,2},{3,35},{35,3},{4,36},{36... | collective-permute-start | bytes 6291464 | tf_op jit(solution)/shard_map/ppermute | solution.py:117
  236.1 3.9 %copy-start.1 = (f32[512,512]{1,0:T(8,128)S(1)}, f32[512,512]{1,0:T(8,128)}, u32[]{:S(2)}) copy-start(f32[512,512]{1,0:T(8,128)} %shard_map.73) | copy-start | bytes 3145732
Sparse Core Ops, SparseCore 0:
  12.3 167.0 all-reduce.1

commit v12 on v10

--- a/solution.py
+++ b/solution.py
@@ -21,7 +21,9 @@
         mine_ref, theirs_ref = lefts[2 * stream], lefts[2 * stream + 1]
         from_theirs = tiles_ref[3 * stream * steps + step] != 0
         left = jnp.where(from_theirs, theirs_ref[...], mine_ref[...])
-        integral = jnp.dot(left, right_ref[...], preferred_element_type=jnp.float32)
+        integral = lax.dot_general(
+            left, right_ref[...], (((0,), (0,)), ((), ())), preferred_element_type=jnp.float32
+        )
         denominator = (pair_ref[...] - scalars_ref[slot]) - scalars_ref[slots + slot]
         scaled = (integral / denominator) * scalars_ref[2 * slots + slot]
         amplitude = scaled.astype(jnp.bfloat16).astype(jnp.float32)
@@ -45,10 +47,10 @@
 
 def summed_tiles(position, scalars, mine, theirs, column, pair_sum):
     slots = position.shape[0]
-    streams = 4
+    streams = 2
     steps = slots // streams
     per_source = slots // column.shape[0]
-    half, rows, depth = mine.shape
+    half, depth, rows = mine.shape
     parts = []
     for stream in range(streams):
         picked = position[stream::streams]
@@ -63,7 +65,7 @@
 
     def left_spec(stream, kind):
         offset = (3 * stream + kind) * steps
-        return pl.BlockSpec((None, rows, depth), lambda p, tiles: (tiles[offset + p], 0, 0))
+        return pl.BlockSpec((None, depth, rows), lambda p, tiles: (tiles[offset + p], 0, 0))
 
     grid_spec = pltpu.PrefetchScalarGridSpec(
         num_scalar_prefetch=1,
@@ -100,12 +102,11 @@
 
     groups_range = jnp.arange(group_count, dtype=jnp.int32)
     i_ids = (groups_range[None, :] * orbit_count + i_plan).reshape(tile_count)
-    own_turned = own_panel.T
     core_ids = lax.dynamic_index_in_dim(
         i_ids.reshape(STEPS, halves, cores), my_core, axis=2, keepdims=False
     ).reshape(-1)
     masked = jnp.where(
-        (core_ids == my_orbital)[:, None, None], own_turned[None], jnp.zeros((), own_panel.dtype)
+        (core_ids == my_orbital)[:, None, None], own_panel[None], jnp.zeros((), own_panel.dtype)
     )
     own_half = lax.psum(masked, ("zh", "orb"))
     other_half = lax.ppermute(own_half, "core", [(c, c ^ 1) for c in range(cores)])

time: 245 us -> 250 us (1.020)
  waiting for transfers between devices: 144 us -> 168 us
  between operations: 29.4 us -> 21.5 us
  other arithmetic: 25.2 us -> 20.1 us
  local copies, waits for them, and re-layouts: 14 us -> 9 us
    psum x1, waiting for transfers between devices: 144 us -> 161 us  [layer(): own_half = lax.psum(masked, ('zh', 'orb'))]
    ppermute x1, waiting for transfers between devices: 0.32 us -> 6.91 us  [layer(): near_meta = lax.ppermute(jnp.stack([meta, far_meta]), 'core', beside)]
    ppermute x1, starting transfers between devices: 4.42 us -> 0.03 us  [layer(): far_meta = lax.ppermute(meta, 'zh', across)]
    ppermute x1, starting transfers between devices: 0.5 us -> 4.41 us  [layer(): far_panel = lax.ppermute(own_panel, 'zh', across)]
    another operation x8 -> x4, other arithmetic: 5.73 us -> 2.87 us  [held_index(): first = jnp.argmax(present)]
    select_n x4 -> x2, other arithmetic: 5.25 us -> 2.64 us  [held_index(): return jnp.where(last >= 0, local[jnp.maximum(last, 0)], local[first])]
    gather x8 -> x4, local copies, waits for them, and re-layouts: 5.12 us -> 2.57 us  [held_index(): return jnp.where(last >= 0, local[jnp.maximum(last, 0)], local[first])]
  transfers between devices with their start and end apart: 6 -> 6, of which waited for: 2 -> 2; matrix products, arithmetic and copies ran while one was open for 13% -> 9% of each run, Pallas kernels for 0% -> 0%
where the time goes in v12:
time: 250 us; the launch traced here: 249 us
  waiting for transfers between devices  168 us (67%)
  between operations  21.5 us (9%)
  other arithmetic  20.1 us (8%)
  Pallas kernels  17.8 us (7%)
  local copies, waits for them, and re-layouts  9 us (4%)
  starting transfers between devices  6.36 us (3%)
  matrix products  6.19 us (2%)
    psum x1, waiting for transfers between devices, layer(): own_half = lax.psum(masked, ('zh', 'orb'))  161 us
    pallas_call x1, Pallas kernels, summed_tiles(): pl.pallas_call(slot_kernel, grid_spec=grid_spec, out_shape=jax.ShapeDtype...  17.8 us
    ppermute x1, waiting for transfers between devices, layer(): near_meta = lax.ppermute(jnp.stack([meta, far_meta]), 'core', beside)  6.91 us
  transfers between devices with their start and end apart: 6, of which 2 were waited for; matrix products, arithmetic and copies ran while one was open for 9% of the time, Pallas kernels for 0%

profile of v12, /device:TPU:1, one launch (start us, length us, event | category | flops | bytes accessed | tf_op | source)
XLA Modules:
  0.0 249.3 jit_solution(9303114232990077529)
XLA Ops:
  6.5 0.0 copy-start
  6.5 0.0 all-reduce.2.cloned.1.call-start
  6.5 0.7 broadcast_add_fusion.1
  7.2 0.1 copy.18
  7.3 0.1 copy.20
  7.5 0.1 eq.64
  7.5 4.4 %broadcast_select_fusion = bf16[6,1024,512]{2,1,0:T(8,128)(2,1)} fusion(pred[6]{0:T(512)(128)(4,1)S(1)} %eq.64, bf16[1024,512]{1,0:T(8,128)(2,1)} %bitcast.64), kind=kLoop, calls=%fused_computation.7 | loop fusion | flops 3145728 | bytes 7340038 | tf_op jit(solution)/shard_map/jit(_where)/select_n | solution.py:108
  11.9 0.0 copy-start.2
  11.9 0.0 all-reduce.2.cloned.1.call-update
  12.0 1.2 copy-done.3
  13.1 4.4 %collective-permute-start.3 = (bf16[1024,512]{1,0:T(8,128)(2,1)S(1)}, bf16[1024,512]{1,0:T(8,128)(2,1)}, u32[]{:S(2)}, u32[]{:S(2)}) collective-permute-start(bf16[1024,512]{1,0:T(8,128)(2,1)S(1)} %bitcast.65), channel_id=1, source_target_pairs={{0,64},{64,0},{1,65},{65,1},{2,66},{66,2},{3,67},{67,3},{4,68},{68... | collective-permute-start | bytes 3145736 | tf_op jit(solution)/shard_map/ppermute | solution.py:117
  17.6 0.1 pad_maximum_fusion.4
  17.6 0.0 collective-permute-start
  17.7 0.1 reshape.204
  17.7 161.3 %all-reduce.2.cloned.1.call-done.refs_0_.refs_2_ = bf16[6,1024,512]{2,1,0:T(8,128)(2,1)} async-done(((bf16[6,1024,512]{2,1,0:T(8,128)(2,1)}), bf16[6,1024,512]{2,1,0:T(8,128)(2,1)}) %all-reduce.2.cloned.1.call-update) | async-done | bytes 6291472 | tf_op jit(solution)/shard_map/psum | solution.py:111
  179.0 1.4 collective-permute-start.2
  180.5 0.7 gather_fusion.4
  181.2 0.1 fusion.19
  181.2 0.1 fusion.7
  181.4 1.1 broadcast_add_fusion.refs_5_
  182.5 0.6 gather_fusion.6
  183.1 0.0 collective-permute-done
  183.1 0.1 collective-permute-start.1
  183.2 0.1 broadcast_in_dim.117
  183.3 0.1 reshape.206
  183.4 0.3 copy.17
  183.7 6.9 %collective-permute-done.1 = f32[2,24]{1,0:T(2,128)S(1)} collective-permute-done((f32[2,24]{1,0:T(2,128)S(1)}, f32[2,24]{1,0:T(2,128)S(1)}, u32[]{:S(2)}, u32[]{:S(2)}) %collective-permute-start.1) | collective-permute-done | bytes 224 | tf_op jit(solution)/shard_map/ppermute | solution.py:120
  190.6 0.1 fusion.14
  190.7 0.2 reduce_window_sum.11
  190.9 0.1 select_reduce_fusion.1
  191.0 0.1 reduce_sum.23
  191.2 0.1 slice.20
  191.3 0.1 slice.19
  191.4 0.7 iota_reduce_fusion.1
  193.4 0.7 not_reduce_fusion.1
  195.5 0.7 iota_reduce_fusion
  197.4 0.7 not_reduce_fusion
  199.5 0.2 reduce-window.19
  199.8 0.0 collective-permute-done.3
  199.8 2.8 %pad_maximum_fusion.1 = bf16[2,1024,512]{2,1,0:T(8,128)(2,1)} fusion(bf16[1,1024,512]{2,1,0:T(8,128)(2,1)} %bitcast.29, bf16[1,1024,512]{2,1,0:T(8,128)(2,1)S(1)} %copy-done.3), kind=kLoop, calls=%fused_computation.9 | loop fusion | flops 1048576 | bytes 4194304 | tf_op jit(solution)/shard_map/stack | solution.py:119
  202.6 0.4 collective-permute-start.4
  202.9 0.1 select_reduce_fusion
  203.0 0.1 reshape.207
  203.1 0.1 reshape.250
  203.2 0.2 reduce-window.15
  203.4 0.2 reduce-window.14
  203.5 0.2 reduce-window.16
  203.7 0.6 gather_fusion.3
  204.4 0.6 gather_fusion.2
  205.1 0.6 gather_fusion.1
  205.7 0.6 gather_fusion
  209.0 0.7 gather_fusion.5
  209.7 0.7 fusion.16
  210.4 0.7 fusion.15
  211.0 1.3 bitcast_select_fusion
  212.4 1.3 bitcast_select_fusion.2
  213.7 0.6 concatenate.17.tiles_ref
  214.3 0.6 pad_maximum_fusion.5.scalars_ref
  214.9 0.0 collective-permute-done.4
  214.9 3.5 %pad_maximum_fusion.refs_4_ = bf16[4,1024,512]{2,1,0:T(8,128)(2,1)} fusion(bf16[2,1024,512]{2,1,0:T(8,128)(2,1)} %collective-permute-done.4, bf16[1,1024,512]{2,1,0:T(8,128)(2,1)} %bitcast.29, bf16[1,1024,512]{2,1,0:T(8,128)(2,1)S(1)} %copy-done.3), kind=kLoop, calls=%fused_computation.8 | loop fusion | flops 4194304 | bytes 8388608 | tf_op jit(solution)/shard_map/stack | solution.py:121
  218.4 0.0 collective-permute-done.2.refs_1_.refs_3_
  218.4 17.8 %shard_map.73 = f32[512,512]{1,0:T(8,128)} custom-call(s32[48]{0:T(128)} %concatenate.17.tiles_ref, f32[48]{0:T(128)} %pad_maximum_fusion.5.scalars_ref, bf16[6,1024,512]{2,1,0:T(8,128)(2,1)} %all-reduce.2.cloned.1.call-done.refs_0_.refs_2_, bf16[6,1024,512]{2,1,0:T(8,128)(2,1)} %collective-permute-done.2.refs_1_.refs_3_, ...), custom_call_target="tpu_custom_call" | custom-call | tf_op jit(solution)/shard_map/pallas_call | solution.py:82
  236.2 3.3 %fusion.11 = f32[512,512]{1,0:T(8,128)S(1)} fusion(f32[512,512]{1,0:T(8,128)} %shard_map.73, f32[512,512]{1,0:T(8,128)S(1)} %copy-done.2, f32[512,512]{0,1:T(8,128)S(1)} %copy.17, f32[512]{0:T(512)S(1)} %copy-done.4), kind=kOutput, calls=%fused_computation.81 | convolution fusion | flops 1611923456 | bytes 4196352 | tf_op jit(solution)/shard_map/dot_general | solution.py:154
  239.5 2.9 %fusion = f32[1,512,512]{2,1,0:T(8,128)} fusion(f32[512,512]{1,0:T(8,128)S(1)} %fusion.11, f32[512,512]{1,0:T(8,128)S(1)} %copy-done.1, f32[512,512]{1,0:T(8,128)S(1)} %copy-done.2, f32[512,512]{0,1:T(8,128)S(1)} %copy.17, f32[512]{0:T(512)S(1)} %copy-done.4), kind=kOutput, calls=%fused_computation.11 | convolution fusion | flops 1612185600 | bytes 5244928 | tf_op jit(solution)/shard_map/dot_general | solution.py:153
  (35 shorter events, 0.2 us)
Async XLA Ops:
  6.5 174.0 %copy-start = (f32[128]{0:T(128)S(1)}, f32[128]{0:T(128)}, u32[]{:S(2)}) copy-start(f32[128]{0:T(128)} %param.8) | copy-start | bytes 1540
  6.5 172.5 %all-reduce.2.cloned.1.call-start = ((), (), s32[]{:S(2)}) async-start(), calls=%async_computation | async-start | bytes 12582912 | tf_op jit(solution)/shard_map/psum | solution.py:111
  11.9 1.2 copy-start.3
  11.9 5.6 %copy-start.5 = (s32[12,1]{0,1:T(1,128)S(1)}, s32[12,1]{0,1:T(1,128)}, u32[]{:S(2)}) copy-start(s32[12,1]{0,1:T(1,128)} %param.12) | copy-start | bytes 148
  11.9 5.6 %copy-start.6 = (f32[12]{0:T(128)S(1)}, f32[12]{0:T(128)}, u32[]{:S(2)}) copy-start(f32[12]{0:T(128)} %param.13) | copy-start | bytes 148
  11.9 169.4 %copy-start.4 = (f32[512]{0:T(512)S(1)}, f32[512]{0:T(512)}, u32[]{:S(2)}) copy-start(f32[512]{0:T(512)} %param.9) | copy-start | bytes 6148
  11.9 171.5 %copy-start.2 = (f32[512,512]{1,0:T(8,128)S(1)}, f32[512,512]{1,0:T(8,128)}, u32[]{:S(2)}) copy-start(f32[512,512]{1,0:T(8,128)} %param.10) | copy-start | bytes 3145732
  13.1 186.6 %collective-permute-start.3 = (bf16[1024,512]{1,0:T(8,128)(2,1)S(1)}, bf16[1024,512]{1,0:T(8,128)(2,1)}, u32[]{:S(2)}, u32[]{:S(2)}) collective-permute-start(bf16[1024,512]{1,0:T(8,128)(2,1)S(1)} %bitcast.65), channel_id=1, source_target_pairs={{0,64},{64,0},{1,65},{65,1},{2,66},{66,2},{3,67},{67,3},{4,68},{68... | collective-permute-start | bytes 3145736 | tf_op jit(solution)/shard_map/ppermute | solution.py:117
  17.6 165.5 %collective-permute-start = (f32[24]{0:T(128)S(1)}, f32[24]{0:T(128)S(1)}, u32[]{:S(2)}, u32[]{:S(2)}) collective-permute-start(f32[24]{0:T(128)S(1)} %pad_maximum_fusion.4), channel_id=1, source_target_pairs={{0,64},{64,0},{1,65},{65,1},{2,66},{66,2},{3,67},{67,3},{4,68},{68... | collective-permute-start | bytes 296 | tf_op jit(solution)/shard_map/ppermute | solution.py:118
  179.0 39.4 %collective-permute-start.2 = (bf16[6,1024,512]{2,1,0:T(8,128)(2,1)}, bf16[6,1024,512]{2,1,0:T(8,128)(2,1)}, u32[]{:S(2)}, u32[]{:S(2)}) collective-permute-start(bf16[6,1024,512]{2,1,0:T(8,128)(2,1)} %all-reduce.2.cloned.1.call-done.refs_0_.refs_2_), channel_id=1, source_target_pairs={{0,32},{32,0},{1,33},{33,1},{2,34},{34,2},{3,35},{35,3},{4,36},{36... | collective-permute-start | bytes 18874376 | tf_op jit(solution)/shard_map/ppermute | solution.py:112
  183.1 7.5 %collective-permute-start.1 = (f32[2,24]{1,0:T(2,128)S(1)}, f32[2,24]{1,0:T(2,128)S(1)}, u32[]{:S(2)}, u32[]{:S(2)}) collective-permute-start(f32[2,24]{1,0:T(2,128)S(1)} %pad_maximum_fusion.3), channel_id=1, source_target_pairs={{0,32},{32,0},{1,33},{33,1},{2,34},{34,2},{3,35},{35,3},{4,36},{36... | collective-permute-start | bytes 584 | tf_op jit(solution)/shard_map/ppermute | solution.py:120
  202.6 12.3 %collective-permute-start.4 = (bf16[2,1024,512]{2,1,0:T(8,128)(2,1)}, bf16[2,1024,512]{2,1,0:T(8,128)(2,1)}, u32[]{:S(2)}, u32[]{:S(2)}) collective-permute-start(bf16[2,1024,512]{2,1,0:T(8,128)(2,1)} %pad_maximum_fusion.1), channel_id=1, source_target_pairs={{0,32},{32,0},{1,33},{33,1},{2,34},{34,2},{3,35},{35,3},{4,36},{36... | collective-permute-start | bytes 6291464 | tf_op jit(solution)/shard_map/ppermute | solution.py:119
  236.2 3.3 %copy-start.1 = (f32[512,512]{1,0:T(8,128)S(1)}, f32[512,512]{1,0:T(8,128)}, u32[]{:S(2)}) copy-start(f32[512,512]{1,0:T(8,128)} %shard_map.73) | copy-start | bytes 3145732
Sparse Core Ops, SparseCore 0:
  12.2 166.8 all-reduce.1
